TPU v7x, 128 devices: a whole 4x4x4 slice. The times are simulated.
128 devices in a mesh: seq: 16 (over y_hi, z, core), mp: 8 (over y_lo, x).
Axes of the slice: x: 4, y: 4 (y_hi: 2, y_lo: 2; y = y_hi * 2 + y_lo), z: 4, core: 2. Of those that a mesh axis runs over, the one named last changes fastest.
Arguments:
- tokens_in: bfloat16 [32768, 2048], P('seq'), may hold values from -6 to 6
- norm_gain: float32 [2048], replicated, may hold values from 0.5 to 200
- q_weight: bfloat16 [2048, 2048], P('seq', 'mp'), may hold values from -0.125 to 0.125
- kv_weight: bfloat16 [4, 2048, 128], P(None, 'seq'), may hold values from -0.125 to 0.125
- out_weight: bfloat16 [2048, 2048], P('seq', 'mp'), may hold values from -0.25 to 0.25
- segment_ids: int32 [32768], P('seq'), may hold values from 0 to 31, never falling along the last dimension, each value on 1 to 8192 neighbouring positions
- page_table: int32 [256], P('seq'), may hold values from 0 to 255, as said below
Outputs:
- layer_out: bfloat16 [32768, 2048], P('seq', 'mp')
- kv_cache: bfloat16 [256, 512, 128], P('seq', 'mp')
Inputs may be any that keep to these rules, and one draw needn't show every extreme that they name: `segment_ids`: segment numbers never fall along the stream; each of the 32 segments holds 1 to 8192 tokens and one holds exactly 8192. `page_table`: A permutation of the 256 cache slots; slot s belongs to index s // 16 of seq. The pages of index i of seq go to the indices i + o, counted round, for 16 distinct offsets o that are the same for every i, among them 1 and 16 / 2; exactly 1 pages to each owner.
All inputs are finite; a program needn't handle non-finite values.
Results may differ from a plain program's by a relative error of at most 0.018.
The roundings to bfloat16 on the way count: a program that leaves them out, or rounds other values in their place, can miss the bound.
Values may be sent and summed in bfloat16 or wider, within the bound.
No kernel may reach another device: no remote copies, remote signals or barrier semaphores. Data moves between devices by JAX's collectives and lax.ppermute only.
A program may use at most 64 MiB of HBM per device.

v0:
```python
import math

import jax
import jax.numpy as jnp
from jax import lax
from jax.sharding import PartitionSpec as P

W = 2048
PAGE = 128


def prefix(value, axis, join, neutral):
    count, mine = (lax.axis_size(axis), lax.axis_index(axis))
    pieces = jax.tree.map(lambda part: lax.all_gather(part, axis), value)
    so_far = jax.tree.map(
        lambda part, zero: jnp.full_like(part, 0) + jnp.asarray(zero, part.dtype), value, neutral
    )

    def hop(position, so_far):
        longer = join(so_far, jax.tree.map(lambda part: part[position], pieces))
        return jax.tree.map(lambda new, old: jnp.where(position < mine, new, old), longer, so_far)

    return lax.fori_loop(0, count - 1, hop, so_far)


def from_behind(x, axis, by):
    peers = lax.axis_size(axis)
    pairs = [(i, i + by) for i in range(peers) if 0 <= i + by < peers]
    return lax.ppermute(x, axis, pairs)


def rotate_half(values, cosine, sine_table):
    half = values.shape[-1] // 2
    first_half = values[..., :half]
    second = values[..., half:]
    return jnp.concatenate(
        [first_half * cosine - second * sine_table, second * cosine + first_half * sine_table],
        axis=-1,
    )


def link_segments(earlier, later):
    seg_early, start_early = earlier
    seg_late, start_late = later
    merged_seg = jnp.maximum(seg_early, seg_late)
    merged_start = jnp.where(
        seg_late > seg_early,
        start_late,
        jnp.where(seg_early > seg_late, start_early, jnp.minimum(start_early, start_late)),
    )
    return (merged_seg, merged_start)


def attend_piece(carry, piece, start, queries, query_first, query_start, block_rows):
    head_size = queries.shape[2]
    count = piece.shape[0]
    key_rows = piece[:, :head_size]
    value_rows = piece[:, head_size:]
    key_index = start + jnp.arange(count, dtype=jnp.int32)
    scale = 1.0 / math.sqrt(head_size)
    blocks = queries.shape[0] // block_rows

    def one_block(block, state):
        row_first = block * block_rows
        query_block = lax.dynamic_slice_in_dim(queries, row_first, block_rows, 0)
        query_index = query_first + row_first + jnp.arange(block_rows, dtype=jnp.int32)
        query_begin = lax.dynamic_slice_in_dim(query_start, row_first, block_rows, 0)
        lowest = jnp.maximum(query_begin[0], query_index[0] - W + 1)
        live = (start <= query_index[-1]) & (start + count - 1 >= lowest)

        def compute(inner):
            best, totals, accum = inner
            best_block = lax.dynamic_slice_in_dim(best, row_first, block_rows, 1)
            total_block = lax.dynamic_slice_in_dim(totals, row_first, block_rows, 1)
            accum_block = lax.dynamic_slice_in_dim(accum, row_first, block_rows, 1)
            scores = (
                jnp.einsum("qhd,kd->hqk", query_block, key_rows, preferred_element_type=jnp.float32)
                * scale
            )
            keep = (key_index[None, :] >= query_begin[:, None]) & (
                key_index[None, :] <= query_index[:, None]
            )
            keep = keep & (query_index[:, None] - key_index[None, :] < W)
            masked = jnp.where(keep[None], scores, -1e30)
            new_best = jnp.maximum(best_block, jnp.max(masked, axis=-1))
            weights = jnp.where(keep[None], jnp.exp(masked - new_best[..., None]), 0.0)
            factor = jnp.exp(best_block - new_best)
            new_total = total_block * factor + jnp.sum(weights, axis=-1)
            mixed = jnp.einsum(
                "hqk,kd->hqd",
                weights.astype(jnp.bfloat16),
                value_rows,
                preferred_element_type=jnp.float32,
            )
            new_accum = accum_block * factor[..., None] + mixed
            best = lax.dynamic_update_slice_in_dim(best, new_best, row_first, 1)
            totals = lax.dynamic_update_slice_in_dim(totals, new_total, row_first, 1)
            accum = lax.dynamic_update_slice_in_dim(accum, new_accum, row_first, 1)
            return (best, totals, accum)

        return lax.cond(live, compute, lambda inner: inner, state)

    return lax.fori_loop(0, blocks, one_block, carry)


def body(tokens_in, norm_gain, q_weight, kv_weight, out_weight, segment_ids, page_table):
    seq_count = lax.axis_size("seq")
    mp_count = lax.axis_size("mp")
    seq_index = lax.axis_index("seq")
    mp_index = lax.axis_index("mp")
    tok_rows = tokens_in.shape[0]
    kv_heads = kv_weight.shape[0]
    head_size = kv_weight.shape[2] // 2
    ratio = mp_count // kv_heads
    own_head = mp_index // ratio
    kv_own = lax.dynamic_index_in_dim(kv_weight, own_head, 0, keepdims=False)
    w_query, w_keyval, w_output = (
        lax.all_gather(q_weight, "seq", axis=0, tiled=True),
        lax.all_gather(kv_own, "seq", axis=0, tiled=True),
        lax.all_gather(out_weight, "seq", axis=0, tiled=True),
    )
    inputs = tokens_in.astype(jnp.float32)
    meansq = jnp.mean(inputs * inputs, axis=-1, keepdims=True)
    normed = (inputs * lax.rsqrt(meansq + 1e-05) * norm_gain).astype(jnp.bfloat16)
    token_first = seq_index * tok_rows
    global_index = token_first + jnp.arange(tok_rows, dtype=jnp.int32)
    boundary = jnp.concatenate([jnp.ones((1,), bool), segment_ids[1:] != segment_ids[:-1]])
    local_start = lax.cummax(jnp.where(boundary, global_index, jnp.int32(0)), axis=0)
    prior_seg, prior_start = prefix(
        (segment_ids[-1], local_start[-1]), "seq", link_segments, (jnp.int32(-1), jnp.int32(0))
    )
    query_start = jnp.where(segment_ids == prior_seg, prior_start, local_start)
    positions = global_index - query_start
    half = head_size // 2
    freqs = jnp.exp(jnp.arange(half, dtype=jnp.float32) * (-2.0 * math.log(10000.0) / head_size))
    angles = positions.astype(jnp.float32)[:, None] * freqs[None, :]
    cosine = jnp.cos(angles)
    sine_table = jnp.sin(angles)
    local_heads = w_query.shape[1] // head_size
    queries = jnp.dot(normed, w_query, preferred_element_type=jnp.float32).reshape(
        tok_rows, local_heads, head_size
    )
    queries = rotate_half(queries, cosine[:, None, :], sine_table[:, None, :]).astype(jnp.bfloat16)
    projected = jnp.dot(normed, w_keyval, preferred_element_type=jnp.float32)
    key_rows = rotate_half(projected[:, :head_size], cosine, sine_table).astype(jnp.bfloat16)
    value_rows = projected[:, head_size:].astype(jnp.bfloat16)
    keyval = jnp.concatenate([key_rows, value_rows], axis=1)
    block_rows = min(512, tok_rows)
    initial = (
        jnp.full((local_heads, tok_rows), -1e30, jnp.float32),
        jnp.zeros((local_heads, tok_rows), jnp.float32),
        jnp.zeros((local_heads, tok_rows, head_size), jnp.float32),
    )

    def fold_piece(carry, piece, start):
        return attend_piece(carry, piece, start, queries, token_first, query_start, block_rows)

    state = fold_piece(initial, keyval, token_first)
    earlier = from_behind(keyval, "seq", 1)
    state = fold_piece(state, earlier, token_first - tok_rows)
    best, totals, accum = state
    attended = (
        (accum / totals[..., None])
        .transpose(1, 0, 2)
        .reshape(tok_rows, local_heads * head_size)
        .astype(jnp.bfloat16)
    )
    partial_term = lax.dot_general(
        attended, w_output, (((1,), (1,)), ((), ())), preferred_element_type=jnp.float32
    )
    layer_out = lax.psum_scatter(
        partial_term.astype(jnp.bfloat16), "mp", scatter_dimension=1, tiled=True
    )
    pages_dev = tok_rows // PAGE
    share_width = 2 * head_size // ratio
    share_index = mp_index % ratio
    share = lax.dynamic_slice_in_dim(keyval, share_index * share_width, share_width, 1)
    page_blocks = share.reshape(pages_dev, PAGE, share_width).transpose(0, 2, 1)
    owners = page_table // pages_dev
    local_slot = page_table % pages_dev
    spread = min(seq_count, pages_dev)
    capacity = pages_dev // spread
    page_order = jnp.arange(pages_dev, dtype=jnp.int32)
    same_owner = (owners[:, None] == owners[None, :]) & (page_order[None, :] < page_order[:, None])
    ranking = jnp.sum(same_owner.astype(jnp.int32), axis=1)
    send_lane = owners * capacity + ranking
    lanes_all = seq_count * capacity
    select = jnp.arange(lanes_all, dtype=jnp.int32)[:, None] == send_lane[None, :]
    outgoing = jnp.einsum(
        "sp,pfk->sfk", select.astype(jnp.bfloat16), page_blocks, preferred_element_type=jnp.float32
    ).astype(jnp.bfloat16)
    outgoing = outgoing.reshape(seq_count, capacity, share_width, PAGE)
    labels = (
        jnp.dot(select.astype(jnp.float32), (local_slot + 1).astype(jnp.float32))
        .astype(jnp.bfloat16)
        .reshape(seq_count, capacity)
    )
    incoming, tags = (
        lax.all_to_all(outgoing, "seq", split_axis=0, concat_axis=0, tiled=True),
        lax.all_to_all(labels, "seq", split_axis=0, concat_axis=0, tiled=True),
    )
    tags_flat = tags.reshape(lanes_all).astype(jnp.float32)
    placement = (tags_flat[None, :] == (page_order + 1).astype(jnp.float32)[:, None]).astype(
        jnp.bfloat16
    )
    kv_cache = jnp.einsum(
        "ps,sfk->pfk",
        placement,
        incoming.reshape(lanes_all, share_width, PAGE),
        preferred_element_type=jnp.float32,
    ).astype(jnp.bfloat16)
    return (layer_out, kv_cache)


def solution(mesh):
    placed = (
        P("seq", None),
        P(),
        P("seq", "mp"),
        P(None, "seq", None),
        P("seq", "mp"),
        P("seq"),
        P("seq"),
    )
    return jax.shard_map(
        body,
        mesh=mesh,
        in_specs=placed,
        out_specs=(P("seq", "mp"), P("seq", "mp", None)),
        check_vma=False,
    )
```

profile of v0, /device:TPU:1, one launch (start us, length us, event | category | flops | bytes accessed | tf_op | source)
XLA Modules:
  0.0 427.0 jit_solution(16916821592554316172)
XLA Ops:
  8.8 5.1 %fusion.50 = f32[2048]{0:T(1024)S(1)} fusion(bf16[2048,2048]{1,0:T(8,128)(2,1)} %param.17), kind=kLoop, calls=%fused_computation.60 | loop fusion | flops 12580864 | bytes 8396800 | tf_op jit(solution)/shard_map/reduce_sum | solution.py:123
  14.0 28.4 %all-gather = bf16[1,2048,128]{2,1,0:T(8,128)(2,1)S(1)} all-gather(bf16[1,128,128]{2,1,0:T(8,128)(2,1)S(1)} %constant_dynamic-slice_fusion), channel_id=2, replica_groups=mesh['seq'=16,'mp'=8] {'seq'}, dimensions={1}, use_global_device_ids=true | all-gather | bytes 557056 | tf_op jit(solution)/shard_map/all_gather | solution.py:119
  42.4 5.4 %fusion.53 = f32[2048,128]{0,1:T(8,128)S(1)} fusion(bf16[2048,2048]{1,0:T(8,128)(2,1)} %param.17, f32[2048]{0:T(1024)} %param.18, f32[2048]{0:T(1024)S(1)} %add_rsqrt_fusion, bf16[1,2048,128]{2,1,0:T(8,128)(2,1)S(1)} %all-gather), kind=kOutput, calls=%fused_computation.64 | convolution fusion | flops 1090519040 | bytes 9977856 | tf_op jit(solution)/shard_map/dot_general | solution.py:144
  50.7 5.6 %all-reduce.2 = (s32[16]{0:T(128)S(1)}, s32[16]{0:T(128)S(1)}) all-reduce(s32[16]{0:T(128)S(1)} %slice_dynamic-update-slice_fusion.1, s32[16]{0:T(128)S(1)} %slice_dynamic-update-slice_fusion), channel_id=1, replica_groups=mesh['seq'=16,'mp'=8] {'seq'}, use_global_device_ids=true, to_apply=%add | all-reduce | flops 32 | bytes 256
  56.4 64.1 %while.61 = (s32[]{:T(128)}, s32[]{:T(128)}, s32[]{:T(128)}, s32[]{:T(128)}, s32[16]{0:T(128)S(1)}, /*index=5*/s32[16]{0:T(128)S(1)}, s32[]{:T(128)}) while((s32[]{:T(128)}, s32[]{:T(128)}, s32[]{:T(128)}, s32[]{:T(128)}, s32[16]{0:T(128)S(1)}, /*index=5*/s32[16]{0:T(128)S(1)}, s32[]{:T(128)}) %tuple.189), condition=%wide.region_4.5_spmd, body=%wide.region_3.4_spmd.sunk | while | flops 11 | bytes 220 | solution.py:23
  126.8 5.1 %collective-permute-done = bf16[2048,128]{0,1:T(8,128)(2,1)S(1)} collective-permute-done((bf16[2048,128]{0,1:T(8,128)(2,1)S(1)}, bf16[2048,128]{0,1:T(8,128)(2,1)S(1)}, u32[]{:S(2)}, u32[]{:S(2)}) %collective-permute-start) | collective-permute-done | bytes 524320 | tf_op jit(solution)/shard_map/ppermute | solution.py:29
  132.7 5.6 %fusion.55 = f32[2048,256]{0,1:T(8,128)S(1)} fusion(bf16[2048,256]{1,0:T(8,128)(2,1)} %all-gather.4.cloned.1.call-done, bf16[2048,2048]{1,0:T(8,128)(2,1)} %param.17, f32[2048]{0:T(1024)S(1)} %copy-done.5, f32[2048]{0:T(1024)S(1)} %add_rsqrt_fusion), kind=kOutput, calls=%fused_computation.65 | convolution fusion | flops 2164260864 | bytes 11550720 | tf_op jit(solution)/shard_map/dot_general | solution.py:140
  139.6 84.6 %while.62 = (s32[]{:T(128)}, f32[4,2048]{1,0:T(4,128)S(1)}, f32[4,2048]{1,0:T(4,128)}, f32[4,2048,64]{1,2,0:T(8,128)S(1)}, s32[]{:T(128)}, /*index=5*/s32[2048]{...) while((s32[]{:T(128)}, f32[4,2048]{1,0:T(4,128)S(1)}, ...), condition=%wide.region_10.11_spmd.clone.clone, body=%wide.region_5.10_spmd.clone.clone.sunk | while | flops 1134828032 | bytes 57706992 | solution.py:103
  142.7 18.0 %conditional.8 = ((f32[4,2048]{1,0:T(4,128)S(1)}, f32[4,2048]{1,0:T(4,128)}, f32[4,2048,64]{1,2,0:T(8,128)S(1)})) conditional(s32[]{:T(128)} %convert_element_type.157, (f32[4,2048]{1,0:T(4,128)S(1)}, f32[4,2048]{1,0:T(4,128)}, f32[4,2048,64]{1,2,0:T(8,128)S(1)}) %tuple.179, (s32[]{:T(128)}, f32[4,2048]{1,0:T(4,128)S(1)}, s32[]{:T(128)}, ...), branch_computations={%region_6.6_spmd, %region_7.9_spmd} | conditional | flops 1134827520 | bytes 57692248 | solution.py:101
  149.9 4.9 %fusion.7 = f32[4,512]{1,0:T(4,128)S(1)} fusion(f32[512,4,2048]{2,0,1:T(8,128)S(1)} %get-tuple-element.1188, f32[4,512]{1,0:T(4,128)S(1)} %get-tuple-element.1180, pred[512,2048]{1,0:T(8,128)(4,1)S(1)} %fusion.12), kind=kLoop, calls=%fused_computation.8 | loop fusion | flops 20969472 | bytes 17842176 | tf_op jit(solution)/shard_map/while/body/eval_jaxpr/cond/branch_1_fun/reduce_sum | solution.py:88
  163.8 18.0 %conditional.8 = ((f32[4,2048]{1,0:T(4,128)S(1)}, f32[4,2048]{1,0:T(4,128)}, f32[4,2048,64]{1,2,0:T(8,128)S(1)})) conditional(s32[]{:T(128)} %convert_element_type.157, (f32[4,2048]{1,0:T(4,128)S(1)}, f32[4,2048]{1,0:T(4,128)}, f32[4,2048,64]{1,2,0:T(8,128)S(1)}) %tuple.179, (s32[]{:T(128)}, f32[4,2048]{1,0:T(4,128)S(1)}, s32[]{:T(128)}, ...), branch_computations={%region_6.6_spmd, %region_7.9_spmd} | conditional | flops 1134827520 | bytes 57692248 | solution.py:101
  171.0 4.9 %fusion.7 = f32[4,512]{1,0:T(4,128)S(1)} fusion(f32[512,4,2048]{2,0,1:T(8,128)S(1)} %get-tuple-element.1188, f32[4,512]{1,0:T(4,128)S(1)} %get-tuple-element.1180, pred[512,2048]{1,0:T(8,128)(4,1)S(1)} %fusion.12), kind=kLoop, calls=%fused_computation.8 | loop fusion | flops 20969472 | bytes 17842176 | tf_op jit(solution)/shard_map/while/body/eval_jaxpr/cond/branch_1_fun/reduce_sum | solution.py:88
  185.0 18.0 %conditional.8 = ((f32[4,2048]{1,0:T(4,128)S(1)}, f32[4,2048]{1,0:T(4,128)}, f32[4,2048,64]{1,2,0:T(8,128)S(1)})) conditional(s32[]{:T(128)} %convert_element_type.157, (f32[4,2048]{1,0:T(4,128)S(1)}, f32[4,2048]{1,0:T(4,128)}, f32[4,2048,64]{1,2,0:T(8,128)S(1)}) %tuple.179, (s32[]{:T(128)}, f32[4,2048]{1,0:T(4,128)S(1)}, s32[]{:T(128)}, ...), branch_computations={%region_6.6_spmd, %region_7.9_spmd} | conditional | flops 1134827520 | bytes 57692248 | solution.py:101
  192.2 4.9 %fusion.7 = f32[4,512]{1,0:T(4,128)S(1)} fusion(f32[512,4,2048]{2,0,1:T(8,128)S(1)} %get-tuple-element.1188, f32[4,512]{1,0:T(4,128)S(1)} %get-tuple-element.1180, pred[512,2048]{1,0:T(8,128)(4,1)S(1)} %fusion.12), kind=kLoop, calls=%fused_computation.8 | loop fusion | flops 20969472 | bytes 17842176 | tf_op jit(solution)/shard_map/while/body/eval_jaxpr/cond/branch_1_fun/reduce_sum | solution.py:88
  206.1 18.0 %conditional.8 = ((f32[4,2048]{1,0:T(4,128)S(1)}, f32[4,2048]{1,0:T(4,128)}, f32[4,2048,64]{1,2,0:T(8,128)S(1)})) conditional(s32[]{:T(128)} %convert_element_type.157, (f32[4,2048]{1,0:T(4,128)S(1)}, f32[4,2048]{1,0:T(4,128)}, f32[4,2048,64]{1,2,0:T(8,128)S(1)}) %tuple.179, (s32[]{:T(128)}, f32[4,2048]{1,0:T(4,128)S(1)}, s32[]{:T(128)}, ...), branch_computations={%region_6.6_spmd, %region_7.9_spmd} | conditional | flops 1134827520 | bytes 57692248 | solution.py:101
  213.3 4.9 %fusion.7 = f32[4,512]{1,0:T(4,128)S(1)} fusion(f32[512,4,2048]{2,0,1:T(8,128)S(1)} %get-tuple-element.1188, f32[4,512]{1,0:T(4,128)S(1)} %get-tuple-element.1180, pred[512,2048]{1,0:T(8,128)(4,1)S(1)} %fusion.12), kind=kLoop, calls=%fused_computation.8 | loop fusion | flops 20969472 | bytes 17842176 | tf_op jit(solution)/shard_map/while/body/eval_jaxpr/cond/branch_1_fun/reduce_sum | solution.py:88
  219.5 4.6 %fusion.16 = f32[4,2048,64]{1,2,0:T(8,128)S(1)} fusion(f32[4,2048,64]{1,2,0:T(8,128)S(1)} %get-tuple-element.931, s32[]{:T(128)S(6)} %select_n.123, f32[512,4,2048]{2,0,1:T(8,128)S(1)} %get-tuple-element.1188, f32[4,512]{1,0:T(4,128)S(1)} %get-tuple-element.1180, pred[512,2048]{1,0:T(8,128)(4,1)S(1)} %fusion.12, ...), kind=kOutput, calls=%fused_computation.15 | convolution fusion | flops 558104576 | bytes 20201476 | tf_op jit(solution)/shard_map/while/body/eval_jaxpr/cond/branch_1_fun/hqk,kd->hqd/dot_general | solution.py:89
  224.1 31.1 %while.63 = (s32[]{:T(128)}, f32[4,2048]{1,0:T(4,128)S(1)}, f32[4,2048]{1,0:T(4,128)}, f32[4,2048,64]{1,2,0:T(8,128)S(1)}, s32[]{:T(128)}, /*index=5*/s32[]{:T(1...) while((s32[]{:T(128)}, f32[4,2048]{1,0:T(4,128)S(1)}, ...), condition=%wide.region_16.17_spmd.clone.clone, body=%wide.region_11.16_spmd.clone.clone.sunk | while | flops 1134828032 | bytes 58755604 | solution.py:103
  227.5 18.1 %conditional.9 = ((f32[4,2048]{1,0:T(4,128)S(1)}, f32[4,2048]{1,0:T(4,128)}, f32[4,2048,64]{1,2,0:T(8,128)S(1)})) conditional(s32[]{:T(128)} %convert_element_type.158, (f32[4,2048]{1,0:T(4,128)S(1)}, f32[4,2048]{1,0:T(4,128)}, f32[4,2048,64]{1,2,0:T(8,128)S(1)}) %tuple.183, (s32[]{:T(128)}, f32[4,2048]{1,0:T(4,128)S(1)}, s32[]{:T(128)}, ...), branch_computations={%region_12.12_spmd, %region_13.15_spmd} | conditional | flops 1134827520 | bytes 58740852 | solution.py:101
  234.8 4.9 %fusion.30 = f32[4,512]{1,0:T(4,128)S(1)} fusion(f32[512,4,2048]{2,0,1:T(8,128)S(1)} %get-tuple-element.1192, f32[4,512]{1,0:T(4,128)S(1)} %get-tuple-element.1184, pred[512,2048]{1,0:T(8,128)(4,1)S(1)} %fusion.35), kind=kLoop, calls=%fused_computation.35 | loop fusion | flops 20969472 | bytes 17842176 | tf_op jit(solution)/shard_map/while/body/eval_jaxpr/cond/branch_1_fun/reduce_sum | solution.py:88
  256.3 6.9 %convolution_convert_fusion = bf16[2048,2048]{1,0:T(8,128)(2,1)} fusion(bf16[2048,256]{0,1:T(8,128)(2,1)S(1)} %bitcast.113, bf16[2048,256]{1,0:T(8,128)(2,1)} %all-gather.6.cloned.1.call-done), kind=kOutput, calls=%fused_computation.63 | convolution fusion | flops 2151677952 | bytes 10485760 | tf_op jit(solution)/shard_map/dot_general | solution.py:168
  264.2 64.1 %all-to-all-start = ((bf16[16,1,1]{2,1,0:T(2,128)(2,1)}), bf16[16,1,1]{2,1,0:T(2,128)(2,1)S(1)}, u32[]{:S(2)}, u32[]{:S(2)}) async-start(bf16[16,1,1]{2,1,0:T(2,128)(2,1)} %copy.19), calls=%async_computation.1 | async-start | bytes 16384 | tf_op jit(solution)/shard_map/all_to_all | solution.py:200
  330.4 5.0 %all-to-all-done = bf16[16,1,1]{2,1,0:T(2,128)(2,1)S(1)} async-done(((bf16[16,1,1]{2,1,0:T(2,128)(2,1)}), bf16[16,1,1]{2,1,0:T(2,128)(2,1)S(1)}, u32[]{:S(2)}, u32[]{:S(2)}) %all-to-all-start) | async-done | bytes 64 | tf_op jit(solution)/shard_map/all_to_all | solution.py:200
  339.4 80.0 %all-to-all-done.1 = bf16[16,1,64,128]{3,2,1,0:T(8,128)(2,1)S(1)} async-done(((bf16[16,1,64,128]{3,2,1,0:T(8,128)(2,1)}), bf16[16,1,64,128]{3,2,1,0:T(8,128)(2,1)S(1)}, u32[]{:S(2)}, u32[]{:S(2)}) %all-to-all-start.1) | async-done | bytes 262176 | tf_op jit(solution)/shard_map/all_to_all | solution.py:199
  (179 shorter events, 110.5 us)
Async XLA Ops:
  7.2 6.8 %copy-start = (bf16[4,128,128]{2,1,0:T(8,128)(2,1)S(1)}, bf16[4,128,128]{2,1,0:T(8,128)(2,1)}, u32[]{:S(2)}) copy-start(bf16[4,128,128]{2,1,0:T(8,128)(2,1)} %param.20) | copy-start | bytes 393220
  7.2 125.5 %all-gather.4.cloned.1.call-start = ((), (), s32[]{:S(2)}) async-start(), calls=%async_computation.3 | async-start | bytes 1114112 | tf_op jit(solution)/shard_map/all_gather | solution.py:118
  7.9 248.4 %all-gather.6.cloned.1.call-start = ((), (), s32[]{:S(2)}) async-start(), calls=%async_computation.4 | async-start | bytes 1114112 | tf_op jit(solution)/shard_map/all_gather | solution.py:120
  8.8 39.5 %copy-start.7 = (u32[128]{0:T(128)S(1)}, u32[128]{0:T(128)}, u32[]{:S(2)}) copy-start(u32[128]{0:T(128)} %constant.282) | copy-start | bytes 1540
  8.8 40.1 %copy-start.4 = (s32[2048]{0:T(1024)S(1)}, s32[2048]{0:T(1024)}, u32[]{:S(2)}) copy-start(s32[2048]{0:T(1024)} %param.22) | copy-start | bytes 24580
  13.9 118.8 %copy-start.5 = (f32[2048]{0:T(1024)S(1)}, f32[2048]{0:T(1024)}, u32[]{:S(2)}) copy-start(f32[2048]{0:T(1024)} %param.18) | copy-start | bytes 24580
  121.7 17.0 %copy-start.2 = (bf16[2048,128]{0,1:T(8,128)(2,1)}, bf16[2048,128]{0,1:T(8,128)(2,1)S(1)}, u32[]{:S(2)}) copy-start(bf16[2048,128]{0,1:T(8,128)(2,1)S(1)} %pad_maximum_fusion.1) | copy-start | bytes 1572868
  121.7 10.2 %collective-permute-start = (bf16[2048,128]{0,1:T(8,128)(2,1)S(1)}, bf16[2048,128]{0,1:T(8,128)(2,1)S(1)}, u32[]{:S(2)}, u32[]{:S(2)}) collective-permute-start(bf16[2048,128]{0,1:T(8,128)(2,1)S(1)} %pad_maximum_fusion.1), channel_id=1, source_target_pairs={{0,8},{8,16},{16,24},{24,32},{32,40},{40,48},{48,56},{56,64},{64,7... | collective-permute-start | bytes 1572872 | tf_op jit(solution)/shard_map/ppermute | solution.py:29
  125.8 294.6 %reduce-scatter.2.cloned.1.call-start = ((), (), s32[]{:S(2)}) async-start(), calls=%async_computation.5 | async-start | bytes 9437184 | tf_op jit(solution)/shard_map/reduce_scatter | solution.py:171
  230.5 10.5 %copy-start.3 = (bf16[2048,64]{0,1:T(8,128)(2,1)S(1)}, bf16[2048,64]{0,1:T(8,128)(2,1)}, u32[]{:S(2)}) copy-start(bf16[2048,64]{0,1:T(8,128)(2,1)} %get-tuple-element.958) | copy-start | bytes 786436 | tf_op jit(solution)/shard_map/while/body/eval_jaxpr/cond
  255.3 7.9 %copy-start.6 = (s32[16]{0:T(128)S(1)}, s32[16]{0:T(128)}, u32[]{:S(2)}) copy-start(s32[16]{0:T(128)} %param.23) | copy-start | bytes 196
  255.3 165.2 %copy-start.1 = (bf16[4,128,128]{2,1,0:T(8,128)(2,1)S(1)}, bf16[4,128,128]{2,1,0:T(8,128)(2,1)}, u32[]{:S(2)}) copy-start(bf16[4,128,128]{2,1,0:T(8,128)(2,1)} %param.20) | copy-start | bytes 393220
  264.2 71.1 %all-to-all-start = ((bf16[16,1,1]{2,1,0:T(2,128)(2,1)}), bf16[16,1,1]{2,1,0:T(2,128)(2,1)S(1)}, u32[]{:S(2)}, u32[]{:S(2)}) async-start(bf16[16,1,1]{2,1,0:T(2,128)(2,1)} %copy.19), calls=%async_computation.1 | async-start | bytes 16384 | tf_op jit(solution)/shard_map/all_to_all | solution.py:200
  335.4 84.0 %all-to-all-start.1 = ((bf16[16,1,64,128]{3,2,1,0:T(8,128)(2,1)}), bf16[16,1,64,128]{3,2,1,0:T(8,128)(2,1)S(1)}, u32[]{:S(2)}, u32[]{:S(2)}) async-start(bf16[16,1,64,128]{3,2,1,0:T(8,128)(2,1)} %copy.20), calls=%async_computation.2 | async-start | bytes 524288 | tf_op jit(solution)/shard_map/all_to_all | solution.py:199
Sparse Core Ops, SparseCore 0:
  10.5 48.7 all-gather.3
  125.9 47.9 all-gather.5
  263.3 150.4 reduce-scatter.1
where the time goes:
time: 429 us; the launch traced here: 427 us
  waiting for transfers between devices  90.8 us (21%)
  starting transfers between devices  72.3 us (17%)
  matrix products  62.5 us (15%)
  loops' own time  62.3 us (15%)
  other arithmetic  55.8 us (13%)
  local copies, waits for them, and re-layouts  35.2 us (8%)
  blocking collectives  34 us (8%)
  between operations  14 us (3%)
    all_to_all x1, waiting for transfers between devices, body(): lax.all_to_all(outgoing, 'seq', split_axis=0, concat_axis=0, tiled=True)  80 us
    all_to_all x1, starting transfers between devices, body(): lax.all_to_all(labels, 'seq', split_axis=0, concat_axis=0, tiled=True)  64.1 us
    another operation x1, loops' own time, prefix(): return lax.fori_loop(0, count - 1, hop, so_far)  46.2 us
    all_gather x1, blocking collectives, body(): lax.all_gather(kv_own, 'seq', axis=0, tiled=True)  28.4 us
    reduce_sum x5, other arithmetic, compute(): new_total = total_block * factor + jnp.sum(weights, axis=-1)  24.4 us
    dot_general x5, matrix products, compute(): jnp.einsum('hqk,kd->hqd', weights.astype(jnp.bfloat16), value_rows, prefe...  23.1 us
    dot_general x5, matrix products, compute(): jnp.einsum('qhd,kd->hqk', query_block, key_rows, preferred_element_type=j...  21 us
    dynamic_slice x30, local copies, waits for them, and re-layouts, hop(): longer = join(so_far, jax.tree.map(lambda part: part[position], pieces))  17.9 us
  transfers between devices with their start and end apart: 6, of which 3 were waited for; matrix products, arithmetic and copies ran while one was open for 34% of the time, Pallas kernels for 0%

commit v1 on v0

--- a/solution.py
+++ b/solution.py
@@ -7,26 +7,18 @@
 
 W = 2048
 PAGE = 128
-
-
-def prefix(value, axis, join, neutral):
-    count, mine = (lax.axis_size(axis), lax.axis_index(axis))
-    pieces = jax.tree.map(lambda part: lax.all_gather(part, axis), value)
-    so_far = jax.tree.map(
-        lambda part, zero: jnp.full_like(part, 0) + jnp.asarray(zero, part.dtype), value, neutral
-    )
-
-    def hop(position, so_far):
-        longer = join(so_far, jax.tree.map(lambda part: part[position], pieces))
-        return jax.tree.map(lambda new, old: jnp.where(position < mine, new, old), longer, so_far)
-
-    return lax.fori_loop(0, count - 1, hop, so_far)
+SEGS = 32
 
 
 def from_behind(x, axis, by):
     peers = lax.axis_size(axis)
     pairs = [(i, i + by) for i in range(peers) if 0 <= i + by < peers]
     return lax.ppermute(x, axis, pairs)
+
+
+def shift_round(x, axis, by):
+    peers = lax.axis_size(axis)
+    return lax.ppermute(x, axis, [(i, (i + by) % peers) for i in range(peers)])
 
 
 def rotate_half(values, cosine, sine_table):
@@ -37,18 +29,6 @@
         [first_half * cosine - second * sine_table, second * cosine + first_half * sine_table],
         axis=-1,
     )
-
-
-def link_segments(earlier, later):
-    seg_early, start_early = earlier
-    seg_late, start_late = later
-    merged_seg = jnp.maximum(seg_early, seg_late)
-    merged_start = jnp.where(
-        seg_late > seg_early,
-        start_late,
-        jnp.where(seg_early > seg_late, start_early, jnp.minimum(start_early, start_late)),
-    )
-    return (merged_seg, merged_start)
 
 
 def attend_piece(carry, piece, start, queries, query_first, query_start, block_rows):
@@ -114,34 +94,34 @@
     ratio = mp_count // kv_heads
     own_head = mp_index // ratio
     kv_own = lax.dynamic_index_in_dim(kv_weight, own_head, 0, keepdims=False)
-    w_query, w_keyval, w_output = (
-        lax.all_gather(q_weight, "seq", axis=0, tiled=True),
-        lax.all_gather(kv_own, "seq", axis=0, tiled=True),
-        lax.all_gather(out_weight, "seq", axis=0, tiled=True),
-    )
+    q_columns = q_weight.shape[1]
+    w_inputs = lax.all_gather(
+        jnp.concatenate([q_weight, kv_own], axis=1), "seq", axis=0, tiled=True
+    )
+    w_output = lax.all_gather(out_weight, "seq", axis=0, tiled=True)
     inputs = tokens_in.astype(jnp.float32)
     meansq = jnp.mean(inputs * inputs, axis=-1, keepdims=True)
     normed = (inputs * lax.rsqrt(meansq + 1e-05) * norm_gain).astype(jnp.bfloat16)
     token_first = seq_index * tok_rows
     global_index = token_first + jnp.arange(tok_rows, dtype=jnp.int32)
-    boundary = jnp.concatenate([jnp.ones((1,), bool), segment_ids[1:] != segment_ids[:-1]])
-    local_start = lax.cummax(jnp.where(boundary, global_index, jnp.int32(0)), axis=0)
-    prior_seg, prior_start = prefix(
-        (segment_ids[-1], local_start[-1]), "seq", link_segments, (jnp.int32(-1), jnp.int32(0))
-    )
-    query_start = jnp.where(segment_ids == prior_seg, prior_start, local_start)
+    seg_values = jnp.arange(SEGS, dtype=jnp.int32)
+    seg_hist = jnp.sum((segment_ids[:, None] == seg_values[None, :]).astype(jnp.int32), axis=0)
+    seg_total = lax.psum(seg_hist, "seq")
+    seg_first = jnp.cumsum(seg_total) - seg_total
+    query_start = jnp.sum(
+        jnp.where(segment_ids[:, None] == seg_values[None, :], seg_first[None, :], 0), axis=1
+    )
     positions = global_index - query_start
     half = head_size // 2
     freqs = jnp.exp(jnp.arange(half, dtype=jnp.float32) * (-2.0 * math.log(10000.0) / head_size))
     angles = positions.astype(jnp.float32)[:, None] * freqs[None, :]
     cosine = jnp.cos(angles)
     sine_table = jnp.sin(angles)
-    local_heads = w_query.shape[1] // head_size
-    queries = jnp.dot(normed, w_query, preferred_element_type=jnp.float32).reshape(
-        tok_rows, local_heads, head_size
-    )
+    local_heads = q_columns // head_size
+    projected_all = jnp.dot(normed, w_inputs, preferred_element_type=jnp.float32)
+    queries = projected_all[:, :q_columns].reshape(tok_rows, local_heads, head_size)
     queries = rotate_half(queries, cosine[:, None, :], sine_table[:, None, :]).astype(jnp.bfloat16)
-    projected = jnp.dot(normed, w_keyval, preferred_element_type=jnp.float32)
+    projected = projected_all[:, q_columns:]
     key_rows = rotate_half(projected[:, :head_size], cosine, sine_table).astype(jnp.bfloat16)
     value_rows = projected[:, head_size:].astype(jnp.bfloat16)
     keyval = jnp.concatenate([key_rows, value_rows], axis=1)
@@ -183,31 +163,25 @@
     page_order = jnp.arange(pages_dev, dtype=jnp.int32)
     same_owner = (owners[:, None] == owners[None, :]) & (page_order[None, :] < page_order[:, None])
     ranking = jnp.sum(same_owner.astype(jnp.int32), axis=1)
-    send_lane = owners * capacity + ranking
     lanes_all = seq_count * capacity
+    send_lane = ((owners - seq_index) % seq_count) * capacity + ranking
     select = jnp.arange(lanes_all, dtype=jnp.int32)[:, None] == send_lane[None, :]
     outgoing = jnp.einsum(
         "sp,pfk->sfk", select.astype(jnp.bfloat16), page_blocks, preferred_element_type=jnp.float32
     ).astype(jnp.bfloat16)
-    outgoing = outgoing.reshape(seq_count, capacity, share_width, PAGE)
-    labels = (
-        jnp.dot(select.astype(jnp.float32), (local_slot + 1).astype(jnp.float32))
-        .astype(jnp.bfloat16)
-        .reshape(seq_count, capacity)
-    )
-    incoming, tags = (
-        lax.all_to_all(outgoing, "seq", split_axis=0, concat_axis=0, tiled=True),
-        lax.all_to_all(labels, "seq", split_axis=0, concat_axis=0, tiled=True),
-    )
-    tags_flat = tags.reshape(lanes_all).astype(jnp.float32)
-    placement = (tags_flat[None, :] == (page_order + 1).astype(jnp.float32)[:, None]).astype(
-        jnp.bfloat16
-    )
+    labels = jnp.sum(jnp.where(select, (local_slot + 1)[None, :], 0), axis=1)
+    label_rows = jnp.broadcast_to(labels.astype(jnp.bfloat16)[:, None, None], (lanes_all, 1, PAGE))
+    payload = jnp.concatenate([outgoing, label_rows], axis=1)
+    arrived = [payload[:capacity]]
+    for offset in range(1, seq_count):
+        lanes = slice(offset * capacity, (offset + 1) * capacity)
+        arrived.append(shift_round(payload[lanes], "seq", offset))
+    landed = jnp.concatenate(arrived, axis=0)
+    incoming = landed[:, :share_width]
+    tags = landed[:, share_width, 0].astype(jnp.int32)
+    placement = (tags[None, :] == (page_order + 1)[:, None]).astype(jnp.bfloat16)
     kv_cache = jnp.einsum(
-        "ps,sfk->pfk",
-        placement,
-        incoming.reshape(lanes_all, share_width, PAGE),
-        preferred_element_type=jnp.float32,
+        "ps,sfk->pfk", placement, incoming, preferred_element_type=jnp.float32
     ).astype(jnp.bfloat16)
     return (layer_out, kv_cache)
 

time: 429 us -> 357 us (0.83)
  starting transfers between devices: 72.3 us -> 150 us
  waiting for transfers between devices: 90.8 us -> 33 us
  loops' own time: 62.3 us -> 16.2 us
  blocking collectives: 34 us -> 13.7 us
  local copies, waits for them, and re-layouts: 35.2 us -> 16.8 us
  other arithmetic: 55.8 us -> 51.3 us
    ppermute x0 -> x15, starting transfers between devices: none -> 147 us  [shift_round(): return lax.ppermute(x, axis, [(i, (i + by) % peers) for i in range(peers)])]
    all_to_all x2 -> x0, waiting for transfers between devices: 85 us -> none  [the longest x1 80 us: body(): lax.all_to_all(outgoing, 'seq', split_axis=0, concat_axis=0, tiled=True)]
    all_to_all x2 -> x0, starting transfers between devices: 68 us -> none  [the longest x1 64.1 us: body(): lax.all_to_all(labels, 'seq', split_axis=0, concat_axis=0, tiled=True)]
    another operation x1 -> x0, loops' own time: 46.2 us -> none  [prefix(): return lax.fori_loop(0, count - 1, hop, so_far)]
    all_gather x2, waiting for transfers between devices: 0.02 us -> 29.6 us  [the longest x1 29.6 us: body(): lax.all_gather(jnp.concatenate([q_weight, kv_own], axis=1), 'seq', axis=0...]
    all_gather x1 -> x0, blocking collectives: 28.4 us -> none  [body(): lax.all_gather(kv_own, 'seq', axis=0, tiled=True)]
    dynamic_slice x31 -> x0, local copies, waits for them, and re-layouts: 17.9 us -> none  [the longest x30 17.9 us: hop(): longer = join(so_far, jax.tree.map(lambda part: part[position], pieces))]
    psum x0 -> x1, blocking collectives: none -> 13.7 us  [body(): seg_total = lax.psum(seg_hist, 'seq')]
  transfers between devices with their start and end apart: 6 -> 19, of which waited for: 3 -> 3; matrix products, arithmetic and copies ran while one was open for 34% -> 33% of each run, Pallas kernels for 0% -> 0%
where the time goes in v1:
time: 357 us; the launch traced here: 353 us
  starting transfers between devices  150 us (42%)
  matrix products  58.4 us (16%)
  other arithmetic  51.3 us (14%)
  waiting for transfers between devices  33 us (9%)
  local copies, waits for them, and re-layouts  16.8 us (5%)
  loops' own time  16.2 us (5%)
  between operations  14 us (4%)
  blocking collectives  13.7 us (4%)
    ppermute x15, starting transfers between devices, shift_round(): return lax.ppermute(x, axis, [(i, (i + by) % peers) for i in range(peers)])  147 us
    all_gather x1, waiting for transfers between devices, body(): lax.all_gather(jnp.concatenate([q_weight, kv_own], axis=1), 'seq', axis=0...  29.6 us
    reduce_sum x5, other arithmetic, compute(): new_total = total_block * factor + jnp.sum(weights, axis=-1)  24.4 us
    dot_general x5, matrix products, compute(): jnp.einsum('hqk,kd->hqd', weights.astype(jnp.bfloat16), value_rows, prefe...  23.2 us
    dot_general x5, matrix products, compute(): jnp.einsum('qhd,kd->hqk', query_block, key_rows, preferred_element_type=j...  21.2 us
    another operation x2, loops' own time, attend_piece(): return lax.fori_loop(0, blocks, one_block, carry)  15.7 us
    and x5, other arithmetic, compute(): keep = keep & (query_index[:, None] - key_index[None, :] < W)  14.5 us
    psum x1, blocking collectives, body(): seg_total = lax.psum(seg_hist, 'seq')  13.7 us
  transfers between devices with their start and end apart: 19, of which 3 were waited for; matrix products, arithmetic and copies ran while one was open for 33% of the time, Pallas kernels for 0%

profile of v1, /device:TPU:1, one launch (start us, length us, event | category | flops | bytes accessed | tf_op | source)
XLA Modules:
  0.0 353.4 jit_solution(13637084981470361492)
XLA Ops:
  11.2 13.7 %psum.7 = s32[32]{0:T(128)S(1)} all-reduce(s32[32]{0:T(128)S(1)} %convert_reduce_fusion), channel_id=1, replica_groups=mesh['seq'=16,'mp'=8] {'seq'}, use_global_device_ids=true, to_apply=%region_2.3 | all-reduce | flops 32 | bytes 256 | tf_op jit(solution)/shard_map/psum | solution.py:109
  26.0 5.1 %fusion.50 = f32[2048]{0:T(1024)S(1)} fusion(bf16[2048,2048]{1,0:T(8,128)(2,1)} %param.15), kind=kLoop, calls=%fused_computation.60 | loop fusion | flops 12580864 | bytes 8396800 | tf_op jit(solution)/shard_map/reduce_sum | solution.py:103
  31.2 29.6 %all-gather.3.cloned.1.call-done = bf16[2048,384]{1,0:T(8,128)(2,1)} async-done(((bf16[128,384]{1,0:T(8,128)(2,1)}), bf16[2048,384]{1,0:T(8,128)(2,1)}) %all-gather.3.cloned.1.call-update) | async-done | bytes 1572880 | tf_op jit(solution)/shard_map/all_gather | solution.py:98
  60.8 6.6 %fusion.53 = f32[2048,384]{0,1:T(8,128)S(1)} fusion(bf16[2048,384]{1,0:T(8,128)(2,1)} %all-gather.3.cloned.1.call-done, bf16[2048,2048]{1,0:T(8,128)(2,1)} %param.15, f32[2048]{0:T(1024)} %param.16, f32[2048]{0:T(1024)S(1)} %add_rsqrt_fusion), kind=kOutput, calls=%fused_computation.63 | convolution fusion | flops 3238002688 | bytes 13123584 | tf_op jit(solution)/shard_map/dot_general | solution.py:121
  73.8 79.6 %while.46 = (s32[]{:T(128)}, f32[4,2048]{1,0:T(4,128)S(1)}, f32[4,2048]{1,0:T(4,128)S(1)}, f32[4,2048,64]{1,2,0:T(8,128)S(1)}, s32[]{:T(128)}, /*index=5*/s32[20...) while((s32[]{:T(128)}, f32[4,2048]{1,0:T(4,128)S(1)}, ...), condition=%wide.region_10.11_spmd.clone.clone, body=%wide.region_5.10_spmd.clone.clone.sunk | while | flops 1134828032 | bytes 57707496 | solution.py:83
  76.9 16.8 %conditional.8 = ((f32[4,2048]{1,0:T(4,128)S(1)}, f32[4,2048]{1,0:T(4,128)S(1)}, f32[4,2048,64]{1,2,0:T(8,128)S(1)})) conditional(s32[]{:T(128)} %convert_element_type.145, (f32[4,2048]{1,0:T(4,128)S(1)}, f32[4,2048]{1,0:T(4,128)S(1)}, f32[4,2048,64]{1,2,0:T(8,128)S(1)}) %tuple.167, (s32[]{:T(128)}, f32[4,2048]{1,0:T(4,128)S(1)}, s32[]{:T(128)}, ...), branch_computations={%region_6.6_spmd, %region_7.9_spmd} | conditional | flops 1134827520 | bytes 57692752 | solution.py:81
  84.1 4.9 %fusion.7 = f32[4,512]{1,0:T(4,128)S(1)} fusion(f32[512,4,2048]{2,0,1:T(8,128)S(1)} %get-tuple-element.1056, f32[4,512]{1,0:T(4,128)S(1)} %get-tuple-element.1050, pred[512,2048]{1,0:T(8,128)(4,1)S(1)} %fusion.12), kind=kLoop, calls=%fused_computation.8 | loop fusion | flops 20969472 | bytes 17842176 | tf_op jit(solution)/shard_map/while/body/eval_jaxpr/cond/branch_1_fun/reduce_sum | solution.py:68
  89.0 4.6 %fusion.16 = f32[4,2048,64]{1,2,0:T(8,128)S(1)} fusion(f32[4,2048,64]{1,2,0:T(8,128)S(1)} %get-tuple-element.823, s32[]{:T(128)S(6)} %select_n.91, f32[512,4,2048]{2,0,1:T(8,128)S(1)} %get-tuple-element.1056, f32[4,512]{1,0:T(4,128)S(1)} %get-tuple-element.1050, pred[512,2048]{1,0:T(8,128)(4,1)S(1)} %fusion.12, ...), kind=kOutput, calls=%fused_computation.15 | convolution fusion | flops 558104576 | bytes 20201476 | tf_op jit(solution)/shard_map/while/body/eval_jaxpr/cond/branch_1_fun/hqk,kd->hqd/dot_general | solution.py:69
  96.8 16.8 %conditional.8 = ((f32[4,2048]{1,0:T(4,128)S(1)}, f32[4,2048]{1,0:T(4,128)S(1)}, f32[4,2048,64]{1,2,0:T(8,128)S(1)})) conditional(s32[]{:T(128)} %convert_element_type.145, (f32[4,2048]{1,0:T(4,128)S(1)}, f32[4,2048]{1,0:T(4,128)S(1)}, f32[4,2048,64]{1,2,0:T(8,128)S(1)}) %tuple.167, (s32[]{:T(128)}, f32[4,2048]{1,0:T(4,128)S(1)}, s32[]{:T(128)}, ...), branch_computations={%region_6.6_spmd, %region_7.9_spmd} | conditional | flops 1134827520 | bytes 57692752 | solution.py:81
  104.0 4.9 %fusion.7 = f32[4,512]{1,0:T(4,128)S(1)} fusion(f32[512,4,2048]{2,0,1:T(8,128)S(1)} %get-tuple-element.1056, f32[4,512]{1,0:T(4,128)S(1)} %get-tuple-element.1050, pred[512,2048]{1,0:T(8,128)(4,1)S(1)} %fusion.12), kind=kLoop, calls=%fused_computation.8 | loop fusion | flops 20969472 | bytes 17842176 | tf_op jit(solution)/shard_map/while/body/eval_jaxpr/cond/branch_1_fun/reduce_sum | solution.py:68
  108.9 4.6 %fusion.16 = f32[4,2048,64]{1,2,0:T(8,128)S(1)} fusion(f32[4,2048,64]{1,2,0:T(8,128)S(1)} %get-tuple-element.823, s32[]{:T(128)S(6)} %select_n.91, f32[512,4,2048]{2,0,1:T(8,128)S(1)} %get-tuple-element.1056, f32[4,512]{1,0:T(4,128)S(1)} %get-tuple-element.1050, pred[512,2048]{1,0:T(8,128)(4,1)S(1)} %fusion.12, ...), kind=kOutput, calls=%fused_computation.15 | convolution fusion | flops 558104576 | bytes 20201476 | tf_op jit(solution)/shard_map/while/body/eval_jaxpr/cond/branch_1_fun/hqk,kd->hqd/dot_general | solution.py:69
  116.7 16.8 %conditional.8 = ((f32[4,2048]{1,0:T(4,128)S(1)}, f32[4,2048]{1,0:T(4,128)S(1)}, f32[4,2048,64]{1,2,0:T(8,128)S(1)})) conditional(s32[]{:T(128)} %convert_element_type.145, (f32[4,2048]{1,0:T(4,128)S(1)}, f32[4,2048]{1,0:T(4,128)S(1)}, f32[4,2048,64]{1,2,0:T(8,128)S(1)}) %tuple.167, (s32[]{:T(128)}, f32[4,2048]{1,0:T(4,128)S(1)}, s32[]{:T(128)}, ...), branch_computations={%region_6.6_spmd, %region_7.9_spmd} | conditional | flops 1134827520 | bytes 57692752 | solution.py:81
  123.9 4.9 %fusion.7 = f32[4,512]{1,0:T(4,128)S(1)} fusion(f32[512,4,2048]{2,0,1:T(8,128)S(1)} %get-tuple-element.1056, f32[4,512]{1,0:T(4,128)S(1)} %get-tuple-element.1050, pred[512,2048]{1,0:T(8,128)(4,1)S(1)} %fusion.12), kind=kLoop, calls=%fused_computation.8 | loop fusion | flops 20969472 | bytes 17842176 | tf_op jit(solution)/shard_map/while/body/eval_jaxpr/cond/branch_1_fun/reduce_sum | solution.py:68
  128.8 4.6 %fusion.16 = f32[4,2048,64]{1,2,0:T(8,128)S(1)} fusion(f32[4,2048,64]{1,2,0:T(8,128)S(1)} %get-tuple-element.823, s32[]{:T(128)S(6)} %select_n.91, f32[512,4,2048]{2,0,1:T(8,128)S(1)} %get-tuple-element.1056, f32[4,512]{1,0:T(4,128)S(1)} %get-tuple-element.1050, pred[512,2048]{1,0:T(8,128)(4,1)S(1)} %fusion.12, ...), kind=kOutput, calls=%fused_computation.15 | convolution fusion | flops 558104576 | bytes 20201476 | tf_op jit(solution)/shard_map/while/body/eval_jaxpr/cond/branch_1_fun/hqk,kd->hqd/dot_general | solution.py:69
  136.6 16.8 %conditional.8 = ((f32[4,2048]{1,0:T(4,128)S(1)}, f32[4,2048]{1,0:T(4,128)S(1)}, f32[4,2048,64]{1,2,0:T(8,128)S(1)})) conditional(s32[]{:T(128)} %convert_element_type.145, (f32[4,2048]{1,0:T(4,128)S(1)}, f32[4,2048]{1,0:T(4,128)S(1)}, f32[4,2048,64]{1,2,0:T(8,128)S(1)}) %tuple.167, (s32[]{:T(128)}, f32[4,2048]{1,0:T(4,128)S(1)}, s32[]{:T(128)}, ...), branch_computations={%region_6.6_spmd, %region_7.9_spmd} | conditional | flops 1134827520 | bytes 57692752 | solution.py:81
  143.8 4.9 %fusion.7 = f32[4,512]{1,0:T(4,128)S(1)} fusion(f32[512,4,2048]{2,0,1:T(8,128)S(1)} %get-tuple-element.1056, f32[4,512]{1,0:T(4,128)S(1)} %get-tuple-element.1050, pred[512,2048]{1,0:T(8,128)(4,1)S(1)} %fusion.12), kind=kLoop, calls=%fused_computation.8 | loop fusion | flops 20969472 | bytes 17842176 | tf_op jit(solution)/shard_map/while/body/eval_jaxpr/cond/branch_1_fun/reduce_sum | solution.py:68
  148.7 4.6 %fusion.16 = f32[4,2048,64]{1,2,0:T(8,128)S(1)} fusion(f32[4,2048,64]{1,2,0:T(8,128)S(1)} %get-tuple-element.823, s32[]{:T(128)S(6)} %select_n.91, f32[512,4,2048]{2,0,1:T(8,128)S(1)} %get-tuple-element.1056, f32[4,512]{1,0:T(4,128)S(1)} %get-tuple-element.1050, pred[512,2048]{1,0:T(8,128)(4,1)S(1)} %fusion.12, ...), kind=kOutput, calls=%fused_computation.15 | convolution fusion | flops 558104576 | bytes 20201476 | tf_op jit(solution)/shard_map/while/body/eval_jaxpr/cond/branch_1_fun/hqk,kd->hqd/dot_general | solution.py:69
  154.5 29.9 %while.47 = (s32[]{:T(128)}, f32[4,2048]{1,0:T(4,128)S(1)}, f32[4,2048]{1,0:T(4,128)S(1)}, f32[4,2048,64]{1,2,0:T(8,128)S(1)}, s32[]{:T(128)}, /*index=5*/s32[]{...) while((s32[]{:T(128)}, f32[4,2048]{1,0:T(4,128)S(1)}, ...), condition=%wide.region_16.17_spmd.clone.clone, body=%wide.region_11.16_spmd.clone.clone.sunk | while | flops 1134828032 | bytes 57707504 | solution.py:83
  157.9 16.8 %conditional.9 = ((f32[4,2048]{1,0:T(4,128)S(1)}, f32[4,2048]{1,0:T(4,128)S(1)}, f32[4,2048,64]{1,2,0:T(8,128)S(1)})) conditional(s32[]{:T(128)} %convert_element_type.146, (f32[4,2048]{1,0:T(4,128)S(1)}, f32[4,2048]{1,0:T(4,128)S(1)}, f32[4,2048,64]{1,2,0:T(8,128)S(1)}) %tuple.171, (s32[]{:T(128)}, f32[4,2048]{1,0:T(4,128)S(1)}, s32[]{:T(128)}, ...), branch_computations={%region_12.12_spmd, %region_13.15_spmd} | conditional | flops 1134827520 | bytes 57692752 | solution.py:81
  165.2 4.9 %fusion.30 = f32[4,512]{1,0:T(4,128)S(1)} fusion(f32[512,4,2048]{2,0,1:T(8,128)S(1)} %get-tuple-element.1060, f32[4,512]{1,0:T(4,128)S(1)} %get-tuple-element.1054, pred[512,2048]{1,0:T(8,128)(4,1)S(1)} %fusion.35), kind=kLoop, calls=%fused_computation.35 | loop fusion | flops 20969472 | bytes 17842176 | tf_op jit(solution)/shard_map/while/body/eval_jaxpr/cond/branch_1_fun/reduce_sum | solution.py:68
  170.1 4.6 %fusion.39 = f32[4,2048,64]{1,2,0:T(8,128)S(1)} fusion(f32[4,2048,64]{1,2,0:T(8,128)S(1)} %get-tuple-element.849, s32[]{:T(128)S(6)} %select_n.96, f32[512,4,2048]{2,0,1:T(8,128)S(1)} %get-tuple-element.1060, f32[4,512]{1,0:T(4,128)S(1)} %get-tuple-element.1054, pred[512,2048]{1,0:T(8,128)(4,1)S(1)} %fusion.35, ...), kind=kOutput, calls=%fused_computation.42 | convolution fusion | flops 558104576 | bytes 20201476 | tf_op jit(solution)/shard_map/while/body/eval_jaxpr/cond/branch_1_fun/hqk,kd->hqd/dot_general | solution.py:69
  184.6 6.9 %convolution_convert_fusion = bf16[2048,2048]{1,0:T(8,128)(2,1)} fusion(bf16[2048,256]{0,1:T(8,128)(2,1)S(1)} %bitcast.85, bf16[2048,256]{1,0:T(8,128)(2,1)} %all-gather.5.cloned.1.call-done), kind=kOutput, calls=%fused_computation.66 | convolution fusion | flops 2151677952 | bytes 10485760 | tf_op jit(solution)/shard_map/dot_general | solution.py:148
  193.7 50.3 %collective-permute-start.2 = (bf16[1,65,128]{2,0,1:T(2,128)(2,1)S(1)}, bf16[1,65,128]{2,0,1:T(2,128)(2,1)S(1)}, u32[]{:S(2)}, u32[]{:S(2)}) collective-permute-start(bf16[1,65,128]{2,0,1:T(2,128)(2,1)S(1)} %get-tuple-element.1072), channel_id=1, source_target_pairs={{0,16},{8,24},{16,32},{24,40},{32,48},{40,56},{48,64},{56,72},{64,... | collective-permute-start | bytes 49928 | tf_op jit(solution)/shard_map/ppermute | solution.py:21
  261.2 76.5 %collective-permute-start.11 = (bf16[1,65,128]{2,0,1:T(2,128)(2,1)S(1)}, bf16[1,65,128]{2,0,1:T(2,128)(2,1)S(1)}, u32[]{:S(2)}, u32[]{:S(2)}) collective-permute-start(bf16[1,65,128]{2,0,1:T(2,128)(2,1)S(1)} %get-tuple-element.1083), channel_id=1, source_target_pairs={{0,88},{8,96},{16,104},{24,112},{32,120},{40,0},{48,8},{56,16},{64... | collective-permute-start | bytes 49928 | tf_op jit(solution)/shard_map/ppermute | solution.py:21
  (164 shorter events, 87.0 us)
Async XLA Ops:
  7.2 0.9 copy-start
  7.2 53.6 %all-gather.3.cloned.1.call-start = ((), (), s32[]{:S(2)}) async-start(), calls=%async_computation.1 | async-start | bytes 1671168 | tf_op jit(solution)/shard_map/all_gather | solution.py:98
  9.6 175.0 %all-gather.5.cloned.1.call-start = ((), (), s32[]{:S(2)}) async-start(), calls=%async_computation.2 | async-start | bytes 1114112 | tf_op jit(solution)/shard_map/all_gather | solution.py:101
  10.3 336.5 %reduce-scatter.2.cloned.1.call-start = ((), (), s32[]{:S(2)}) async-start(), calls=%async_computation.3 | async-start | bytes 9437184 | tf_op jit(solution)/shard_map/reduce_scatter | solution.py:151
  68.9 4.8 %copy-start.2 = (bf16[2048,128]{0,1:T(8,128)(2,1)}, bf16[2048,128]{0,1:T(8,128)(2,1)S(1)}, u32[]{:S(2)}) copy-start(bf16[2048,128]{0,1:T(8,128)(2,1)S(1)} %pad_maximum_fusion.1) | copy-start | bytes 1572868
  68.9 84.5 %collective-permute-start = (bf16[2048,128]{0,1:T(8,128)(2,1)S(1)}, bf16[2048,128]{0,1:T(8,128)(2,1)}, u32[]{:S(2)}, u32[]{:S(2)}) collective-permute-start(bf16[2048,128]{0,1:T(8,128)(2,1)S(1)} %pad_maximum_fusion.1), channel_id=1, source_target_pairs={{0,8},{8,16},{16,24},{24,32},{32,40},{40,48},{48,56},{56,64},{64,7... | collective-permute-start | bytes 1572872 | tf_op jit(solution)/shard_map/ppermute | solution.py:16
  184.4 7.1 %copy-start.3 = (s32[16]{0:T(128)S(1)}, s32[16]{0:T(128)}, u32[]{:S(2)}) copy-start(s32[16]{0:T(128)} %param.21) | copy-start | bytes 196
  184.4 162.5 %copy-start.1 = (bf16[4,128,128]{2,1,0:T(8,128)(2,1)S(1)}, bf16[4,128,128]{2,1,0:T(8,128)(2,1)}, u32[]{:S(2)}) copy-start(bf16[4,128,128]{2,1,0:T(8,128)(2,1)} %param.18) | copy-start | bytes 393220
  193.4 55.2 %collective-permute-start.1 = (bf16[1,65,128]{2,0,1:T(2,128)(2,1)S(1)}, bf16[1,65,128]{2,0,1:T(2,128)(2,1)S(1)}, u32[]{:S(2)}, u32[]{:S(2)}) collective-permute-start(bf16[1,65,128]{2,0,1:T(2,128)(2,1)S(1)} %get-tuple-element.1071), channel_id=1, source_target_pairs={{0,8},{8,16},{16,24},{24,32},{32,40},{40,48},{48,56},{56,64},{64,7... | collective-permute-start | bytes 49928 | tf_op jit(solution)/shard_map/ppermute | solution.py:21
  193.7 57.2 %collective-permute-start.2 = (bf16[1,65,128]{2,0,1:T(2,128)(2,1)S(1)}, bf16[1,65,128]{2,0,1:T(2,128)(2,1)S(1)}, u32[]{:S(2)}, u32[]{:S(2)}) collective-permute-start(bf16[1,65,128]{2,0,1:T(2,128)(2,1)S(1)} %get-tuple-element.1072), channel_id=1, source_target_pairs={{0,16},{8,24},{16,32},{24,40},{32,48},{40,56},{48,64},{56,72},{64,... | collective-permute-start | bytes 49928 | tf_op jit(solution)/shard_map/ppermute | solution.py:21
  243.9 10.3 %collective-permute-start.3 = (bf16[1,65,128]{2,0,1:T(2,128)(2,1)S(1)}, bf16[1,65,128]{2,0,1:T(2,128)(2,1)S(1)}, u32[]{:S(2)}, u32[]{:S(2)}) collective-permute-start(bf16[1,65,128]{2,0,1:T(2,128)(2,1)S(1)} %get-tuple-element.1073), channel_id=1, source_target_pairs={{0,24},{8,32},{16,40},{24,48},{32,56},{40,64},{48,72},{56,80},{64,... | collective-permute-start | bytes 49928 | tf_op jit(solution)/shard_map/ppermute | solution.py:21
  247.4 8.9 %collective-permute-start.4 = (bf16[1,65,128]{2,0,1:T(2,128)(2,1)S(1)}, bf16[1,65,128]{2,0,1:T(2,128)(2,1)S(1)}, u32[]{:S(2)}, u32[]{:S(2)}) collective-permute-start(bf16[1,65,128]{2,0,1:T(2,128)(2,1)S(1)} %get-tuple-element.1074), channel_id=1, source_target_pairs={{0,32},{8,40},{16,48},{24,56},{32,64},{40,72},{48,80},{56,88},{64,... | collective-permute-start | bytes 49928 | tf_op jit(solution)/shard_map/ppermute | solution.py:21
  247.6 10.9 %collective-permute-start.5 = (bf16[1,65,128]{2,0,1:T(2,128)(2,1)S(1)}, bf16[1,65,128]{2,0,1:T(2,128)(2,1)S(1)}, u32[]{:S(2)}, u32[]{:S(2)}) collective-permute-start(bf16[1,65,128]{2,0,1:T(2,128)(2,1)S(1)} %get-tuple-element.1076), channel_id=1, source_target_pairs={{0,40},{8,48},{16,56},{24,64},{32,72},{40,80},{48,88},{56,96},{64,... | collective-permute-start | bytes 49928 | tf_op jit(solution)/shard_map/ppermute | solution.py:21
  248.6 12.6 %collective-permute-start.6 = (bf16[1,65,128]{2,0,1:T(2,128)(2,1)S(1)}, bf16[1,65,128]{2,0,1:T(2,128)(2,1)S(1)}, u32[]{:S(2)}, u32[]{:S(2)}) collective-permute-start(bf16[1,65,128]{2,0,1:T(2,128)(2,1)S(1)} %get-tuple-element.1077), channel_id=1, source_target_pairs={{0,48},{8,56},{16,64},{24,72},{32,80},{40,88},{48,96},{56,104},{64... | collective-permute-start | bytes 49928 | tf_op jit(solution)/shard_map/ppermute | solution.py:21
  250.9 86.9 %collective-permute-start.7 = (bf16[1,65,128]{2,0,1:T(2,128)(2,1)S(1)}, bf16[1,65,128]{2,0,1:T(2,128)(2,1)S(1)}, u32[]{:S(2)}, u32[]{:S(2)}) collective-permute-start(bf16[1,65,128]{2,0,1:T(2,128)(2,1)S(1)} %get-tuple-element.1078), channel_id=1, source_target_pairs={{0,56},{8,64},{16,72},{24,80},{32,88},{40,96},{48,104},{56,112},{6... | collective-permute-start | bytes 49928 | tf_op jit(solution)/shard_map/ppermute | solution.py:21
  254.2 84.0 %collective-permute-start.8 = (bf16[1,65,128]{2,0,1:T(2,128)(2,1)S(1)}, bf16[1,65,128]{2,0,1:T(2,128)(2,1)S(1)}, u32[]{:S(2)}, u32[]{:S(2)}) collective-permute-start(bf16[1,65,128]{2,0,1:T(2,128)(2,1)S(1)} %get-tuple-element.1079), channel_id=1, source_target_pairs={{0,64},{8,72},{16,80},{24,88},{32,96},{40,104},{48,112},{56,120},{... | collective-permute-start | bytes 49928 | tf_op jit(solution)/shard_map/ppermute | solution.py:21
  256.3 82.8 %collective-permute-start.9 = (bf16[1,65,128]{2,0,1:T(2,128)(2,1)S(1)}, bf16[1,65,128]{2,0,1:T(2,128)(2,1)S(1)}, u32[]{:S(2)}, u32[]{:S(2)}) collective-permute-start(bf16[1,65,128]{2,0,1:T(2,128)(2,1)S(1)} %get-tuple-element.1080), channel_id=1, source_target_pairs={{0,72},{8,80},{16,88},{24,96},{32,104},{40,112},{48,120},{56,0},{6... | collective-permute-start | bytes 49928 | tf_op jit(solution)/shard_map/ppermute | solution.py:21
  258.5 80.6 %collective-permute-start.10 = (bf16[1,65,128]{2,0,1:T(2,128)(2,1)S(1)}, bf16[1,65,128]{2,0,1:T(2,128)(2,1)S(1)}, u32[]{:S(2)}, u32[]{:S(2)}) collective-permute-start(bf16[1,65,128]{2,0,1:T(2,128)(2,1)S(1)} %get-tuple-element.1082), channel_id=1, source_target_pairs={{0,80},{8,88},{16,96},{24,104},{32,112},{40,120},{48,0},{56,8},{64... | collective-permute-start | bytes 49928 | tf_op jit(solution)/shard_map/ppermute | solution.py:21
  261.2 79.2 %collective-permute-start.11 = (bf16[1,65,128]{2,0,1:T(2,128)(2,1)S(1)}, bf16[1,65,128]{2,0,1:T(2,128)(2,1)S(1)}, u32[]{:S(2)}, u32[]{:S(2)}) collective-permute-start(bf16[1,65,128]{2,0,1:T(2,128)(2,1)S(1)} %get-tuple-element.1083), channel_id=1, source_target_pairs={{0,88},{8,96},{16,104},{24,112},{32,120},{40,0},{48,8},{56,16},{64... | collective-permute-start | bytes 49928 | tf_op jit(solution)/shard_map/ppermute | solution.py:21
  337.7 4.3 %collective-permute-start.12 = (bf16[1,65,128]{2,0,1:T(2,128)(2,1)S(1)}, bf16[1,65,128]{2,0,1:T(2,128)(2,1)S(1)}, u32[]{:S(2)}, u32[]{:S(2)}) collective-permute-start(bf16[1,65,128]{2,0,1:T(2,128)(2,1)S(1)} %get-tuple-element.1084), channel_id=1, source_target_pairs={{0,96},{8,104},{16,112},{24,120},{32,0},{40,8},{48,16},{56,24},{64... | collective-permute-start | bytes 49928 | tf_op jit(solution)/shard_map/ppermute | solution.py:21
  338.2 4.8 %collective-permute-start.13 = (bf16[1,65,128]{2,0,1:T(2,128)(2,1)S(1)}, bf16[1,65,128]{2,0,1:T(2,128)(2,1)S(1)}, u32[]{:S(2)}, u32[]{:S(2)}) collective-permute-start(bf16[1,65,128]{2,0,1:T(2,128)(2,1)S(1)} %get-tuple-element.1081), channel_id=1, source_target_pairs={{0,104},{8,112},{16,120},{24,0},{32,8},{40,16},{48,24},{56,32},{64... | collective-permute-start | bytes 49928 | tf_op jit(solution)/shard_map/ppermute | solution.py:21
  339.1 3.9 %collective-permute-start.14 = (bf16[1,65,128]{2,0,1:T(2,128)(2,1)S(1)}, bf16[1,65,128]{2,0,1:T(2,128)(2,1)S(1)}, u32[]{:S(2)}, u32[]{:S(2)}) collective-permute-start(bf16[1,65,128]{2,0,1:T(2,128)(2,1)S(1)} %get-tuple-element.1075), channel_id=1, source_target_pairs={{0,112},{8,120},{16,0},{24,8},{32,16},{40,24},{48,32},{56,40},{64,... | collective-permute-start | bytes 49928 | tf_op jit(solution)/shard_map/ppermute | solution.py:21
  339.1 3.9 %collective-permute-start.15 = (bf16[1,65,128]{2,0,1:T(2,128)(2,1)S(1)}, bf16[1,65,128]{2,0,1:T(2,128)(2,1)S(1)}, u32[]{:S(2)}, u32[]{:S(2)}) collective-permute-start(bf16[1,65,128]{2,0,1:T(2,128)(2,1)S(1)} %get-tuple-element.1069), channel_id=1, source_target_pairs={{0,120},{8,0},{16,8},{24,16},{32,24},{40,32},{48,40},{56,48},{64,5... | collective-permute-start | bytes 49928 | tf_op jit(solution)/shard_map/ppermute | solution.py:21
Sparse Core Ops, SparseCore 0:
  11.0 49.6 all-gather.2
  63.2 45.6 all-gather.4
  191.6 141.0 reduce-scatter.1

commit v2 on v1

--- a/solution.py
+++ b/solution.py
@@ -148,9 +148,14 @@
     partial_term = lax.dot_general(
         attended, w_output, (((1,), (1,)), ((), ())), preferred_element_type=jnp.float32
     )
-    layer_out = lax.psum_scatter(
-        partial_term.astype(jnp.bfloat16), "mp", scatter_dimension=1, tiled=True
-    )
+    out_width = partial_term.shape[1] // mp_count
+    partial_groups = partial_term.astype(jnp.bfloat16).reshape(tok_rows, mp_count, out_width)
+    summed = partial_groups[:, mp_index].astype(jnp.float32)
+    for offset in range(1, mp_count):
+        target = (mp_index + offset) % mp_count
+        sent = shift_round(partial_groups[:, target], "mp", offset)
+        summed = summed + sent.astype(jnp.float32)
+    layer_out = summed.astype(jnp.bfloat16)
     pages_dev = tok_rows // PAGE
     share_width = 2 * head_size // ratio
     share_index = mp_index % ratio

time: 357 us -> 413 us (1.16)
  waiting for transfers between devices: 33 us -> 112 us
  starting transfers between devices: 150 us -> 103 us
  local copies, waits for them, and re-layouts: 16.8 us -> 34.2 us
  other arithmetic: 51.3 us -> 57.1 us
    ppermute x15 -> x22, waiting for transfers between devices: 2.63 us -> 82.5 us  [shift_round(): return lax.ppermute(x, axis, [(i, (i + by) % peers) for i in range(peers)])]
    ppermute x15 -> x22, starting transfers between devices: 147 us -> 100 us  [shift_round(): return lax.ppermute(x, axis, [(i, (i + by) % peers) for i in range(peers)])]
    dynamic_slice x0 -> x8, local copies, waits for them, and re-layouts: none -> 16.5 us  [the longest x7 14 us: body(): sent = shift_round(partial_groups[:, target], 'mp', offset)]
    convert_element_type x0 -> x1, other arithmetic: none -> 4.82 us  [body(): layer_out = summed.astype(jnp.bfloat16)]
  transfers between devices with their start and end apart: 19 -> 25, of which waited for: 3 -> 10; matrix products, arithmetic and copies ran while one was open for 33% -> 32% of each run, Pallas kernels for 0% -> 0%
where the time goes in v2:
time: 413 us; the launch traced here: 408 us
  waiting for transfers between devices  112 us (27%)
  starting transfers between devices  103 us (25%)
  other arithmetic  57.1 us (14%)
  matrix products  55.8 us (14%)
  local copies, waits for them, and re-layouts  34.2 us (8%)
  loops' own time  16.7 us (4%)
  between operations  14.5 us (4%)
  blocking collectives  14.1 us (3%)
    ppermute x22, starting transfers between devices, shift_round(): return lax.ppermute(x, axis, [(i, (i + by) % peers) for i in range(peers)])  100 us
    ppermute x22, waiting for transfers between devices, shift_round(): return lax.ppermute(x, axis, [(i, (i + by) % peers) for i in range(peers)])  82.5 us
    all_gather x1, waiting for transfers between devices, body(): lax.all_gather(jnp.concatenate([q_weight, kv_own], axis=1), 'seq', axis=0...  29.3 us
    reduce_sum x5, other arithmetic, compute(): new_total = total_block * factor + jnp.sum(weights, axis=-1)  24.4 us
    dot_general x5, matrix products, compute(): jnp.einsum('hqk,kd->hqd', weights.astype(jnp.bfloat16), value_rows, prefe...  23.2 us
    dot_general x5, matrix products, compute(): jnp.einsum('qhd,kd->hqk', query_block, key_rows, preferred_element_type=j...  21.9 us
    another operation x2, loops' own time, attend_piece(): return lax.fori_loop(0, blocks, one_block, carry)  16.3 us
    and x5, other arithmetic, compute(): keep = keep & (query_index[:, None] - key_index[None, :] < W)  14.5 us
  transfers between devices with their start and end apart: 25, of which 10 were waited for; matrix products, arithmetic and copies ran while one was open for 32% of the time, Pallas kernels for 0%

profile of v2, /device:TPU:1, one launch (start us, length us, event | category | flops | bytes accessed | tf_op | source)
XLA Modules:
  0.0 408.4 jit_solution(17382293755825889251)
XLA Ops:
  10.5 5.1 %fusion.50 = f32[2048]{0:T(1024)S(1)} fusion(bf16[2048,2048]{1,0:T(8,128)(2,1)} %param.15), kind=kLoop, calls=%fused_computation.60 | loop fusion | flops 12580864 | bytes 8396800 | tf_op jit(solution)/shard_map/reduce_sum | solution.py:103
  15.7 14.1 %psum.7 = s32[32]{0:T(128)S(1)} all-reduce(s32[32]{0:T(128)S(1)} %convert_reduce_fusion), channel_id=1, replica_groups=mesh['seq'=16,'mp'=8] {'seq'}, use_global_device_ids=true, to_apply=%region_2.3 | all-reduce | flops 32 | bytes 256 | tf_op jit(solution)/shard_map/psum | solution.py:109
  31.5 29.3 %all-gather.3.cloned.1.call-done = bf16[2048,384]{1,0:T(8,128)(2,1)} async-done(((bf16[128,384]{1,0:T(8,128)(2,1)}), bf16[2048,384]{1,0:T(8,128)(2,1)}) %all-gather.3.cloned.1.call-update) | async-done | bytes 1572880 | tf_op jit(solution)/shard_map/all_gather | solution.py:98
  60.8 6.6 %fusion.53 = f32[2048,384]{0,1:T(8,128)S(1)} fusion(bf16[2048,384]{1,0:T(8,128)(2,1)} %all-gather.3.cloned.1.call-done, bf16[2048,2048]{1,0:T(8,128)(2,1)} %param.15, f32[2048]{0:T(1024)S(1)} %copy-done.9, f32[2048]{0:T(1024)S(1)} %add_rsqrt_fusion), kind=kOutput, calls=%fused_computation.63 | convolution fusion | flops 3238002688 | bytes 13123584 | tf_op jit(solution)/shard_map/dot_general | solution.py:121
  74.6 80.8 %while.46 = (s32[]{:T(128)}, f32[4,2048]{1,0:T(4,128)S(1)}, f32[4,2048]{1,0:T(4,128)S(1)}, f32[4,2048,64]{1,2,0:T(8,128)S(1)}, s32[]{:T(128)}, /*index=5*/s32[20...) while((s32[]{:T(128)}, f32[4,2048]{1,0:T(4,128)S(1)}, ...), condition=%wide.region_10.11_spmd.clone.clone, body=%wide.region_5.10_spmd.clone.clone.sunk | while | flops 1134828032 | bytes 57707488 | solution.py:83
  77.8 17.0 %conditional.8 = ((f32[4,2048]{1,0:T(4,128)S(1)}, f32[4,2048]{1,0:T(4,128)S(1)}, f32[4,2048,64]{1,2,0:T(8,128)S(1)})) conditional(s32[]{:T(128)} %convert_element_type.194, (f32[4,2048]{1,0:T(4,128)S(1)}, f32[4,2048]{1,0:T(4,128)S(1)}, f32[4,2048,64]{1,2,0:T(8,128)S(1)}) %tuple.174, (s32[]{:T(128)}, f32[4,2048]{1,0:T(4,128)S(1)}, s32[]{:T(128)}, ...), branch_computations={%region_6.6_spmd, %region_7.9_spmd} | conditional | flops 1134827520 | bytes 57692752 | solution.py:81
  85.2 4.9 %fusion.7 = f32[4,512]{1,0:T(4,128)S(1)} fusion(f32[512,4,2048]{2,0,1:T(8,128)S(1)} %get-tuple-element.1056, f32[4,512]{1,0:T(4,128)S(1)} %get-tuple-element.1050, pred[512,2048]{1,0:T(8,128)(4,1)S(1)} %fusion.12), kind=kLoop, calls=%fused_computation.8 | loop fusion | flops 20969472 | bytes 17842176 | tf_op jit(solution)/shard_map/while/body/eval_jaxpr/cond/branch_1_fun/reduce_sum | solution.py:68
  98.0 17.0 %conditional.8 = ((f32[4,2048]{1,0:T(4,128)S(1)}, f32[4,2048]{1,0:T(4,128)S(1)}, f32[4,2048,64]{1,2,0:T(8,128)S(1)})) conditional(s32[]{:T(128)} %convert_element_type.194, (f32[4,2048]{1,0:T(4,128)S(1)}, f32[4,2048]{1,0:T(4,128)S(1)}, f32[4,2048,64]{1,2,0:T(8,128)S(1)}) %tuple.174, (s32[]{:T(128)}, f32[4,2048]{1,0:T(4,128)S(1)}, s32[]{:T(128)}, ...), branch_computations={%region_6.6_spmd, %region_7.9_spmd} | conditional | flops 1134827520 | bytes 57692752 | solution.py:81
  105.4 4.9 %fusion.7 = f32[4,512]{1,0:T(4,128)S(1)} fusion(f32[512,4,2048]{2,0,1:T(8,128)S(1)} %get-tuple-element.1056, f32[4,512]{1,0:T(4,128)S(1)} %get-tuple-element.1050, pred[512,2048]{1,0:T(8,128)(4,1)S(1)} %fusion.12), kind=kLoop, calls=%fused_computation.8 | loop fusion | flops 20969472 | bytes 17842176 | tf_op jit(solution)/shard_map/while/body/eval_jaxpr/cond/branch_1_fun/reduce_sum | solution.py:68
  110.3 4.6 %fusion.16 = f32[4,2048,64]{1,2,0:T(8,128)S(1)} fusion(f32[4,2048,64]{1,2,0:T(8,128)S(1)} %get-tuple-element.823, s32[]{:T(128)S(6)} %select_n.128, f32[512,4,2048]{2,0,1:T(8,128)S(1)} %get-tuple-element.1056, f32[4,512]{1,0:T(4,128)S(1)} %get-tuple-element.1050, pred[512,2048]{1,0:T(8,128)(4,1)S(1)} %fusion.12, ...), kind=kOutput, calls=%fused_computation.15 | convolution fusion | flops 558104576 | bytes 20201476 | tf_op jit(solution)/shard_map/while/body/eval_jaxpr/cond/branch_1_fun/hqk,kd->hqd/dot_general | solution.py:69
  118.2 17.0 %conditional.8 = ((f32[4,2048]{1,0:T(4,128)S(1)}, f32[4,2048]{1,0:T(4,128)S(1)}, f32[4,2048,64]{1,2,0:T(8,128)S(1)})) conditional(s32[]{:T(128)} %convert_element_type.194, (f32[4,2048]{1,0:T(4,128)S(1)}, f32[4,2048]{1,0:T(4,128)S(1)}, f32[4,2048,64]{1,2,0:T(8,128)S(1)}) %tuple.174, (s32[]{:T(128)}, f32[4,2048]{1,0:T(4,128)S(1)}, s32[]{:T(128)}, ...), branch_computations={%region_6.6_spmd, %region_7.9_spmd} | conditional | flops 1134827520 | bytes 57692752 | solution.py:81
  125.6 4.9 %fusion.7 = f32[4,512]{1,0:T(4,128)S(1)} fusion(f32[512,4,2048]{2,0,1:T(8,128)S(1)} %get-tuple-element.1056, f32[4,512]{1,0:T(4,128)S(1)} %get-tuple-element.1050, pred[512,2048]{1,0:T(8,128)(4,1)S(1)} %fusion.12), kind=kLoop, calls=%fused_computation.8 | loop fusion | flops 20969472 | bytes 17842176 | tf_op jit(solution)/shard_map/while/body/eval_jaxpr/cond/branch_1_fun/reduce_sum | solution.py:68
  138.4 17.0 %conditional.8 = ((f32[4,2048]{1,0:T(4,128)S(1)}, f32[4,2048]{1,0:T(4,128)S(1)}, f32[4,2048,64]{1,2,0:T(8,128)S(1)})) conditional(s32[]{:T(128)} %convert_element_type.194, (f32[4,2048]{1,0:T(4,128)S(1)}, f32[4,2048]{1,0:T(4,128)S(1)}, f32[4,2048,64]{1,2,0:T(8,128)S(1)}) %tuple.174, (s32[]{:T(128)}, f32[4,2048]{1,0:T(4,128)S(1)}, s32[]{:T(128)}, ...), branch_computations={%region_6.6_spmd, %region_7.9_spmd} | conditional | flops 1134827520 | bytes 57692752 | solution.py:81
  145.8 4.9 %fusion.7 = f32[4,512]{1,0:T(4,128)S(1)} fusion(f32[512,4,2048]{2,0,1:T(8,128)S(1)} %get-tuple-element.1056, f32[4,512]{1,0:T(4,128)S(1)} %get-tuple-element.1050, pred[512,2048]{1,0:T(8,128)(4,1)S(1)} %fusion.12), kind=kLoop, calls=%fused_computation.8 | loop fusion | flops 20969472 | bytes 17842176 | tf_op jit(solution)/shard_map/while/body/eval_jaxpr/cond/branch_1_fun/reduce_sum | solution.py:68
  155.5 30.5 %while.47 = (s32[]{:T(128)}, f32[4,2048]{1,0:T(4,128)S(1)}, f32[4,2048]{1,0:T(4,128)S(1)}, f32[4,2048,64]{1,2,0:T(8,128)S(1)}, s32[]{:T(128)}, /*index=5*/s32[]{...) while((s32[]{:T(128)}, f32[4,2048]{1,0:T(4,128)S(1)}, ...), condition=%wide.region_16.17_spmd.clone.clone, body=%wide.region_11.16_spmd.clone.clone.sunk | while | flops 1134828032 | bytes 57707496 | solution.py:83
  159.0 16.8 %conditional.9 = ((f32[4,2048]{1,0:T(4,128)S(1)}, f32[4,2048]{1,0:T(4,128)S(1)}, f32[4,2048,64]{1,2,0:T(8,128)S(1)})) conditional(s32[]{:T(128)} %convert_element_type.195, (f32[4,2048]{1,0:T(4,128)S(1)}, f32[4,2048]{1,0:T(4,128)S(1)}, f32[4,2048,64]{1,2,0:T(8,128)S(1)}) %tuple.178, (s32[]{:T(128)}, f32[4,2048]{1,0:T(4,128)S(1)}, s32[]{:T(128)}, ...), branch_computations={%region_12.12_spmd, %region_13.15_spmd} | conditional | flops 1134827520 | bytes 57692752 | solution.py:81
  166.3 4.9 %fusion.30 = f32[4,512]{1,0:T(4,128)S(1)} fusion(f32[512,4,2048]{2,0,1:T(8,128)S(1)} %get-tuple-element.1060, f32[4,512]{1,0:T(4,128)S(1)} %get-tuple-element.1054, pred[512,2048]{1,0:T(8,128)(4,1)S(1)} %fusion.35), kind=kLoop, calls=%fused_computation.35 | loop fusion | flops 20969472 | bytes 17842176 | tf_op jit(solution)/shard_map/while/body/eval_jaxpr/cond/branch_1_fun/reduce_sum | solution.py:68
  202.1 51.4 %collective-permute-start.10 = (bf16[1,65,128]{2,0,1:T(2,128)(2,1)S(1)}, bf16[1,65,128]{2,0,1:T(2,128)(2,1)S(1)}, u32[]{:S(2)}, u32[]{:S(2)}) collective-permute-start(bf16[1,65,128]{2,0,1:T(2,128)(2,1)S(1)} %get-tuple-element.1081), channel_id=1, source_target_pairs={{0,24},{8,32},{16,40},{24,48},{32,56},{40,64},{48,72},{56,80},{64,... | collective-permute-start | bytes 49928 | tf_op jit(solution)/shard_map/ppermute | solution.py:21
  257.8 15.8 %collective-permute-start.13 = (bf16[1,65,128]{2,0,1:T(2,128)(2,1)S(1)}, bf16[1,65,128]{2,0,1:T(2,128)(2,1)S(1)}, u32[]{:S(2)}, u32[]{:S(2)}) collective-permute-start(bf16[1,65,128]{2,0,1:T(2,128)(2,1)S(1)} %get-tuple-element.1085), channel_id=1, source_target_pairs={{0,48},{8,56},{16,64},{24,72},{32,80},{40,88},{48,96},{56,104},{64... | collective-permute-start | bytes 49928 | tf_op jit(solution)/shard_map/ppermute | solution.py:21
  273.6 23.7 %collective-permute-done.11 = bf16[1,65,128]{2,0,1:T(2,128)(2,1)S(1)} collective-permute-done((bf16[1,65,128]{2,0,1:T(2,128)(2,1)S(1)}, bf16[1,65,128]{2,0,1:T(2,128)(2,1)S(1)}, u32[]{:S(2)}, u32[]{:S(2)}) %collective-permute-start.11) | collective-permute-done | bytes 16672 | tf_op jit(solution)/shard_map/ppermute | solution.py:21
  310.0 6.6 %collective-permute-start.18 = (bf16[1,65,128]{2,0,1:T(2,128)(2,1)}, bf16[1,65,128]{2,0,1:T(2,128)(2,1)}, u32[]{:S(2)}, u32[]{:S(2)}) collective-permute-start(bf16[1,65,128]{2,0,1:T(2,128)(2,1)} %get-tuple-element.1091), channel_id=1, source_target_pairs={{0,88},{8,96},{16,104},{24,112},{32,120},{40,0},{48,8},{56,16},{64... | collective-permute-start | bytes 49928 | tf_op jit(solution)/shard_map/ppermute | solution.py:21
  339.4 34.6 %collective-permute-done.3 = bf16[2048,256]{1,0:T(8,128)(2,1)S(1)} collective-permute-done((bf16[2048,256]{1,0:T(8,128)(2,1)}, bf16[2048,256]{1,0:T(8,128)(2,1)S(1)}, u32[]{:S(2)}, u32[]{:S(2)}) %collective-permute-start.3) | collective-permute-done | bytes 1048608 | tf_op jit(solution)/shard_map/ppermute | solution.py:21
  378.1 18.6 %collective-permute-done.7 = bf16[2048,256]{1,0:T(8,128)(2,1)} collective-permute-done((bf16[2048,256]{1,0:T(8,128)(2,1)}, bf16[2048,256]{1,0:T(8,128)(2,1)}, u32[]{:S(2)}, u32[]{:S(2)}) %collective-permute-start.7) | collective-permute-done | bytes 1048608 | tf_op jit(solution)/shard_map/ppermute | solution.py:21
  396.7 4.8 %fusion.63 = bf16[2048,256]{1,0:T(8,128)(2,1)} fusion(bf16[2048,256]{1,0:T(8,128)(2,1)} %collective-permute-done.7, bf16[2048,256]{1,0:T(8,128)(2,1)} %collective-permute-done.6, bf16[2048,256]{1,0:T(8,128)(2,1)} %collective-permute-done.5, bf16[2048,256]{1,0:T(8,128)(2,1)} %collective-permute-done.4, bf16[2048,256]{1,0:T(8,128)(2,1)S(1)} %collective-permute-done.3, ...), kind=kLoop, calls=%fused_computation.74 | loop fusion | flops 8388608 | bytes 9437184 | tf_op jit(solution)/shard_map/convert_element_type | solution.py:158
  (201 shorter events, 137.4 us)
Async XLA Ops:
  7.2 53.6 %all-gather.3.cloned.1.call-start = ((), (), s32[]{:S(2)}) async-start(), calls=%async_computation | async-start | bytes 1671168 | tf_op jit(solution)/shard_map/all_gather | solution.py:98
  9.6 176.6 %all-gather.5.cloned.1.call-start = ((), (), s32[]{:S(2)}) async-start(), calls=%async_computation.1 | async-start | bytes 1114112 | tf_op jit(solution)/shard_map/all_gather | solution.py:101
  69.7 85.7 %collective-permute-start = (bf16[2048,128]{0,1:T(8,128)(2,1)S(1)}, bf16[2048,128]{0,1:T(8,128)(2,1)S(1)}, u32[]{:S(2)}, u32[]{:S(2)}) collective-permute-start(bf16[2048,128]{0,1:T(8,128)(2,1)S(1)} %pad_maximum_fusion.1), channel_id=1, source_target_pairs={{0,8},{8,16},{16,24},{24,32},{32,40},{40,48},{48,56},{56,64},{64,7... | collective-permute-start | bytes 1572872 | tf_op jit(solution)/shard_map/ppermute | solution.py:16
  194.6 137.7 %collective-permute-start.1 = (bf16[2048,256]{1,0:T(8,128)(2,1)}, bf16[2048,256]{1,0:T(8,128)(2,1)}, u32[]{:S(2)}, u32[]{:S(2)}) collective-permute-start(bf16[2048,256]{1,0:T(8,128)(2,1)} %bitcast.100), channel_id=1, source_target_pairs={{0,1},{1,2},{2,3},{3,4},{4,5},{5,6},{6,7},{7,0},{8,9},{9,10},{10,1... | collective-permute-start | bytes 3145736 | tf_op jit(solution)/shard_map/ppermute | solution.py:21
  198.0 134.2 %collective-permute-start.2 = (bf16[2048,256]{1,0:T(8,128)(2,1)}, bf16[2048,256]{1,0:T(8,128)(2,1)}, u32[]{:S(2)}, u32[]{:S(2)}) collective-permute-start(bf16[2048,256]{1,0:T(8,128)(2,1)} %bitcast.99), channel_id=1, source_target_pairs={{0,2},{1,3},{2,4},{3,5},{4,6},{5,7},{6,0},{7,1},{8,10},{9,11},{10,... | collective-permute-start | bytes 3145736 | tf_op jit(solution)/shard_map/ppermute | solution.py:21
  202.1 55.8 %collective-permute-start.10 = (bf16[1,65,128]{2,0,1:T(2,128)(2,1)S(1)}, bf16[1,65,128]{2,0,1:T(2,128)(2,1)S(1)}, u32[]{:S(2)}, u32[]{:S(2)}) collective-permute-start(bf16[1,65,128]{2,0,1:T(2,128)(2,1)S(1)} %get-tuple-element.1081), channel_id=1, source_target_pairs={{0,24},{8,32},{16,40},{24,48},{32,56},{40,64},{48,72},{56,80},{64,... | collective-permute-start | bytes 49928 | tf_op jit(solution)/shard_map/ppermute | solution.py:21
  253.5 43.8 %collective-permute-start.11 = (bf16[1,65,128]{2,0,1:T(2,128)(2,1)S(1)}, bf16[1,65,128]{2,0,1:T(2,128)(2,1)S(1)}, u32[]{:S(2)}, u32[]{:S(2)}) collective-permute-start(bf16[1,65,128]{2,0,1:T(2,128)(2,1)S(1)} %get-tuple-element.1082), channel_id=1, source_target_pairs={{0,32},{8,40},{16,48},{24,56},{32,64},{40,72},{48,80},{56,88},{64,... | collective-permute-start | bytes 49928 | tf_op jit(solution)/shard_map/ppermute | solution.py:21
  253.7 43.8 %collective-permute-start.12 = (bf16[1,65,128]{2,0,1:T(2,128)(2,1)S(1)}, bf16[1,65,128]{2,0,1:T(2,128)(2,1)S(1)}, u32[]{:S(2)}, u32[]{:S(2)}) collective-permute-start(bf16[1,65,128]{2,0,1:T(2,128)(2,1)S(1)} %get-tuple-element.1084), channel_id=1, source_target_pairs={{0,40},{8,48},{16,56},{24,64},{32,72},{40,80},{48,88},{56,96},{64,... | collective-permute-start | bytes 49928 | tf_op jit(solution)/shard_map/ppermute | solution.py:21
  257.8 42.5 %collective-permute-start.13 = (bf16[1,65,128]{2,0,1:T(2,128)(2,1)S(1)}, bf16[1,65,128]{2,0,1:T(2,128)(2,1)S(1)}, u32[]{:S(2)}, u32[]{:S(2)}) collective-permute-start(bf16[1,65,128]{2,0,1:T(2,128)(2,1)S(1)} %get-tuple-element.1085), channel_id=1, source_target_pairs={{0,48},{8,56},{16,64},{24,72},{32,80},{40,88},{48,96},{56,104},{64... | collective-permute-start | bytes 49928 | tf_op jit(solution)/shard_map/ppermute | solution.py:21
  297.3 6.0 %collective-permute-start.14 = (bf16[1,65,128]{2,0,1:T(2,128)(2,1)S(1)}, bf16[1,65,128]{2,0,1:T(2,128)(2,1)S(1)}, u32[]{:S(2)}, u32[]{:S(2)}) collective-permute-start(bf16[1,65,128]{2,0,1:T(2,128)(2,1)S(1)} %get-tuple-element.1086), channel_id=1, source_target_pairs={{0,56},{8,64},{16,72},{24,80},{32,88},{40,96},{48,104},{56,112},{6... | collective-permute-start | bytes 49928 | tf_op jit(solution)/shard_map/ppermute | solution.py:21
  297.5 5.8 %collective-permute-start.15 = (bf16[1,65,128]{2,0,1:T(2,128)(2,1)S(1)}, bf16[1,65,128]{2,0,1:T(2,128)(2,1)S(1)}, u32[]{:S(2)}, u32[]{:S(2)}) collective-permute-start(bf16[1,65,128]{2,0,1:T(2,128)(2,1)S(1)} %get-tuple-element.1087), channel_id=1, source_target_pairs={{0,64},{8,72},{16,80},{24,88},{32,96},{40,104},{48,112},{56,120},{... | collective-permute-start | bytes 49928 | tf_op jit(solution)/shard_map/ppermute | solution.py:21
  300.3 5.0 %collective-permute-start.16 = (bf16[1,65,128]{2,0,1:T(2,128)(2,1)S(1)}, bf16[1,65,128]{2,0,1:T(2,128)(2,1)}, u32[]{:S(2)}, u32[]{:S(2)}) collective-permute-start(bf16[1,65,128]{2,0,1:T(2,128)(2,1)S(1)} %get-tuple-element.1088), channel_id=1, source_target_pairs={{0,72},{8,80},{16,88},{24,96},{32,104},{40,112},{48,120},{56,0},{6... | collective-permute-start | bytes 49928 | tf_op jit(solution)/shard_map/ppermute | solution.py:21
  303.3 5.1 %collective-permute-start.22 = (bf16[1,65,128]{2,0,1:T(2,128)(2,1)S(1)}, bf16[1,65,128]{2,0,1:T(2,128)(2,1)}, u32[]{:S(2)}, u32[]{:S(2)}) collective-permute-start(bf16[1,65,128]{2,0,1:T(2,128)(2,1)S(1)} %get-tuple-element.1077), channel_id=1, source_target_pairs={{0,120},{8,0},{16,8},{24,16},{32,24},{40,32},{48,40},{56,48},{64,5... | collective-permute-start | bytes 49928 | tf_op jit(solution)/shard_map/ppermute | solution.py:21
  305.3 4.7 %collective-permute-start.8 = (bf16[1,65,128]{2,0,1:T(2,128)(2,1)S(1)}, bf16[1,65,128]{2,0,1:T(2,128)(2,1)S(1)}, u32[]{:S(2)}, u32[]{:S(2)}) collective-permute-start(bf16[1,65,128]{2,0,1:T(2,128)(2,1)S(1)} %get-tuple-element.1079), channel_id=1, source_target_pairs={{0,8},{8,16},{16,24},{24,32},{32,40},{40,48},{48,56},{56,64},{64,7... | collective-permute-start | bytes 49928 | tf_op jit(solution)/shard_map/ppermute | solution.py:21
  307.9 8.7 %collective-permute-start.9 = (bf16[1,65,128]{2,0,1:T(2,128)(2,1)S(1)}, bf16[1,65,128]{2,0,1:T(2,128)(2,1)S(1)}, u32[]{:S(2)}, u32[]{:S(2)}) collective-permute-start(bf16[1,65,128]{2,0,1:T(2,128)(2,1)S(1)} %get-tuple-element.1080), channel_id=1, source_target_pairs={{0,16},{8,24},{16,32},{24,40},{32,48},{40,56},{48,64},{56,72},{64,... | collective-permute-start | bytes 49928 | tf_op jit(solution)/shard_map/ppermute | solution.py:21
  308.4 11.9 %collective-permute-start.17 = (bf16[1,65,128]{2,0,1:T(2,128)(2,1)S(1)}, bf16[1,65,128]{2,0,1:T(2,128)(2,1)}, u32[]{:S(2)}, u32[]{:S(2)}) collective-permute-start(bf16[1,65,128]{2,0,1:T(2,128)(2,1)S(1)} %get-tuple-element.1090), channel_id=1, source_target_pairs={{0,80},{8,88},{16,96},{24,104},{32,112},{40,120},{48,0},{56,8},{64... | collective-permute-start | bytes 49928 | tf_op jit(solution)/shard_map/ppermute | solution.py:21
  310.0 19.8 %collective-permute-start.18 = (bf16[1,65,128]{2,0,1:T(2,128)(2,1)}, bf16[1,65,128]{2,0,1:T(2,128)(2,1)}, u32[]{:S(2)}, u32[]{:S(2)}) collective-permute-start(bf16[1,65,128]{2,0,1:T(2,128)(2,1)} %get-tuple-element.1091), channel_id=1, source_target_pairs={{0,88},{8,96},{16,104},{24,112},{32,120},{40,0},{48,8},{56,16},{64... | collective-permute-start | bytes 49928 | tf_op jit(solution)/shard_map/ppermute | solution.py:21
  317.2 12.6 %collective-permute-start.19 = (bf16[1,65,128]{2,0,1:T(2,128)(2,1)}, bf16[1,65,128]{2,0,1:T(2,128)(2,1)}, u32[]{:S(2)}, u32[]{:S(2)}) collective-permute-start(bf16[1,65,128]{2,0,1:T(2,128)(2,1)} %get-tuple-element.1092), channel_id=1, source_target_pairs={{0,96},{8,104},{16,112},{24,120},{32,0},{40,8},{48,16},{56,24},{64... | collective-permute-start | bytes 49928 | tf_op jit(solution)/shard_map/ppermute | solution.py:21
  320.3 9.6 %collective-permute-start.20 = (bf16[1,65,128]{2,0,1:T(2,128)(2,1)}, bf16[1,65,128]{2,0,1:T(2,128)(2,1)}, u32[]{:S(2)}, u32[]{:S(2)}) collective-permute-start(bf16[1,65,128]{2,0,1:T(2,128)(2,1)} %get-tuple-element.1089), channel_id=1, source_target_pairs={{0,104},{8,112},{16,120},{24,0},{32,8},{40,16},{48,24},{56,32},{64... | collective-permute-start | bytes 49928 | tf_op jit(solution)/shard_map/ppermute | solution.py:21
  329.8 44.2 %collective-permute-start.3 = (bf16[2048,256]{1,0:T(8,128)(2,1)}, bf16[2048,256]{1,0:T(8,128)(2,1)S(1)}, u32[]{:S(2)}, u32[]{:S(2)}) collective-permute-start(bf16[2048,256]{1,0:T(8,128)(2,1)} %bitcast.105), channel_id=1, source_target_pairs={{0,3},{1,4},{2,5},{3,6},{4,7},{5,0},{6,1},{7,2},{8,11},{9,12},{10,... | collective-permute-start | bytes 3145736 | tf_op jit(solution)/shard_map/ppermute | solution.py:21
  329.8 47.1 %collective-permute-start.4 = (bf16[2048,256]{1,0:T(8,128)(2,1)}, bf16[2048,256]{1,0:T(8,128)(2,1)}, u32[]{:S(2)}, u32[]{:S(2)}) collective-permute-start(bf16[2048,256]{1,0:T(8,128)(2,1)} %bitcast.104), channel_id=1, source_target_pairs={{0,4},{1,5},{2,6},{3,7},{4,0},{5,1},{6,2},{7,3},{8,12},{9,13},{10,... | collective-permute-start | bytes 3145736 | tf_op jit(solution)/shard_map/ppermute | solution.py:21
  329.9 47.7 %collective-permute-start.5 = (bf16[2048,256]{1,0:T(8,128)(2,1)}, bf16[2048,256]{1,0:T(8,128)(2,1)}, u32[]{:S(2)}, u32[]{:S(2)}) collective-permute-start(bf16[2048,256]{1,0:T(8,128)(2,1)} %bitcast.103), channel_id=1, source_target_pairs={{0,5},{1,6},{2,7},{3,0},{4,1},{5,2},{6,3},{7,4},{8,13},{9,14},{10,... | collective-permute-start | bytes 3145736 | tf_op jit(solution)/shard_map/ppermute | solution.py:21
  332.2 45.9 %collective-permute-start.6 = (bf16[2048,256]{1,0:T(8,128)(2,1)}, bf16[2048,256]{1,0:T(8,128)(2,1)}, u32[]{:S(2)}, u32[]{:S(2)}) collective-permute-start(bf16[2048,256]{1,0:T(8,128)(2,1)} %bitcast.102), channel_id=1, source_target_pairs={{0,6},{1,7},{2,0},{3,1},{4,2},{5,3},{6,4},{7,5},{8,14},{9,15},{10,... | collective-permute-start | bytes 3145736 | tf_op jit(solution)/shard_map/ppermute | solution.py:21
  332.3 64.5 %collective-permute-start.7 = (bf16[2048,256]{1,0:T(8,128)(2,1)}, bf16[2048,256]{1,0:T(8,128)(2,1)}, u32[]{:S(2)}, u32[]{:S(2)}) collective-permute-start(bf16[2048,256]{1,0:T(8,128)(2,1)} %bitcast.101), channel_id=1, source_target_pairs={{0,7},{1,0},{2,1},{3,2},{4,3},{5,4},{6,5},{7,6},{8,15},{9,8},{10,9... | collective-permute-start | bytes 3145736 | tf_op jit(solution)/shard_map/ppermute | solution.py:21
  (13 other events, 245.6 us)
Sparse Core Ops, SparseCore 0:
  11.1 49.7 all-gather.2
  63.3 46.3 all-gather.4

commit v3 on v1

--- a/solution.py
+++ b/solution.py
@@ -3,11 +3,12 @@
 import jax
 import jax.numpy as jnp
 from jax import lax
-from jax.sharding import PartitionSpec as P
+from jax.sharding import Mesh, PartitionSpec as P
 
 W = 2048
 PAGE = 128
 SEGS = 32
+MP = ("ylo", "x")
 
 
 def from_behind(x, axis, by):
@@ -85,9 +86,9 @@
 
 def body(tokens_in, norm_gain, q_weight, kv_weight, out_weight, segment_ids, page_table):
     seq_count = lax.axis_size("seq")
-    mp_count = lax.axis_size("mp")
+    mp_count = lax.axis_size(MP)
     seq_index = lax.axis_index("seq")
-    mp_index = lax.axis_index("mp")
+    mp_index = lax.axis_index(MP)
     tok_rows = tokens_in.shape[0]
     kv_heads = kv_weight.shape[0]
     head_size = kv_weight.shape[2] // 2
@@ -145,12 +146,14 @@
         .reshape(tok_rows, local_heads * head_size)
         .astype(jnp.bfloat16)
     )
-    partial_term = lax.dot_general(
-        attended, w_output, (((1,), (1,)), ((), ())), preferred_element_type=jnp.float32
-    )
-    layer_out = lax.psum_scatter(
-        partial_term.astype(jnp.bfloat16), "mp", scatter_dimension=1, tiled=True
-    )
+    rows_mp, cols_mp = (lax.axis_size(MP[0]), lax.axis_size(MP[1]))
+    out_blocks = w_output.reshape(rows_mp, cols_mp, -1, w_output.shape[1])
+    grouped = jnp.einsum(
+        "tk,yxck->yxtc", attended, out_blocks, preferred_element_type=jnp.float32
+    ).astype(jnp.bfloat16)
+    grouped = lax.psum_scatter(grouped, MP[0], scatter_dimension=0, tiled=True)
+    grouped = lax.psum_scatter(grouped, MP[1], scatter_dimension=1, tiled=True)
+    layer_out = grouped.reshape(tok_rows, -1)
     pages_dev = tok_rows // PAGE
     share_width = 2 * head_size // ratio
     share_index = mp_index % ratio
@@ -187,19 +190,21 @@
 
 
 def solution(mesh):
+    seq_size, mp_size = (mesh.shape["seq"], mesh.shape["mp"])
+    split = Mesh(mesh.devices.reshape(seq_size, 2, mp_size // 2), ("seq",) + MP)
     placed = (
         P("seq", None),
         P(),
-        P("seq", "mp"),
+        P("seq", MP),
         P(None, "seq", None),
-        P("seq", "mp"),
+        P("seq", MP),
         P("seq"),
         P("seq"),
     )
     return jax.shard_map(
         body,
-        mesh=mesh,
+        mesh=split,
         in_specs=placed,
-        out_specs=(P("seq", "mp"), P("seq", "mp", None)),
+        out_specs=(P("seq", MP), P("seq", MP, None)),
         check_vma=False,
     )

time: 357 us -> 400 us (1.12)
  waiting for transfers between devices: 33 us -> 198 us
  starting transfers between devices: 150 us -> 32.4 us
    reduce_scatter x1 -> x2, waiting for transfers between devices: 0.01 us -> 165 us  [the longest x1 151 us: body(): grouped = lax.psum_scatter(grouped, MP[0], scatter_dimension=0, tiled=True)]
    ppermute x15, starting transfers between devices: 147 us -> 29 us  [shift_round(): return lax.ppermute(x, axis, [(i, (i + by) % peers) for i in range(peers)])]
  transfers between devices with their start and end apart: 19 -> 20, of which waited for: 3 -> 5; matrix products, arithmetic and copies ran while one was open for 33% -> 29% of each run, Pallas kernels for 0% -> 0%
where the time goes in v3:
time: 400 us; the launch traced here: 399 us
  waiting for transfers between devices  198 us (50%)
  matrix products  59 us (15%)
  other arithmetic  52 us (13%)
  starting transfers between devices  32.4 us (8%)
  loops' own time  15.6 us (4%)
  local copies, waits for them, and re-layouts  14.9 us (4%)
  between operations  14.1 us (4%)
  blocking collectives  13.7 us (3%)
    reduce_scatter x1, waiting for transfers between devices, body(): grouped = lax.psum_scatter(grouped, MP[0], scatter_dimension=0, tiled=True)  151 us
    all_gather x1, waiting for transfers between devices, body(): lax.all_gather(jnp.concatenate([q_weight, kv_own], axis=1), 'seq', axis=0...  29.6 us
    ppermute x15, starting transfers between devices, shift_round(): return lax.ppermute(x, axis, [(i, (i + by) % peers) for i in range(peers)])  29 us
    reduce_sum x5, other arithmetic, compute(): new_total = total_block * factor + jnp.sum(weights, axis=-1)  24.4 us
    dot_general x5, matrix products, compute(): jnp.einsum('hqk,kd->hqd', weights.astype(jnp.bfloat16), value_rows, prefe...  23.2 us
    dot_general x5, matrix products, compute(): jnp.einsum('qhd,kd->hqk', query_block, key_rows, preferred_element_type=j...  21.9 us
    another operation x2, loops' own time, attend_piece(): return lax.fori_loop(0, blocks, one_block, carry)  15.2 us
    and x5, other arithmetic, compute(): keep = keep & (query_index[:, None] - key_index[None, :] < W)  14.5 us
  transfers between devices with their start and end apart: 20, of which 5 were waited for; matrix products, arithmetic and copies ran while one was open for 29% of the time, Pallas kernels for 0%

profile of v3, /device:TPU:1, one launch (start us, length us, event | category | flops | bytes accessed | tf_op | source)
XLA Modules:
  0.0 399.3 jit_solution(8088610650476132452)
XLA Ops:
  11.2 13.7 %psum.7 = s32[32]{0:T(128)S(1)} all-reduce(s32[32]{0:T(128)S(1)} %convert_reduce_fusion), channel_id=1, replica_groups=mesh['seq'=16,'ylo'=2,'x'=4] {'seq'}, use_global_device_ids=true, to_apply=%region_2.3 | all-reduce | flops 32 | bytes 256 | tf_op jit(solution)/shard_map/psum | solution.py:110
  26.0 5.1 %fusion.50 = f32[2048]{0:T(1024)S(1)} fusion(bf16[2048,2048]{1,0:T(8,128)(2,1)} %param.15), kind=kLoop, calls=%fused_computation.60 | loop fusion | flops 12580864 | bytes 8396800 | tf_op jit(solution)/shard_map/reduce_sum | solution.py:104
  31.2 29.6 %all-gather.3.cloned.1.call-done = bf16[2048,384]{1,0:T(8,128)(2,1)} async-done(((bf16[128,384]{1,0:T(8,128)(2,1)}), bf16[2048,384]{1,0:T(8,128)(2,1)}) %all-gather.3.cloned.1.call-update) | async-done | bytes 1572880 | tf_op jit(solution)/shard_map/all_gather | solution.py:99
  60.8 6.6 %fusion.53 = f32[2048,384]{0,1:T(8,128)S(1)} fusion(bf16[2048,384]{1,0:T(8,128)(2,1)} %all-gather.3.cloned.1.call-done, bf16[2048,2048]{1,0:T(8,128)(2,1)} %param.15, f32[2048]{0:T(1024)S(1)} %copy-done.4, f32[2048]{0:T(1024)S(1)} %add_rsqrt_fusion), kind=kOutput, calls=%fused_computation.63 | convolution fusion | flops 3238002688 | bytes 13123584 | tf_op jit(solution)/shard_map/dot_general | solution.py:122
  74.5 80.3 %while.46 = (s32[]{:T(128)}, f32[4,2048]{1,0:T(4,128)S(1)}, f32[4,2048]{1,0:T(4,128)S(1)}, f32[4,2048,64]{1,2,0:T(8,128)S(1)}, s32[]{:T(128)}, /*index=5*/s32[20...) while((s32[]{:T(128)}, f32[4,2048]{1,0:T(4,128)S(1)}, ...), condition=%wide.region_10.11_spmd.clone.clone, body=%wide.region_5.10_spmd.clone.clone.sunk | while | flops 1134828032 | bytes 57707496 | solution.py:84
  77.5 17.0 %conditional.8 = ((f32[4,2048]{1,0:T(4,128)S(1)}, f32[4,2048]{1,0:T(4,128)S(1)}, f32[4,2048,64]{1,2,0:T(8,128)S(1)})) conditional(s32[]{:T(128)} %convert_element_type.149, (f32[4,2048]{1,0:T(4,128)S(1)}, f32[4,2048]{1,0:T(4,128)S(1)}, f32[4,2048,64]{1,2,0:T(8,128)S(1)}) %tuple.167, (s32[]{:T(128)}, f32[4,2048]{1,0:T(4,128)S(1)}, s32[]{:T(128)}, ...), branch_computations={%region_6.6_spmd, %region_7.9_spmd} | conditional | flops 1134827520 | bytes 57692752 | solution.py:82
  84.9 4.9 %fusion.7 = f32[4,512]{1,0:T(4,128)S(1)} fusion(f32[512,4,2048]{2,0,1:T(8,128)S(1)} %get-tuple-element.1056, f32[4,512]{1,0:T(4,128)S(1)} %get-tuple-element.1050, pred[512,2048]{1,0:T(8,128)(4,1)S(1)} %fusion.12), kind=kLoop, calls=%fused_computation.8 | loop fusion | flops 20969472 | bytes 17842176 | tf_op jit(solution)/shard_map/while/body/eval_jaxpr/cond/branch_1_fun/reduce_sum | solution.py:69
  89.9 4.6 %fusion.16 = f32[4,2048,64]{1,2,0:T(8,128)S(1)} fusion(f32[4,2048,64]{1,2,0:T(8,128)S(1)} %get-tuple-element.823, s32[]{:T(128)S(6)} %select_n.91, f32[512,4,2048]{2,0,1:T(8,128)S(1)} %get-tuple-element.1056, f32[4,512]{1,0:T(4,128)S(1)} %get-tuple-element.1050, pred[512,2048]{1,0:T(8,128)(4,1)S(1)} %fusion.12, ...), kind=kOutput, calls=%fused_computation.15 | convolution fusion | flops 558104576 | bytes 20201476 | tf_op jit(solution)/shard_map/while/body/eval_jaxpr/cond/branch_1_fun/hqk,kd->hqd/dot_general | solution.py:70
  97.6 17.0 %conditional.8 = ((f32[4,2048]{1,0:T(4,128)S(1)}, f32[4,2048]{1,0:T(4,128)S(1)}, f32[4,2048,64]{1,2,0:T(8,128)S(1)})) conditional(s32[]{:T(128)} %convert_element_type.149, (f32[4,2048]{1,0:T(4,128)S(1)}, f32[4,2048]{1,0:T(4,128)S(1)}, f32[4,2048,64]{1,2,0:T(8,128)S(1)}) %tuple.167, (s32[]{:T(128)}, f32[4,2048]{1,0:T(4,128)S(1)}, s32[]{:T(128)}, ...), branch_computations={%region_6.6_spmd, %region_7.9_spmd} | conditional | flops 1134827520 | bytes 57692752 | solution.py:82
  105.0 4.9 %fusion.7 = f32[4,512]{1,0:T(4,128)S(1)} fusion(f32[512,4,2048]{2,0,1:T(8,128)S(1)} %get-tuple-element.1056, f32[4,512]{1,0:T(4,128)S(1)} %get-tuple-element.1050, pred[512,2048]{1,0:T(8,128)(4,1)S(1)} %fusion.12), kind=kLoop, calls=%fused_computation.8 | loop fusion | flops 20969472 | bytes 17842176 | tf_op jit(solution)/shard_map/while/body/eval_jaxpr/cond/branch_1_fun/reduce_sum | solution.py:69
  109.9 4.6 %fusion.16 = f32[4,2048,64]{1,2,0:T(8,128)S(1)} fusion(f32[4,2048,64]{1,2,0:T(8,128)S(1)} %get-tuple-element.823, s32[]{:T(128)S(6)} %select_n.91, f32[512,4,2048]{2,0,1:T(8,128)S(1)} %get-tuple-element.1056, f32[4,512]{1,0:T(4,128)S(1)} %get-tuple-element.1050, pred[512,2048]{1,0:T(8,128)(4,1)S(1)} %fusion.12, ...), kind=kOutput, calls=%fused_computation.15 | convolution fusion | flops 558104576 | bytes 20201476 | tf_op jit(solution)/shard_map/while/body/eval_jaxpr/cond/branch_1_fun/hqk,kd->hqd/dot_general | solution.py:70
  117.7 17.0 %conditional.8 = ((f32[4,2048]{1,0:T(4,128)S(1)}, f32[4,2048]{1,0:T(4,128)S(1)}, f32[4,2048,64]{1,2,0:T(8,128)S(1)})) conditional(s32[]{:T(128)} %convert_element_type.149, (f32[4,2048]{1,0:T(4,128)S(1)}, f32[4,2048]{1,0:T(4,128)S(1)}, f32[4,2048,64]{1,2,0:T(8,128)S(1)}) %tuple.167, (s32[]{:T(128)}, f32[4,2048]{1,0:T(4,128)S(1)}, s32[]{:T(128)}, ...), branch_computations={%region_6.6_spmd, %region_7.9_spmd} | conditional | flops 1134827520 | bytes 57692752 | solution.py:82
  125.1 4.9 %fusion.7 = f32[4,512]{1,0:T(4,128)S(1)} fusion(f32[512,4,2048]{2,0,1:T(8,128)S(1)} %get-tuple-element.1056, f32[4,512]{1,0:T(4,128)S(1)} %get-tuple-element.1050, pred[512,2048]{1,0:T(8,128)(4,1)S(1)} %fusion.12), kind=kLoop, calls=%fused_computation.8 | loop fusion | flops 20969472 | bytes 17842176 | tf_op jit(solution)/shard_map/while/body/eval_jaxpr/cond/branch_1_fun/reduce_sum | solution.py:69
  130.0 4.6 %fusion.16 = f32[4,2048,64]{1,2,0:T(8,128)S(1)} fusion(f32[4,2048,64]{1,2,0:T(8,128)S(1)} %get-tuple-element.823, s32[]{:T(128)S(6)} %select_n.91, f32[512,4,2048]{2,0,1:T(8,128)S(1)} %get-tuple-element.1056, f32[4,512]{1,0:T(4,128)S(1)} %get-tuple-element.1050, pred[512,2048]{1,0:T(8,128)(4,1)S(1)} %fusion.12, ...), kind=kOutput, calls=%fused_computation.15 | convolution fusion | flops 558104576 | bytes 20201476 | tf_op jit(solution)/shard_map/while/body/eval_jaxpr/cond/branch_1_fun/hqk,kd->hqd/dot_general | solution.py:70
  137.7 17.0 %conditional.8 = ((f32[4,2048]{1,0:T(4,128)S(1)}, f32[4,2048]{1,0:T(4,128)S(1)}, f32[4,2048,64]{1,2,0:T(8,128)S(1)})) conditional(s32[]{:T(128)} %convert_element_type.149, (f32[4,2048]{1,0:T(4,128)S(1)}, f32[4,2048]{1,0:T(4,128)S(1)}, f32[4,2048,64]{1,2,0:T(8,128)S(1)}) %tuple.167, (s32[]{:T(128)}, f32[4,2048]{1,0:T(4,128)S(1)}, s32[]{:T(128)}, ...), branch_computations={%region_6.6_spmd, %region_7.9_spmd} | conditional | flops 1134827520 | bytes 57692752 | solution.py:82
  145.1 4.9 %fusion.7 = f32[4,512]{1,0:T(4,128)S(1)} fusion(f32[512,4,2048]{2,0,1:T(8,128)S(1)} %get-tuple-element.1056, f32[4,512]{1,0:T(4,128)S(1)} %get-tuple-element.1050, pred[512,2048]{1,0:T(8,128)(4,1)S(1)} %fusion.12), kind=kLoop, calls=%fused_computation.8 | loop fusion | flops 20969472 | bytes 17842176 | tf_op jit(solution)/shard_map/while/body/eval_jaxpr/cond/branch_1_fun/reduce_sum | solution.py:69
  150.1 4.6 %fusion.16 = f32[4,2048,64]{1,2,0:T(8,128)S(1)} fusion(f32[4,2048,64]{1,2,0:T(8,128)S(1)} %get-tuple-element.823, s32[]{:T(128)S(6)} %select_n.91, f32[512,4,2048]{2,0,1:T(8,128)S(1)} %get-tuple-element.1056, f32[4,512]{1,0:T(4,128)S(1)} %get-tuple-element.1050, pred[512,2048]{1,0:T(8,128)(4,1)S(1)} %fusion.12, ...), kind=kOutput, calls=%fused_computation.15 | convolution fusion | flops 558104576 | bytes 20201476 | tf_op jit(solution)/shard_map/while/body/eval_jaxpr/cond/branch_1_fun/hqk,kd->hqd/dot_general | solution.py:70
  154.8 29.5 %while.47 = (s32[]{:T(128)}, f32[4,2048]{1,0:T(4,128)S(1)}, f32[4,2048]{1,0:T(4,128)S(1)}, f32[4,2048,64]{1,2,0:T(8,128)S(1)}, s32[]{:T(128)}, /*index=5*/s32[]{...) while((s32[]{:T(128)}, f32[4,2048]{1,0:T(4,128)S(1)}, ...), condition=%wide.region_16.17_spmd.clone.clone, body=%wide.region_11.16_spmd.clone.clone.sunk | while | flops 1134828032 | bytes 57707504 | solution.py:84
  158.1 16.8 %conditional.9 = ((f32[4,2048]{1,0:T(4,128)S(1)}, f32[4,2048]{1,0:T(4,128)S(1)}, f32[4,2048,64]{1,2,0:T(8,128)S(1)})) conditional(s32[]{:T(128)} %convert_element_type.150, (f32[4,2048]{1,0:T(4,128)S(1)}, f32[4,2048]{1,0:T(4,128)S(1)}, f32[4,2048,64]{1,2,0:T(8,128)S(1)}) %tuple.171, (s32[]{:T(128)}, f32[4,2048]{1,0:T(4,128)S(1)}, s32[]{:T(128)}, ...), branch_computations={%region_12.12_spmd, %region_13.15_spmd} | conditional | flops 1134827520 | bytes 57692752 | solution.py:82
  165.4 4.9 %fusion.30 = f32[4,512]{1,0:T(4,128)S(1)} fusion(f32[512,4,2048]{2,0,1:T(8,128)S(1)} %get-tuple-element.1060, f32[4,512]{1,0:T(4,128)S(1)} %get-tuple-element.1054, pred[512,2048]{1,0:T(8,128)(4,1)S(1)} %fusion.35), kind=kLoop, calls=%fused_computation.35 | loop fusion | flops 20969472 | bytes 17842176 | tf_op jit(solution)/shard_map/while/body/eval_jaxpr/cond/branch_1_fun/reduce_sum | solution.py:69
  170.3 4.6 %fusion.39 = f32[4,2048,64]{1,2,0:T(8,128)S(1)} fusion(f32[4,2048,64]{1,2,0:T(8,128)S(1)} %get-tuple-element.849, s32[]{:T(128)S(6)} %select_n.96, f32[512,4,2048]{2,0,1:T(8,128)S(1)} %get-tuple-element.1060, f32[4,512]{1,0:T(4,128)S(1)} %get-tuple-element.1054, pred[512,2048]{1,0:T(8,128)(4,1)S(1)} %fusion.35, ...), kind=kOutput, calls=%fused_computation.42 | convolution fusion | flops 558104576 | bytes 20201476 | tf_op jit(solution)/shard_map/while/body/eval_jaxpr/cond/branch_1_fun/hqk,kd->hqd/dot_general | solution.py:70
  184.5 6.8 %convert_bitcast_fusion = bf16[2,4,2048,256]{3,2,1,0:T(8,128)(2,1)} fusion(bf16[2048,256,1,1]{0,1,3,2:T(8,128)(2,1)S(1)} %bitcast.91, bf16[2,4,256,256]{3,2,1,0:T(8,128)(2,1)} %bitcast.92), kind=kOutput, calls=%fused_computation.64 | convolution fusion | flops 2151677952 | bytes 10485760 | tf_op jit(solution)/shard_map/tk,yxck->yxtc/dot_general | solution.py:151
  191.5 150.6 %reduce-scatter.3.cloned.1.call-done = bf16[1,4,2048,256]{3,2,1,0:T(8,128)(2,1)} async-done(((bf16[2,4,2048,256]{3,2,1,0:T(8,128)(2,1)}), bf16[1,4,2048,256]{3,2,1,0:T(8,128)(2,1)}) %reduce-scatter.3.cloned.1.call-update) | async-done | bytes 4194320 | tf_op jit(solution)/shard_map/reduce_scatter | solution.py:154
  378.6 14.2 %reduce-scatter.5.cloned.1.call-done = bf16[1,1,2048,256]{3,2,1,0:T(8,128)(2,1)} async-done(((bf16[1,4,2048,256]{3,2,1,0:T(8,128)(2,1)}), bf16[1,1,2048,256]{3,2,1,0:T(8,128)(2,1)}) %reduce-scatter.5.cloned.1.call-update) | async-done | bytes 1048592 | tf_op jit(solution)/shard_map/reduce_scatter | solution.py:155
  (171 shorter events, 95.4 us)
Async XLA Ops:
  7.2 53.6 %copy-start.4 = (f32[2048]{0:T(1024)S(1)}, f32[2048]{0:T(1024)}, u32[]{:S(2)}) copy-start(f32[2048]{0:T(1024)} %param.16) | copy-start | bytes 24580
  7.2 53.6 %all-gather.3.cloned.1.call-start = ((), (), s32[]{:S(2)}) async-start(), calls=%async_computation.2 | async-start | bytes 1671168 | tf_op jit(solution)/shard_map/all_gather | solution.py:99
  9.6 174.9 %all-gather.5.cloned.1.call-start = ((), (), s32[]{:S(2)}) async-start(), calls=%async_computation.3 | async-start | bytes 1114112 | tf_op jit(solution)/shard_map/all_gather | solution.py:102
  10.3 331.7 %reduce-scatter.3.cloned.1.call-start = ((), (), s32[]{:S(2)}) async-start(), calls=%async_computation.4 | async-start | bytes 12582912 | tf_op jit(solution)/shard_map/reduce_scatter | solution.py:154
  69.6 85.1 %collective-permute-start = (bf16[2048,128]{0,1:T(8,128)(2,1)S(1)}, bf16[2048,128]{0,1:T(8,128)(2,1)S(1)}, u32[]{:S(2)}, u32[]{:S(2)}) collective-permute-start(bf16[2048,128]{0,1:T(8,128)(2,1)S(1)} %pad_maximum_fusion.1), channel_id=1, source_target_pairs={{0,8},{8,16},{16,24},{24,32},{32,40},{40,48},{48,56},{56,64},{64,7... | collective-permute-start | bytes 1572872 | tf_op jit(solution)/shard_map/ppermute | solution.py:17
  191.4 150.7 %copy-start.5 = (s32[16]{0:T(128)S(1)}, s32[16]{0:T(128)}, u32[]{:S(2)}) copy-start(s32[16]{0:T(128)} %param.21) | copy-start | bytes 196
  191.4 151.1 %copy-start.3 = (bf16[2048,128]{0,1:T(8,128)(2,1)S(1)}, bf16[2048,128]{0,1:T(8,128)(2,1)}, u32[]{:S(2)}) copy-start(bf16[2048,128]{0,1:T(8,128)(2,1)} %copy-done.2) | copy-start | bytes 1572868
  191.4 201.4 %copy-start.1 = (bf16[4,128,128]{2,1,0:T(8,128)(2,1)S(1)}, bf16[4,128,128]{2,1,0:T(8,128)(2,1)}, u32[]{:S(2)}) copy-start(bf16[4,128,128]{2,1,0:T(8,128)(2,1)} %param.18) | copy-start | bytes 393220
  191.4 201.4 %reduce-scatter.5.cloned.1.call-start = ((), (), s32[]{:S(2)}) async-start(), calls=%async_computation.5 | async-start | bytes 5242880 | tf_op jit(solution)/shard_map/reduce_scatter | solution.py:155
  343.0 10.1 %collective-permute-start.1 = (bf16[1,65,128]{2,0,1:T(2,128)(2,1)S(1)}, bf16[1,65,128]{2,0,1:T(2,128)(2,1)S(1)}, u32[]{:S(2)}, u32[]{:S(2)}) collective-permute-start(bf16[1,65,128]{2,0,1:T(2,128)(2,1)S(1)} %get-tuple-element.1071), channel_id=1, source_target_pairs={{0,8},{8,16},{16,24},{24,32},{32,40},{40,48},{48,56},{56,64},{64,7... | collective-permute-start | bytes 49928 | tf_op jit(solution)/shard_map/ppermute | solution.py:22
  345.1 9.2 %collective-permute-start.2 = (bf16[1,65,128]{2,0,1:T(2,128)(2,1)S(1)}, bf16[1,65,128]{2,0,1:T(2,128)(2,1)S(1)}, u32[]{:S(2)}, u32[]{:S(2)}) collective-permute-start(bf16[1,65,128]{2,0,1:T(2,128)(2,1)S(1)} %get-tuple-element.1072), channel_id=1, source_target_pairs={{0,16},{8,24},{16,32},{24,40},{32,48},{40,56},{48,64},{56,72},{64,... | collective-permute-start | bytes 49928 | tf_op jit(solution)/shard_map/ppermute | solution.py:22
  346.3 11.8 %collective-permute-start.3 = (bf16[1,65,128]{2,0,1:T(2,128)(2,1)S(1)}, bf16[1,65,128]{2,0,1:T(2,128)(2,1)S(1)}, u32[]{:S(2)}, u32[]{:S(2)}) collective-permute-start(bf16[1,65,128]{2,0,1:T(2,128)(2,1)S(1)} %get-tuple-element.1073), channel_id=1, source_target_pairs={{0,24},{8,32},{16,40},{24,48},{32,56},{40,64},{48,72},{56,80},{64,... | collective-permute-start | bytes 49928 | tf_op jit(solution)/shard_map/ppermute | solution.py:22
  348.0 10.7 %collective-permute-start.4 = (bf16[1,65,128]{2,0,1:T(2,128)(2,1)S(1)}, bf16[1,65,128]{2,0,1:T(2,128)(2,1)S(1)}, u32[]{:S(2)}, u32[]{:S(2)}) collective-permute-start(bf16[1,65,128]{2,0,1:T(2,128)(2,1)S(1)} %get-tuple-element.1074), channel_id=1, source_target_pairs={{0,32},{8,40},{16,48},{24,56},{32,64},{40,72},{48,80},{56,88},{64,... | collective-permute-start | bytes 49928 | tf_op jit(solution)/shard_map/ppermute | solution.py:22
  350.7 10.4 %collective-permute-start.5 = (bf16[1,65,128]{2,0,1:T(2,128)(2,1)S(1)}, bf16[1,65,128]{2,0,1:T(2,128)(2,1)S(1)}, u32[]{:S(2)}, u32[]{:S(2)}) collective-permute-start(bf16[1,65,128]{2,0,1:T(2,128)(2,1)S(1)} %get-tuple-element.1076), channel_id=1, source_target_pairs={{0,40},{8,48},{16,56},{24,64},{32,72},{40,80},{48,88},{56,96},{64,... | collective-permute-start | bytes 49928 | tf_op jit(solution)/shard_map/ppermute | solution.py:22
  353.1 11.1 %collective-permute-start.6 = (bf16[1,65,128]{2,0,1:T(2,128)(2,1)S(1)}, bf16[1,65,128]{2,0,1:T(2,128)(2,1)S(1)}, u32[]{:S(2)}, u32[]{:S(2)}) collective-permute-start(bf16[1,65,128]{2,0,1:T(2,128)(2,1)S(1)} %get-tuple-element.1077), channel_id=1, source_target_pairs={{0,48},{8,56},{16,64},{24,72},{32,80},{40,88},{48,96},{56,104},{64... | collective-permute-start | bytes 49928 | tf_op jit(solution)/shard_map/ppermute | solution.py:22
  354.2 11.3 %collective-permute-start.7 = (bf16[1,65,128]{2,0,1:T(2,128)(2,1)S(1)}, bf16[1,65,128]{2,0,1:T(2,128)(2,1)S(1)}, u32[]{:S(2)}, u32[]{:S(2)}) collective-permute-start(bf16[1,65,128]{2,0,1:T(2,128)(2,1)S(1)} %get-tuple-element.1078), channel_id=1, source_target_pairs={{0,56},{8,64},{16,72},{24,80},{32,88},{40,96},{48,104},{56,112},{6... | collective-permute-start | bytes 49928 | tf_op jit(solution)/shard_map/ppermute | solution.py:22
  358.2 9.3 %collective-permute-start.8 = (bf16[1,65,128]{2,0,1:T(2,128)(2,1)S(1)}, bf16[1,65,128]{2,0,1:T(2,128)(2,1)S(1)}, u32[]{:S(2)}, u32[]{:S(2)}) collective-permute-start(bf16[1,65,128]{2,0,1:T(2,128)(2,1)S(1)} %get-tuple-element.1079), channel_id=1, source_target_pairs={{0,64},{8,72},{16,80},{24,88},{32,96},{40,104},{48,112},{56,120},{... | collective-permute-start | bytes 49928 | tf_op jit(solution)/shard_map/ppermute | solution.py:22
  358.7 10.9 %collective-permute-start.9 = (bf16[1,65,128]{2,0,1:T(2,128)(2,1)S(1)}, bf16[1,65,128]{2,0,1:T(2,128)(2,1)S(1)}, u32[]{:S(2)}, u32[]{:S(2)}) collective-permute-start(bf16[1,65,128]{2,0,1:T(2,128)(2,1)S(1)} %get-tuple-element.1080), channel_id=1, source_target_pairs={{0,72},{8,80},{16,88},{24,96},{32,104},{40,112},{48,120},{56,0},{6... | collective-permute-start | bytes 49928 | tf_op jit(solution)/shard_map/ppermute | solution.py:22
  361.1 9.9 %collective-permute-start.10 = (bf16[1,65,128]{2,0,1:T(2,128)(2,1)S(1)}, bf16[1,65,128]{2,0,1:T(2,128)(2,1)S(1)}, u32[]{:S(2)}, u32[]{:S(2)}) collective-permute-start(bf16[1,65,128]{2,0,1:T(2,128)(2,1)S(1)} %get-tuple-element.1082), channel_id=1, source_target_pairs={{0,80},{8,88},{16,96},{24,104},{32,112},{40,120},{48,0},{56,8},{64... | collective-permute-start | bytes 49928 | tf_op jit(solution)/shard_map/ppermute | solution.py:22
  364.1 8.2 %collective-permute-start.11 = (bf16[1,65,128]{2,0,1:T(2,128)(2,1)S(1)}, bf16[1,65,128]{2,0,1:T(2,128)(2,1)S(1)}, u32[]{:S(2)}, u32[]{:S(2)}) collective-permute-start(bf16[1,65,128]{2,0,1:T(2,128)(2,1)S(1)} %get-tuple-element.1083), channel_id=1, source_target_pairs={{0,88},{8,96},{16,104},{24,112},{32,120},{40,0},{48,8},{56,16},{64... | collective-permute-start | bytes 49928 | tf_op jit(solution)/shard_map/ppermute | solution.py:22
  365.5 6.9 %collective-permute-start.12 = (bf16[1,65,128]{2,0,1:T(2,128)(2,1)S(1)}, bf16[1,65,128]{2,0,1:T(2,128)(2,1)S(1)}, u32[]{:S(2)}, u32[]{:S(2)}) collective-permute-start(bf16[1,65,128]{2,0,1:T(2,128)(2,1)S(1)} %get-tuple-element.1084), channel_id=1, source_target_pairs={{0,96},{8,104},{16,112},{24,120},{32,0},{40,8},{48,16},{56,24},{64... | collective-permute-start | bytes 49928 | tf_op jit(solution)/shard_map/ppermute | solution.py:22
  367.5 4.9 %collective-permute-start.13 = (bf16[1,65,128]{2,0,1:T(2,128)(2,1)S(1)}, bf16[1,65,128]{2,0,1:T(2,128)(2,1)S(1)}, u32[]{:S(2)}, u32[]{:S(2)}) collective-permute-start(bf16[1,65,128]{2,0,1:T(2,128)(2,1)S(1)} %get-tuple-element.1081), channel_id=1, source_target_pairs={{0,104},{8,112},{16,120},{24,0},{32,8},{40,16},{48,24},{56,32},{64... | collective-permute-start | bytes 49928 | tf_op jit(solution)/shard_map/ppermute | solution.py:22
  369.6 3.5 collective-permute-start.14
  371.0 3.7 collective-permute-start.15
  (2 other events, 5.8 us)
Sparse Core Ops, SparseCore 0:
  11.1 49.6 all-gather.2
  63.2 46.3 all-gather.4
  191.5 150.4 reduce-scatter.2
  344.9 47.8 reduce-scatter.4

commit v4 on v1

--- a/solution.py
+++ b/solution.py
@@ -1,8 +1,11 @@
+import functools
 import math
 
 import jax
 import jax.numpy as jnp
 from jax import lax
+from jax.experimental import pallas as pl
+from jax.experimental.pallas import tpu as pltpu
 from jax.sharding import PartitionSpec as P
 
 W = 2048
@@ -31,56 +34,93 @@
     )
 
 
-def attend_piece(carry, piece, start, queries, query_first, query_start, block_rows):
-    head_size = queries.shape[2]
-    count = piece.shape[0]
-    key_rows = piece[:, :head_size]
-    value_rows = piece[:, head_size:]
-    key_index = start + jnp.arange(count, dtype=jnp.int32)
-    scale = 1.0 / math.sqrt(head_size)
-    blocks = queries.shape[0] // block_rows
-
-    def one_block(block, state):
-        row_first = block * block_rows
-        query_block = lax.dynamic_slice_in_dim(queries, row_first, block_rows, 0)
-        query_index = query_first + row_first + jnp.arange(block_rows, dtype=jnp.int32)
-        query_begin = lax.dynamic_slice_in_dim(query_start, row_first, block_rows, 0)
-        lowest = jnp.maximum(query_begin[0], query_index[0] - W + 1)
-        live = (start <= query_index[-1]) & (start + count - 1 >= lowest)
-
-        def compute(inner):
-            best, totals, accum = inner
-            best_block = lax.dynamic_slice_in_dim(best, row_first, block_rows, 1)
-            total_block = lax.dynamic_slice_in_dim(totals, row_first, block_rows, 1)
-            accum_block = lax.dynamic_slice_in_dim(accum, row_first, block_rows, 1)
-            scores = (
-                jnp.einsum("qhd,kd->hqk", query_block, key_rows, preferred_element_type=jnp.float32)
-                * scale
-            )
-            keep = (key_index[None, :] >= query_begin[:, None]) & (
-                key_index[None, :] <= query_index[:, None]
-            )
-            keep = keep & (query_index[:, None] - key_index[None, :] < W)
-            masked = jnp.where(keep[None], scores, -1e30)
-            new_best = jnp.maximum(best_block, jnp.max(masked, axis=-1))
-            weights = jnp.where(keep[None], jnp.exp(masked - new_best[..., None]), 0.0)
-            factor = jnp.exp(best_block - new_best)
-            new_total = total_block * factor + jnp.sum(weights, axis=-1)
-            mixed = jnp.einsum(
-                "hqk,kd->hqd",
-                weights.astype(jnp.bfloat16),
-                value_rows,
-                preferred_element_type=jnp.float32,
-            )
-            new_accum = accum_block * factor[..., None] + mixed
-            best = lax.dynamic_update_slice_in_dim(best, new_best, row_first, 1)
-            totals = lax.dynamic_update_slice_in_dim(totals, new_total, row_first, 1)
-            accum = lax.dynamic_update_slice_in_dim(accum, new_accum, row_first, 1)
-            return (best, totals, accum)
-
-        return lax.cond(live, compute, lambda inner: inner, state)
-
-    return lax.fori_loop(0, blocks, one_block, carry)
+def flash_kernel(q_rows, tokens, first_ref, lowest_ref, q_ref, k_ref, v_ref, qs_ref, o_ref, m_sc, l_sc, acc_sc):
+    block = pl.program_id(0)
+    step = pl.program_id(1)
+    rows = q_ref.shape[0]
+    k_rows = k_ref.shape[0]
+    head_size = q_ref.shape[1]
+
+    @pl.when(step == 0)
+    def _():
+        m_sc[...] = jnp.full(m_sc.shape, -1e30, jnp.float32)
+        l_sc[...] = jnp.zeros(l_sc.shape, jnp.float32)
+        acc_sc[...] = jnp.zeros(acc_sc.shape, jnp.float32)
+
+    token_first = first_ref[0]
+    query_first = token_first + block * q_rows
+    key_first = token_first - tokens + (block * q_rows // k_rows + step) * k_rows
+    key_last = key_first + k_rows - 1
+    live = (key_last >= lowest_ref[block]) & (key_first <= query_first + q_rows - 1)
+    live = live & (query_first - key_last < W)
+
+    @pl.when(live)
+    def _():
+        scores = lax.dot_general(
+            q_ref[...], k_ref[...], (((1,), (1,)), ((), ())), preferred_element_type=jnp.float32
+        ) * (1.0 / math.sqrt(head_size))
+        key_index = key_first + lax.broadcasted_iota(jnp.int32, (rows, k_rows), 1)
+        query_index = query_first + lax.broadcasted_iota(jnp.int32, (rows, k_rows), 0) % q_rows
+        keep = (key_index >= qs_ref[...]) & (key_index <= query_index)
+        keep = keep & (query_index - key_index < W)
+        masked = jnp.where(keep, scores, -1e30)
+        best = m_sc[...]
+        new_best = jnp.maximum(best, jnp.max(masked, axis=1, keepdims=True))
+        weights = jnp.where(keep, jnp.exp(masked - new_best), 0.0)
+        factor = jnp.exp(best - new_best)
+        l_sc[...] = l_sc[...] * factor + jnp.sum(weights, axis=1, keepdims=True)
+        mixed = jnp.dot(weights.astype(jnp.bfloat16), v_ref[...], preferred_element_type=jnp.float32)
+        acc_sc[...] = acc_sc[...] * factor + mixed
+        m_sc[...] = new_best
+
+    @pl.when(step == pl.num_programs(1) - 1)
+    def _():
+        o_ref[...] = (acc_sc[...] / l_sc[...]).astype(o_ref.dtype)
+
+
+def flash_attention(queries, keys, values, query_start, token_first):
+    tokens, heads, head_size = queries.shape
+    q_rows = min(256, tokens)
+    k_rows = 2 * q_rows
+    blocks = tokens // q_rows
+    steps = (W + q_rows) // k_rows + 1
+    stacked = queries.reshape(blocks, q_rows, heads, head_size).transpose(0, 2, 1, 3)
+    stacked = stacked.reshape(blocks * heads * q_rows, head_size)
+    starts = jnp.broadcast_to(
+        query_start.reshape(blocks, 1, q_rows), (blocks, heads, q_rows)
+    ).reshape(blocks * heads * q_rows, 1)
+    lowest = jnp.min(query_start.reshape(blocks, q_rows), axis=1)
+    rows = heads * q_rows
+
+    def kv_map(i, j, first, low):
+        return (i * q_rows // k_rows + j, 0)
+
+    out = pl.pallas_call(
+        functools.partial(flash_kernel, q_rows, tokens),
+        grid_spec=pltpu.PrefetchScalarGridSpec(
+            num_scalar_prefetch=2,
+            grid=(blocks, steps),
+            in_specs=[
+                pl.BlockSpec((rows, head_size), lambda i, j, first, low: (i, 0)),
+                pl.BlockSpec((k_rows, head_size), kv_map),
+                pl.BlockSpec((k_rows, head_size), kv_map),
+                pl.BlockSpec((rows, 1), lambda i, j, first, low: (i, 0)),
+            ],
+            out_specs=pl.BlockSpec((rows, head_size), lambda i, j, first, low: (i, 0)),
+            scratch_shapes=[
+                pltpu.VMEM((rows, 1), jnp.float32),
+                pltpu.VMEM((rows, 1), jnp.float32),
+                pltpu.VMEM((rows, head_size), jnp.float32),
+            ],
+        ),
+        out_shape=jax.ShapeDtypeStruct((blocks * rows, head_size), jnp.bfloat16),
+        compiler_params=pltpu.CompilerParams(dimension_semantics=("arbitrary", "arbitrary")),
+    )(token_first.reshape(1), lowest, stacked, keys, values, starts)
+    return (
+        out.reshape(blocks, heads, q_rows, head_size)
+        .transpose(0, 2, 1, 3)
+        .reshape(tokens, heads * head_size)
+    )
 
 
 def body(tokens_in, norm_gain, q_weight, kv_weight, out_weight, segment_ids, page_table):
@@ -125,25 +165,10 @@
     key_rows = rotate_half(projected[:, :head_size], cosine, sine_table).astype(jnp.bfloat16)
     value_rows = projected[:, head_size:].astype(jnp.bfloat16)
     keyval = jnp.concatenate([key_rows, value_rows], axis=1)
-    block_rows = min(512, tok_rows)
-    initial = (
-        jnp.full((local_heads, tok_rows), -1e30, jnp.float32),
-        jnp.zeros((local_heads, tok_rows), jnp.float32),
-        jnp.zeros((local_heads, tok_rows, head_size), jnp.float32),
-    )
-
-    def fold_piece(carry, piece, start):
-        return attend_piece(carry, piece, start, queries, token_first, query_start, block_rows)
-
-    state = fold_piece(initial, keyval, token_first)
     earlier = from_behind(keyval, "seq", 1)
-    state = fold_piece(state, earlier, token_first - tok_rows)
-    best, totals, accum = state
-    attended = (
-        (accum / totals[..., None])
-        .transpose(1, 0, 2)
-        .reshape(tok_rows, local_heads * head_size)
-        .astype(jnp.bfloat16)
+    window = jnp.concatenate([earlier, keyval], axis=0)
+    attended = flash_attention(
+        queries, window[:, :head_size], window[:, head_size:], query_start, token_first
     )
     partial_term = lax.dot_general(
         attended, w_output, (((1,), (1,)), ((), ())), preferred_element_type=jnp.float32

time: 357 us -> 320 us (0.90)
  Pallas kernels: 0 us -> 59.7 us
  matrix products: 58.4 us -> 14 us
  other arithmetic: 51.3 us -> 20.3 us
  loops' own time: 16.2 us -> 0 us
  starting transfers between devices: 150 us -> 137 us
  local copies, waits for them, and re-layouts: 16.8 us -> 27.7 us
    pallas_call x0 -> x1, Pallas kernels: none -> 59.7 us  [flash_attention(): pl.pallas_call(functools.partial(flash_kernel, q_rows, tokens), grid_spec...]
    dot_general x10 -> x0, matrix products: 44.4 us -> none  [the longest x5 23.2 us: compute(): jnp.einsum('hqk,kd->hqd', weights.astype(jnp.bfloat16), value_rows, prefe...]
    reduce_sum x5 -> x0, other arithmetic: 24.4 us -> none  [compute(): new_total = total_block * factor + jnp.sum(weights, axis=-1)]
    another operation x10 -> x0, loops' own time: 16.2 us -> none  [the longest x2 15.7 us: attend_piece(): return lax.fori_loop(0, blocks, one_block, carry)]
    and x5 -> x0, other arithmetic: 14.5 us -> none  [compute(): keep = keep & (query_index[:, None] - key_index[None, :] < W)]
    ppermute x15, starting transfers between devices: 147 us -> 134 us  [shift_round(): return lax.ppermute(x, axis, [(i, (i + by) % peers) for i in range(peers)])]
    reshape x0 -> x4, local copies, waits for them, and re-layouts: none -> 7.71 us  [the longest x1 5.27 us: flash_attention(): starts = jnp.broadcast_to(query_start.reshape(blocks, 1, q_rows), (blocks...]
    slice x17 -> x2, local copies, waits for them, and re-layouts: 10.1 us -> 2.55 us  [the longest x1 1.69 us: body(): window[:, head_size:]]
  transfers between devices with their start and end apart: 19 -> 19, of which waited for: 3 -> 3; matrix products, arithmetic and copies ran while one was open for 33% -> 16% of each run, Pallas kernels for 0% -> 19%
where the time goes in v4:
time: 320 us; the launch traced here: 318 us
  starting transfers between devices  137 us (43%)
  Pallas kernels  59.7 us (19%)
  waiting for transfers between devices  30.2 us (9%)
  local copies, waits for them, and re-layouts  27.7 us (9%)
  other arithmetic  20.3 us (6%)
  blocking collectives  14.1 us (4%)
  between operations  14.1 us (4%)
  matrix products  14 us (4%)
    ppermute x15, starting transfers between devices, shift_round(): return lax.ppermute(x, axis, [(i, (i + by) % peers) for i in range(peers)])  134 us
    pallas_call x1, Pallas kernels, flash_attention(): pl.pallas_call(functools.partial(flash_kernel, q_rows, tokens), grid_spec...  59.7 us
    all_gather x1, waiting for transfers between devices, body(): lax.all_gather(jnp.concatenate([q_weight, kv_own], axis=1), 'seq', axis=0...  24.6 us
    psum x1, blocking collectives, body(): seg_total = lax.psum(seg_hist, 'seq')  14.1 us
    another operation x4, other arithmetic  8.99 us
    unnamed x21, local copies, waits for them, and re-layouts  7.58 us
    dot_general x1, matrix products, body(): lax.dot_general(attended, w_output, (((1,), (1,)), ((), ())), preferred_e...  6.86 us
    dot_general x1, matrix products, body(): jnp.dot(normed, w_inputs, preferred_element_type=jnp.float32)  6.65 us
  transfers between devices with their start and end apart: 19, of which 3 were waited for; matrix products, arithmetic and copies ran while one was open for 16% of the time, Pallas kernels for 19%

profile of v4, /device:TPU:1, one launch (start us, length us, event | category | flops | bytes accessed | tf_op | source)
XLA Modules:
  0.0 317.6 jit_solution(11483928351654577740)
XLA Ops:
  10.4 5.1 %fusion = f32[2048]{0:T(1024)S(1)} fusion(bf16[2048,2048]{1,0:T(8,128)(2,1)} %param.7), kind=kLoop, calls=%fused_computation.2 | loop fusion | flops 12580864 | bytes 8396800 | tf_op jit(solution)/shard_map/reduce_sum | solution.py:143
  15.7 14.1 %psum.7 = s32[32]{0:T(128)S(1)} all-reduce(s32[32]{0:T(128)S(1)} %convert_reduce_fusion), channel_id=1, replica_groups=mesh['seq'=16,'mp'=8] {'seq'}, use_global_device_ids=true, to_apply=%region_1.2 | all-reduce | flops 32 | bytes 256 | tf_op jit(solution)/shard_map/psum | solution.py:149
  30.2 5.3 %reshape.165.qs_ref = s32[8192,1]{1,0:T(8,128)} reshape(s32[8,4,256]{2,1,0:T(4,128)S(1)} %broadcast_in_dim.26) | data formatting | bytes 65536 | tf_op jit(solution)/shard_map/reshape | solution.py:91
  36.2 24.6 %all-gather.3.cloned.1.call-done = bf16[2048,384]{1,0:T(8,128)(2,1)} async-done(((bf16[128,384]{1,0:T(8,128)(2,1)}), bf16[2048,384]{1,0:T(8,128)(2,1)}) %all-gather.3.cloned.1.call-update) | async-done | bytes 1572880 | tf_op jit(solution)/shard_map/all_gather | solution.py:138
  60.8 6.6 %fusion.3 = f32[2048,384]{0,1:T(8,128)S(1)} fusion(bf16[2048,384]{1,0:T(8,128)(2,1)} %all-gather.3.cloned.1.call-done, bf16[2048,2048]{1,0:T(8,128)(2,1)} %param.7, f32[2048]{0:T(1024)S(1)} %copy-done.5, f32[2048]{0:T(1024)S(1)} %add_rsqrt_fusion), kind=kOutput, calls=%fused_computation.5 | convolution fusion | flops 3238002688 | bytes 13123584 | tf_op jit(solution)/shard_map/dot_general | solution.py:161
  68.3 2.5 copy.51
  72.4 7.6 %subtract_convert_fusion = (bf16[2048,32]{1,0:T(8,128)(2,1)S(1)}, bf16[2048,32]{1,0:T(8,128)(2,1)S(1)}, f32[2048,32]{1,0:T(8,128)}, f32[2048,32]{1,0:T(8,128)}) fusion(f32[2048,32]{1,0:T(8,128)S(1)} %copy.52, f32[2048,32]{1,0:T(8,128)} %copy.51, f32[2048]{0:T(1024)S(1)} %subtract_convert_fusion.2, f32[32]{0:T(128)S(1)} %multiply_exponential_fusion), kind=kLoop, calls=%fused_computation.31 | loop fusion | flops 589824 | bytes 1319040 | tf_op jit(solution)/shard_map/convert.2
  82.0 3.2 %collective-permute-start = (bf16[2048,128]{1,0:T(8,128)(2,1)}, bf16[2048,128]{1,0:T(8,128)(2,1)}, u32[]{:S(2)}, u32[]{:S(2)}) collective-permute-start(bf16[2048,128]{1,0:T(8,128)(2,1)} %pad_maximum_fusion), channel_id=1, source_target_pairs={{0,8},{8,16},{16,24},{24,32},{32,40},{40,48},{48,56},{56,64},{64,7... | collective-permute-start | bytes 1572872 | tf_op jit(solution)/shard_map/ppermute | solution.py:19
  85.3 1.5 copy.40
  86.8 2.2 copy.41
  90.6 2.0 copy.42
  92.7 1.5 maximum_maximum_fusion
  94.2 1.7 fusion.36
  95.9 59.7 %shard_map.86 = bf16[8192,64]{1,0:T(8,128)(2,1)} custom-call(s32[1]{0:T(128)} %bitcast.first_ref, s32[8]{0:T(128)} %reduce_min.9.lowest_ref, bf16[8192,64]{1,0:T(8,128)(2,1)} %bitcast.41, bf16[4096,64]{1,0:T(8,128)(2,1)} %get-tuple-element.17.k_ref, bf16[4096,64]{1,0:T(8,128)(2,1)} %get-tuple-element.16.v_ref, s32[8192,1]{1,0:T(8,128)} %reshape.165.qs_ref), custom_call_target="tpu_custom_call" | custom-call | tf_op jit(solution)/shard_map/pallas_call | solution.py:98
  155.6 2.2 copy.47
  158.1 6.9 %convolution_convert_fusion = bf16[2048,2048]{1,0:T(8,128)(2,1)} fusion(bf16[2048,256]{0,1:T(8,128)(2,1)S(1)} %bitcast.43, bf16[2048,256]{1,0:T(8,128)(2,1)} %all-gather.5.cloned.1.call-done), kind=kOutput, calls=%fused_computation.8 | convolution fusion | flops 2151677952 | bytes 10485760 | tf_op jit(solution)/shard_map/dot_general | solution.py:173
  167.9 34.2 %collective-permute-start.1 = (bf16[1,65,128]{2,0,1:T(2,128)(2,1)S(1)}, bf16[1,65,128]{2,0,1:T(2,128)(2,1)S(1)}, u32[]{:S(2)}, u32[]{:S(2)}) collective-permute-start(bf16[1,65,128]{2,0,1:T(2,128)(2,1)S(1)} %get-tuple-element.20), channel_id=1, source_target_pairs={{0,8},{8,16},{16,24},{24,32},{32,40},{40,48},{48,56},{56,64},{64,7... | collective-permute-start | bytes 49928 | tf_op jit(solution)/shard_map/ppermute | solution.py:24
  203.8 2.1 collective-permute-start.3
  205.9 5.2 %collective-permute-start.4 = (bf16[1,65,128]{2,0,1:T(2,128)(2,1)S(1)}, bf16[1,65,128]{2,0,1:T(2,128)(2,1)S(1)}, u32[]{:S(2)}, u32[]{:S(2)}) collective-permute-start(bf16[1,65,128]{2,0,1:T(2,128)(2,1)S(1)} %get-tuple-element.23), channel_id=1, source_target_pairs={{0,32},{8,40},{16,48},{24,56},{32,64},{40,72},{48,80},{56,88},{64,... | collective-permute-start | bytes 49928 | tf_op jit(solution)/shard_map/ppermute | solution.py:24
  212.2 5.8 %collective-permute-start.7 = (bf16[1,65,128]{2,0,1:T(2,128)(2,1)S(1)}, bf16[1,65,128]{2,0,1:T(2,128)(2,1)S(1)}, u32[]{:S(2)}, u32[]{:S(2)}) collective-permute-start(bf16[1,65,128]{2,0,1:T(2,128)(2,1)S(1)} %get-tuple-element.27), channel_id=1, source_target_pairs={{0,56},{8,64},{16,72},{24,80},{32,88},{40,96},{48,104},{56,112},{6... | collective-permute-start | bytes 49928 | tf_op jit(solution)/shard_map/ppermute | solution.py:24
  218.2 78.6 %collective-permute-start.9 = (bf16[1,65,128]{2,0,1:T(2,128)(2,1)S(1)}, bf16[1,65,128]{2,0,1:T(2,128)(2,1)S(1)}, u32[]{:S(2)}, u32[]{:S(2)}) collective-permute-start(bf16[1,65,128]{2,0,1:T(2,128)(2,1)S(1)} %get-tuple-element.29), channel_id=1, source_target_pairs={{0,72},{8,80},{16,88},{24,96},{32,104},{40,112},{48,120},{56,0},{6... | collective-permute-start | bytes 49928 | tf_op jit(solution)/shard_map/ppermute | solution.py:24
  298.1 4.3 %collective-permute-start.12 = (bf16[1,65,128]{2,0,1:T(2,128)(2,1)S(1)}, bf16[1,65,128]{2,0,1:T(2,128)(2,1)S(1)}, u32[]{:S(2)}, u32[]{:S(2)}) collective-permute-start(bf16[1,65,128]{2,0,1:T(2,128)(2,1)S(1)} %get-tuple-element.33), channel_id=1, source_target_pairs={{0,96},{8,104},{16,112},{24,120},{32,0},{40,8},{48,16},{56,24},{64... | collective-permute-start | bytes 49928 | tf_op jit(solution)/shard_map/ppermute | solution.py:24
  303.4 3.8 %collective-permute-done.13 = bf16[1,65,128]{2,0,1:T(2,128)(2,1)S(1)} collective-permute-done((bf16[1,65,128]{2,0,1:T(2,128)(2,1)S(1)}, bf16[1,65,128]{2,0,1:T(2,128)(2,1)S(1)}, u32[]{:S(2)}, u32[]{:S(2)}) %collective-permute-start.13) | collective-permute-done | bytes 16672 | tf_op jit(solution)/shard_map/ppermute | solution.py:24
  307.2 2.6 concatenate.34
  (88 shorter events, 20.3 us)
Async XLA Ops:
  7.2 53.6 %all-gather.3.cloned.1.call-start = ((), (), s32[]{:S(2)}) async-start(), calls=%async_computation.1 | async-start | bytes 1671168 | tf_op jit(solution)/shard_map/all_gather | solution.py:138
  9.6 148.5 %all-gather.5.cloned.1.call-start = ((), (), s32[]{:S(2)}) async-start(), calls=%async_computation.2 | async-start | bytes 1114112 | tf_op jit(solution)/shard_map/all_gather | solution.py:141
  10.3 300.7 %reduce-scatter.2.cloned.1.call-start = ((), (), s32[]{:S(2)}) async-start(), calls=%async_computation.3 | async-start | bytes 9437184 | tf_op jit(solution)/shard_map/reduce_scatter | solution.py:176
  10.4 5.1 %copy-start.4 = (s32[2048]{0:T(1024)S(1)}, s32[2048]{0:T(1024)}, u32[]{:S(2)}) copy-start(s32[2048]{0:T(1024)} %param.12) | copy-start | bytes 24580
  15.5 45.3 %copy-start.5 = (f32[2048]{0:T(1024)S(1)}, f32[2048]{0:T(1024)}, u32[]{:S(2)}) copy-start(f32[2048]{0:T(1024)} %param.8) | copy-start | bytes 24580
  67.4 3.4 %copy-start.1 = (f32[2048,384]{0,1:T(8,128)}, f32[2048,384]{0,1:T(8,128)S(1)}, u32[]{:S(2)}) copy-start(f32[2048,384]{0,1:T(8,128)S(1)} %fusion.3) | copy-start | bytes 9437188
  79.9 9.1 %slice-start = ((f32[2048,384]{0,1:T(8,128)}), f32[2048,256]{0,1:T(8,128)S(1)}, s32[]{:S(2)}) async-start(f32[2048,384]{0,1:T(8,128)} %copy-done.1), calls=%async_computation.4 | async-start | bytes 4194304 | tf_op jit(solution)/shard_map/slice | solution.py:162
  82.0 10.6 %collective-permute-start = (bf16[2048,128]{1,0:T(8,128)(2,1)}, bf16[2048,128]{1,0:T(8,128)(2,1)}, u32[]{:S(2)}, u32[]{:S(2)}) collective-permute-start(bf16[2048,128]{1,0:T(8,128)(2,1)} %pad_maximum_fusion), channel_id=1, source_target_pairs={{0,8},{8,16},{16,24},{24,32},{32,40},{40,48},{48,56},{56,64},{64,7... | collective-permute-start | bytes 1572872 | tf_op jit(solution)/shard_map/ppermute | solution.py:19
  90.4 2.3 copy-start.3
  167.9 37.9 %collective-permute-start.1 = (bf16[1,65,128]{2,0,1:T(2,128)(2,1)S(1)}, bf16[1,65,128]{2,0,1:T(2,128)(2,1)S(1)}, u32[]{:S(2)}, u32[]{:S(2)}) collective-permute-start(bf16[1,65,128]{2,0,1:T(2,128)(2,1)S(1)} %get-tuple-element.20), channel_id=1, source_target_pairs={{0,8},{8,16},{16,24},{24,32},{32,40},{40,48},{48,56},{56,64},{64,7... | collective-permute-start | bytes 49928 | tf_op jit(solution)/shard_map/ppermute | solution.py:24
  202.3 8.8 %collective-permute-start.14 = (bf16[1,65,128]{2,0,1:T(2,128)(2,1)S(1)}, bf16[1,65,128]{2,0,1:T(2,128)(2,1)S(1)}, u32[]{:S(2)}, u32[]{:S(2)}) collective-permute-start(bf16[1,65,128]{2,0,1:T(2,128)(2,1)S(1)} %get-tuple-element.24), channel_id=1, source_target_pairs={{0,112},{8,120},{16,0},{24,8},{32,16},{40,24},{48,32},{56,40},{64,... | collective-permute-start | bytes 49928 | tf_op jit(solution)/shard_map/ppermute | solution.py:24
  202.3 9.8 %collective-permute-start.15 = (bf16[1,65,128]{2,0,1:T(2,128)(2,1)S(1)}, bf16[1,65,128]{2,0,1:T(2,128)(2,1)S(1)}, u32[]{:S(2)}, u32[]{:S(2)}) collective-permute-start(bf16[1,65,128]{2,0,1:T(2,128)(2,1)S(1)} %get-tuple-element.18), channel_id=1, source_target_pairs={{0,120},{8,0},{16,8},{24,16},{32,24},{40,32},{48,40},{56,48},{64,5... | collective-permute-start | bytes 49928 | tf_op jit(solution)/shard_map/ppermute | solution.py:24
  202.4 9.8 %collective-permute-start.2 = (bf16[1,65,128]{2,0,1:T(2,128)(2,1)S(1)}, bf16[1,65,128]{2,0,1:T(2,128)(2,1)S(1)}, u32[]{:S(2)}, u32[]{:S(2)}) collective-permute-start(bf16[1,65,128]{2,0,1:T(2,128)(2,1)S(1)} %get-tuple-element.21), channel_id=1, source_target_pairs={{0,16},{8,24},{16,32},{24,40},{32,48},{40,56},{48,64},{56,72},{64,... | collective-permute-start | bytes 49928 | tf_op jit(solution)/shard_map/ppermute | solution.py:24
  203.8 14.3 %collective-permute-start.3 = (bf16[1,65,128]{2,0,1:T(2,128)(2,1)S(1)}, bf16[1,65,128]{2,0,1:T(2,128)(2,1)S(1)}, u32[]{:S(2)}, u32[]{:S(2)}) collective-permute-start(bf16[1,65,128]{2,0,1:T(2,128)(2,1)S(1)} %get-tuple-element.22), channel_id=1, source_target_pairs={{0,24},{8,32},{16,40},{24,48},{32,56},{40,64},{48,72},{56,80},{64,... | collective-permute-start | bytes 49928 | tf_op jit(solution)/shard_map/ppermute | solution.py:24
  205.9 12.3 %collective-permute-start.4 = (bf16[1,65,128]{2,0,1:T(2,128)(2,1)S(1)}, bf16[1,65,128]{2,0,1:T(2,128)(2,1)S(1)}, u32[]{:S(2)}, u32[]{:S(2)}) collective-permute-start(bf16[1,65,128]{2,0,1:T(2,128)(2,1)S(1)} %get-tuple-element.23), channel_id=1, source_target_pairs={{0,32},{8,40},{16,48},{24,56},{32,64},{40,72},{48,80},{56,88},{64,... | collective-permute-start | bytes 49928 | tf_op jit(solution)/shard_map/ppermute | solution.py:24
  211.0 85.7 %collective-permute-start.5 = (bf16[1,65,128]{2,0,1:T(2,128)(2,1)S(1)}, bf16[1,65,128]{2,0,1:T(2,128)(2,1)S(1)}, u32[]{:S(2)}, u32[]{:S(2)}) collective-permute-start(bf16[1,65,128]{2,0,1:T(2,128)(2,1)S(1)} %get-tuple-element.25), channel_id=1, source_target_pairs={{0,40},{8,48},{16,56},{24,64},{32,72},{40,80},{48,88},{56,96},{64,... | collective-permute-start | bytes 49928 | tf_op jit(solution)/shard_map/ppermute | solution.py:24
  212.1 85.0 %collective-permute-start.6 = (bf16[1,65,128]{2,0,1:T(2,128)(2,1)S(1)}, bf16[1,65,128]{2,0,1:T(2,128)(2,1)S(1)}, u32[]{:S(2)}, u32[]{:S(2)}) collective-permute-start(bf16[1,65,128]{2,0,1:T(2,128)(2,1)S(1)} %get-tuple-element.26), channel_id=1, source_target_pairs={{0,48},{8,56},{16,64},{24,72},{32,80},{40,88},{48,96},{56,104},{64... | collective-permute-start | bytes 49928 | tf_op jit(solution)/shard_map/ppermute | solution.py:24
  212.2 85.9 %collective-permute-start.7 = (bf16[1,65,128]{2,0,1:T(2,128)(2,1)S(1)}, bf16[1,65,128]{2,0,1:T(2,128)(2,1)S(1)}, u32[]{:S(2)}, u32[]{:S(2)}) collective-permute-start(bf16[1,65,128]{2,0,1:T(2,128)(2,1)S(1)} %get-tuple-element.27), channel_id=1, source_target_pairs={{0,56},{8,64},{16,72},{24,80},{32,88},{40,96},{48,104},{56,112},{6... | collective-permute-start | bytes 49928 | tf_op jit(solution)/shard_map/ppermute | solution.py:24
  218.1 84.3 %collective-permute-start.8 = (bf16[1,65,128]{2,0,1:T(2,128)(2,1)S(1)}, bf16[1,65,128]{2,0,1:T(2,128)(2,1)S(1)}, u32[]{:S(2)}, u32[]{:S(2)}) collective-permute-start(bf16[1,65,128]{2,0,1:T(2,128)(2,1)S(1)} %get-tuple-element.28), channel_id=1, source_target_pairs={{0,64},{8,72},{16,80},{24,88},{32,96},{40,104},{48,112},{56,120},{... | collective-permute-start | bytes 49928 | tf_op jit(solution)/shard_map/ppermute | solution.py:24
  218.2 84.2 %collective-permute-start.9 = (bf16[1,65,128]{2,0,1:T(2,128)(2,1)S(1)}, bf16[1,65,128]{2,0,1:T(2,128)(2,1)S(1)}, u32[]{:S(2)}, u32[]{:S(2)}) collective-permute-start(bf16[1,65,128]{2,0,1:T(2,128)(2,1)S(1)} %get-tuple-element.29), channel_id=1, source_target_pairs={{0,72},{8,80},{16,88},{24,96},{32,104},{40,112},{48,120},{56,0},{6... | collective-permute-start | bytes 49928 | tf_op jit(solution)/shard_map/ppermute | solution.py:24
  296.8 5.6 %collective-permute-start.10 = (bf16[1,65,128]{2,0,1:T(2,128)(2,1)S(1)}, bf16[1,65,128]{2,0,1:T(2,128)(2,1)S(1)}, u32[]{:S(2)}, u32[]{:S(2)}) collective-permute-start(bf16[1,65,128]{2,0,1:T(2,128)(2,1)S(1)} %get-tuple-element.31), channel_id=1, source_target_pairs={{0,80},{8,88},{16,96},{24,104},{32,112},{40,120},{48,0},{56,8},{64... | collective-permute-start | bytes 49928 | tf_op jit(solution)/shard_map/ppermute | solution.py:24
  297.1 5.3 %collective-permute-start.11 = (bf16[1,65,128]{2,0,1:T(2,128)(2,1)S(1)}, bf16[1,65,128]{2,0,1:T(2,128)(2,1)S(1)}, u32[]{:S(2)}, u32[]{:S(2)}) collective-permute-start(bf16[1,65,128]{2,0,1:T(2,128)(2,1)S(1)} %get-tuple-element.32), channel_id=1, source_target_pairs={{0,88},{8,96},{16,104},{24,112},{32,120},{40,0},{48,8},{56,16},{64... | collective-permute-start | bytes 49928 | tf_op jit(solution)/shard_map/ppermute | solution.py:24
  298.1 5.3 %collective-permute-start.12 = (bf16[1,65,128]{2,0,1:T(2,128)(2,1)S(1)}, bf16[1,65,128]{2,0,1:T(2,128)(2,1)S(1)}, u32[]{:S(2)}, u32[]{:S(2)}) collective-permute-start(bf16[1,65,128]{2,0,1:T(2,128)(2,1)S(1)} %get-tuple-element.33), channel_id=1, source_target_pairs={{0,96},{8,104},{16,112},{24,120},{32,0},{40,8},{48,16},{56,24},{64... | collective-permute-start | bytes 49928 | tf_op jit(solution)/shard_map/ppermute | solution.py:24
  302.4 4.8 %collective-permute-start.13 = (bf16[1,65,128]{2,0,1:T(2,128)(2,1)S(1)}, bf16[1,65,128]{2,0,1:T(2,128)(2,1)S(1)}, u32[]{:S(2)}, u32[]{:S(2)}) collective-permute-start(bf16[1,65,128]{2,0,1:T(2,128)(2,1)S(1)} %get-tuple-element.30), channel_id=1, source_target_pairs={{0,104},{8,112},{16,120},{24,0},{32,8},{40,16},{48,24},{56,32},{64... | collective-permute-start | bytes 49928 | tf_op jit(solution)/shard_map/ppermute | solution.py:24
  (3 other events, 2.4 us)
Sparse Core Ops, SparseCore 0:
  11.0 49.6 all-gather.2
  63.2 43.5 all-gather.4
  165.1 126.5 reduce-scatter.1

commit v5 on v4

--- a/solution.py
+++ b/solution.py
@@ -34,12 +34,11 @@
     )
 
 
-def flash_kernel(q_rows, tokens, first_ref, lowest_ref, q_ref, k_ref, v_ref, qs_ref, o_ref, m_sc, l_sc, acc_sc):
+def flash_kernel(q_rows, tokens, first_ref, lowest_ref, highest_ref, q_ref, k_ref, v_ref, qs_ref, o_ref, m_sc, l_sc, acc_sc):
     block = pl.program_id(0)
     step = pl.program_id(1)
     rows = q_ref.shape[0]
     k_rows = k_ref.shape[0]
-    head_size = q_ref.shape[1]
 
     @pl.when(step == 0)
     def _():
@@ -54,24 +53,35 @@
     live = (key_last >= lowest_ref[block]) & (key_first <= query_first + q_rows - 1)
     live = live & (query_first - key_last < W)
 
-    @pl.when(live)
-    def _():
-        scores = lax.dot_general(
-            q_ref[...], k_ref[...], (((1,), (1,)), ((), ())), preferred_element_type=jnp.float32
-        ) * (1.0 / math.sqrt(head_size))
-        key_index = key_first + lax.broadcasted_iota(jnp.int32, (rows, k_rows), 1)
-        query_index = query_first + lax.broadcasted_iota(jnp.int32, (rows, k_rows), 0) % q_rows
-        keep = (key_index >= qs_ref[...]) & (key_index <= query_index)
-        keep = keep & (query_index - key_index < W)
-        masked = jnp.where(keep, scores, -1e30)
+    full = (key_first >= highest_ref[block]) & (key_last <= query_first)
+    full = full & (query_first + q_rows - 1 - key_first < W)
+
+    def update(masked):
         best = m_sc[...]
         new_best = jnp.maximum(best, jnp.max(masked, axis=1, keepdims=True))
-        weights = jnp.where(keep, jnp.exp(masked - new_best), 0.0)
+        weights = jnp.exp(masked - new_best)
         factor = jnp.exp(best - new_best)
         l_sc[...] = l_sc[...] * factor + jnp.sum(weights, axis=1, keepdims=True)
         mixed = jnp.dot(weights.astype(jnp.bfloat16), v_ref[...], preferred_element_type=jnp.float32)
         acc_sc[...] = acc_sc[...] * factor + mixed
         m_sc[...] = new_best
+
+    def scores():
+        return lax.dot_general(
+            q_ref[...], k_ref[...], (((1,), (1,)), ((), ())), preferred_element_type=jnp.float32
+        )
+
+    @pl.when(live & full)
+    def _():
+        update(scores())
+
+    @pl.when(live & jnp.logical_not(full))
+    def _():
+        key_index = key_first + lax.broadcasted_iota(jnp.int32, (rows, k_rows), 1)
+        query_index = query_first + lax.broadcasted_iota(jnp.int32, (rows, k_rows), 0) % q_rows
+        keep = (key_index >= qs_ref[...]) & (key_index <= query_index)
+        keep = keep & (query_index - key_index < W)
+        update(jnp.where(keep, scores(), -jnp.inf))
 
     @pl.when(step == pl.num_programs(1) - 1)
     def _():
@@ -84,29 +94,31 @@
     k_rows = 2 * q_rows
     blocks = tokens // q_rows
     steps = (W + q_rows) // k_rows + 1
-    stacked = queries.reshape(blocks, q_rows, heads, head_size).transpose(0, 2, 1, 3)
+    scaled = queries * jnp.asarray(1.0 / math.sqrt(head_size), queries.dtype)
+    stacked = scaled.reshape(blocks, q_rows, heads, head_size).transpose(0, 2, 1, 3)
     stacked = stacked.reshape(blocks * heads * q_rows, head_size)
     starts = jnp.broadcast_to(
         query_start.reshape(blocks, 1, q_rows), (blocks, heads, q_rows)
     ).reshape(blocks * heads * q_rows, 1)
     lowest = jnp.min(query_start.reshape(blocks, q_rows), axis=1)
+    highest = jnp.max(query_start.reshape(blocks, q_rows), axis=1)
     rows = heads * q_rows
 
-    def kv_map(i, j, first, low):
+    def kv_map(i, j, first, low, high):
         return (i * q_rows // k_rows + j, 0)
 
     out = pl.pallas_call(
         functools.partial(flash_kernel, q_rows, tokens),
         grid_spec=pltpu.PrefetchScalarGridSpec(
-            num_scalar_prefetch=2,
+            num_scalar_prefetch=3,
             grid=(blocks, steps),
             in_specs=[
-                pl.BlockSpec((rows, head_size), lambda i, j, first, low: (i, 0)),
+                pl.BlockSpec((rows, head_size), lambda i, j, first, low, high: (i, 0)),
                 pl.BlockSpec((k_rows, head_size), kv_map),
                 pl.BlockSpec((k_rows, head_size), kv_map),
-                pl.BlockSpec((rows, 1), lambda i, j, first, low: (i, 0)),
+                pl.BlockSpec((rows, 1), lambda i, j, first, low, high: (i, 0)),
             ],
-            out_specs=pl.BlockSpec((rows, head_size), lambda i, j, first, low: (i, 0)),
+            out_specs=pl.BlockSpec((rows, head_size), lambda i, j, first, low, high: (i, 0)),
             scratch_shapes=[
                 pltpu.VMEM((rows, 1), jnp.float32),
                 pltpu.VMEM((rows, 1), jnp.float32),
@@ -115,7 +127,7 @@
         ),
         out_shape=jax.ShapeDtypeStruct((blocks * rows, head_size), jnp.bfloat16),
         compiler_params=pltpu.CompilerParams(dimension_semantics=("arbitrary", "arbitrary")),
-    )(token_first.reshape(1), lowest, stacked, keys, values, starts)
+    )(token_first.reshape(1), lowest, highest, stacked, keys, values, starts)
     return (
         out.reshape(blocks, heads, q_rows, head_size)
         .transpose(0, 2, 1, 3)

time: 320 us -> 333 us (1.041)
  starting transfers between devices: 137 us -> 161 us
  Pallas kernels: 59.7 us -> 51.3 us
    ppermute x15, starting transfers between devices: 134 us -> 158 us  [shift_round(): return lax.ppermute(x, axis, [(i, (i + by) % peers) for i in range(peers)])]
    pallas_call x1, Pallas kernels: 59.7 us -> 51.3 us  [flash_attention(): pl.pallas_call(functools.partial(flash_kernel, q_rows, tokens), grid_spec...]
  transfers between devices with their start and end apart: 19 -> 19, of which waited for: 3 -> 3; matrix products, arithmetic and copies ran while one was open for 16% -> 15% of each run, Pallas kernels for 19% -> 15%
where the time goes in v5:
time: 333 us; the launch traced here: 332 us
  starting transfers between devices  161 us (48%)
  Pallas kernels  51.3 us (15%)
  waiting for transfers between devices  29 us (9%)
  local copies, waits for them, and re-layouts  27.7 us (8%)
  other arithmetic  20.4 us (6%)
  blocking collectives  14.1 us (4%)
  between operations  14.1 us (4%)
  matrix products  14 us (4%)
    ppermute x15, starting transfers between devices, shift_round(): return lax.ppermute(x, axis, [(i, (i + by) % peers) for i in range(peers)])  158 us
    pallas_call x1, Pallas kernels, flash_attention(): pl.pallas_call(functools.partial(flash_kernel, q_rows, tokens), grid_spec...  51.3 us
    all_gather x1, waiting for transfers between devices, body(): lax.all_gather(jnp.concatenate([q_weight, kv_own], axis=1), 'seq', axis=0...  24.6 us
    psum x1, blocking collectives, body(): seg_total = lax.psum(seg_hist, 'seq')  14.1 us
    another operation x4, other arithmetic  8.99 us
    unnamed x21, local copies, waits for them, and re-layouts  7.58 us
    dot_general x1, matrix products, body(): lax.dot_general(attended, w_output, (((1,), (1,)), ((), ())), preferred_e...  6.87 us
  transfers between devices with their start and end apart: 19, of which 3 were waited for; matrix products, arithmetic and copies ran while one was open for 15% of the time, Pallas kernels for 15%

profile of v5, /device:TPU:1, one launch (start us, length us, event | category | flops | bytes accessed | tf_op | source)
XLA Modules:
  0.0 332.1 jit_solution(2176913674115532660)
XLA Ops:
  10.4 5.1 %fusion = f32[2048]{0:T(1024)S(1)} fusion(bf16[2048,2048]{1,0:T(8,128)(2,1)} %param.7), kind=kLoop, calls=%fused_computation.2 | loop fusion | flops 12580864 | bytes 8396800 | tf_op jit(solution)/shard_map/reduce_sum | solution.py:155
  15.7 14.1 %psum.7 = s32[32]{0:T(128)S(1)} all-reduce(s32[32]{0:T(128)S(1)} %convert_reduce_fusion), channel_id=1, replica_groups=mesh['seq'=16,'mp'=8] {'seq'}, use_global_device_ids=true, to_apply=%region_1.2 | all-reduce | flops 32 | bytes 256 | tf_op jit(solution)/shard_map/psum | solution.py:161
  30.9 5.2 %reshape.166.qs_ref = s32[8192,1]{1,0:T(8,128)} reshape(s32[8,4,256]{2,1,0:T(4,128)S(1)} %broadcast_in_dim.26) | data formatting | bytes 65536 | tf_op jit(solution)/shard_map/reshape | solution.py:102
  36.2 24.6 %all-gather.3.cloned.1.call-done = bf16[2048,384]{1,0:T(8,128)(2,1)} async-done(((bf16[128,384]{1,0:T(8,128)(2,1)}), bf16[2048,384]{1,0:T(8,128)(2,1)}) %all-gather.3.cloned.1.call-update) | async-done | bytes 1572880 | tf_op jit(solution)/shard_map/all_gather | solution.py:150
  60.8 6.6 %fusion.3 = f32[2048,384]{0,1:T(8,128)S(1)} fusion(bf16[2048,384]{1,0:T(8,128)(2,1)} %all-gather.3.cloned.1.call-done, bf16[2048,2048]{1,0:T(8,128)(2,1)} %param.7, f32[2048]{0:T(1024)S(1)} %copy-done.5, f32[2048]{0:T(1024)S(1)} %add_rsqrt_fusion), kind=kOutput, calls=%fused_computation.5 | convolution fusion | flops 3238002688 | bytes 13123584 | tf_op jit(solution)/shard_map/dot_general | solution.py:173
  68.3 2.5 copy.51
  72.4 7.6 %subtract_convert_fusion = (bf16[2048,32]{1,0:T(8,128)(2,1)S(1)}, bf16[2048,32]{1,0:T(8,128)(2,1)S(1)}, f32[2048,32]{1,0:T(8,128)}, f32[2048,32]{1,0:T(8,128)}) fusion(f32[2048,32]{1,0:T(8,128)S(1)} %copy.52, f32[2048,32]{1,0:T(8,128)} %copy.51, f32[2048]{0:T(1024)S(1)} %subtract_convert_fusion.2, f32[32]{0:T(128)S(1)} %multiply_exponential_fusion), kind=kLoop, calls=%fused_computation.32 | loop fusion | flops 589824 | bytes 1319040 | tf_op jit(solution)/shard_map/convert.2
  82.0 3.2 collective-permute-start
  86.8 2.2 copy.41
  90.7 2.0 copy.42
  94.2 1.7 fusion.38
  95.9 51.3 %shard_map.86 = bf16[8192,64]{1,0:T(8,128)(2,1)} custom-call(s32[1]{0:T(128)} %bitcast.first_ref, s32[8]{0:T(128)} %get-tuple-element.11.lowest_ref, s32[8]{0:T(128)} %get-tuple-element.10.highest_ref, bf16[8192,64]{1,0:T(8,128)(2,1)} %bitcast.41, bf16[4096,64]{1,0:T(8,128)(2,1)} %get-tuple-element.19.k_ref, bf16[4096,64]{1,0:T(8,128)(2,1)} %get-tuple-element.18.v_ref, ...), custom_call_target="tpu_custom_call" | custom-call | tf_op jit(solution)/shard_map/pallas_call | solution.py:110
  147.3 2.2 copy.47
  149.8 6.9 %convolution_convert_fusion = bf16[2048,2048]{1,0:T(8,128)(2,1)} fusion(bf16[2048,256]{0,1:T(8,128)(2,1)S(1)} %bitcast.43, bf16[2048,256]{1,0:T(8,128)(2,1)} %all-gather.5.cloned.1.call-done), kind=kOutput, calls=%fused_computation.8 | convolution fusion | flops 2151677952 | bytes 10485760 | tf_op jit(solution)/shard_map/dot_general | solution.py:185
  159.6 8.8 %collective-permute-start.1 = (bf16[1,65,128]{2,0,1:T(2,128)(2,1)S(1)}, bf16[1,65,128]{2,0,1:T(2,128)(2,1)S(1)}, u32[]{:S(2)}, u32[]{:S(2)}) collective-permute-start(bf16[1,65,128]{2,0,1:T(2,128)(2,1)S(1)} %get-tuple-element.22), channel_id=1, source_target_pairs={{0,8},{8,16},{16,24},{24,32},{32,40},{40,48},{48,56},{56,64},{64,7... | collective-permute-start | bytes 49928 | tf_op jit(solution)/shard_map/ppermute | solution.py:24
  168.6 33.7 %collective-permute-start.14 = (bf16[1,65,128]{2,0,1:T(2,128)(2,1)S(1)}, bf16[1,65,128]{2,0,1:T(2,128)(2,1)S(1)}, u32[]{:S(2)}, u32[]{:S(2)}) collective-permute-start(bf16[1,65,128]{2,0,1:T(2,128)(2,1)S(1)} %get-tuple-element.26), channel_id=1, source_target_pairs={{0,112},{8,120},{16,0},{24,8},{32,16},{40,24},{48,32},{56,40},{64,... | collective-permute-start | bytes 49928 | tf_op jit(solution)/shard_map/ppermute | solution.py:24
  203.0 7.6 %collective-permute-start.2 = (bf16[1,65,128]{2,0,1:T(2,128)(2,1)S(1)}, bf16[1,65,128]{2,0,1:T(2,128)(2,1)S(1)}, u32[]{:S(2)}, u32[]{:S(2)}) collective-permute-start(bf16[1,65,128]{2,0,1:T(2,128)(2,1)S(1)} %get-tuple-element.23), channel_id=1, source_target_pairs={{0,16},{8,24},{16,32},{24,40},{32,48},{40,56},{48,64},{56,72},{64,... | collective-permute-start | bytes 49928 | tf_op jit(solution)/shard_map/ppermute | solution.py:24
  210.6 8.2 %collective-permute-start.3 = (bf16[1,65,128]{2,0,1:T(2,128)(2,1)S(1)}, bf16[1,65,128]{2,0,1:T(2,128)(2,1)S(1)}, u32[]{:S(2)}, u32[]{:S(2)}) collective-permute-start(bf16[1,65,128]{2,0,1:T(2,128)(2,1)S(1)} %get-tuple-element.24), channel_id=1, source_target_pairs={{0,24},{8,32},{16,40},{24,48},{32,56},{40,64},{48,72},{56,80},{64,... | collective-permute-start | bytes 49928 | tf_op jit(solution)/shard_map/ppermute | solution.py:24
  218.8 10.1 %collective-permute-start.4 = (bf16[1,65,128]{2,0,1:T(2,128)(2,1)S(1)}, bf16[1,65,128]{2,0,1:T(2,128)(2,1)S(1)}, u32[]{:S(2)}, u32[]{:S(2)}) collective-permute-start(bf16[1,65,128]{2,0,1:T(2,128)(2,1)S(1)} %get-tuple-element.25), channel_id=1, source_target_pairs={{0,32},{8,40},{16,48},{24,56},{32,64},{40,72},{48,80},{56,88},{64,... | collective-permute-start | bytes 49928 | tf_op jit(solution)/shard_map/ppermute | solution.py:24
  229.0 80.2 %collective-permute-start.7 = (bf16[1,65,128]{2,0,1:T(2,128)(2,1)S(1)}, bf16[1,65,128]{2,0,1:T(2,128)(2,1)S(1)}, u32[]{:S(2)}, u32[]{:S(2)}) collective-permute-start(bf16[1,65,128]{2,0,1:T(2,128)(2,1)S(1)} %get-tuple-element.29), channel_id=1, source_target_pairs={{0,56},{8,64},{16,72},{24,80},{32,88},{40,96},{48,104},{56,112},{6... | collective-permute-start | bytes 49928 | tf_op jit(solution)/shard_map/ppermute | solution.py:24
  309.8 3.2 collective-permute-start.9
  313.1 3.7 %collective-permute-start.12 = (bf16[1,65,128]{2,0,1:T(2,128)(2,1)S(1)}, bf16[1,65,128]{2,0,1:T(2,128)(2,1)S(1)}, u32[]{:S(2)}, u32[]{:S(2)}) collective-permute-start(bf16[1,65,128]{2,0,1:T(2,128)(2,1)S(1)} %get-tuple-element.35), channel_id=1, source_target_pairs={{0,96},{8,104},{16,112},{24,120},{32,0},{40,8},{48,16},{56,24},{64... | collective-permute-start | bytes 49928 | tf_op jit(solution)/shard_map/ppermute | solution.py:24
  318.7 3.0 collective-permute-done.13
  321.7 2.6 concatenate.34
  (88 shorter events, 21.6 us)
Async XLA Ops:
  7.2 53.6 %all-gather.3.cloned.1.call-start = ((), (), s32[]{:S(2)}) async-start(), calls=%async_computation.1 | async-start | bytes 1671168 | tf_op jit(solution)/shard_map/all_gather | solution.py:150
  9.6 140.2 %all-gather.5.cloned.1.call-start = ((), (), s32[]{:S(2)}) async-start(), calls=%async_computation.2 | async-start | bytes 1114112 | tf_op jit(solution)/shard_map/all_gather | solution.py:153
  10.3 315.2 %reduce-scatter.2.cloned.1.call-start = ((), (), s32[]{:S(2)}) async-start(), calls=%async_computation.3 | async-start | bytes 9437184 | tf_op jit(solution)/shard_map/reduce_scatter | solution.py:188
  10.4 5.1 %copy-start.4 = (s32[2048]{0:T(1024)S(1)}, s32[2048]{0:T(1024)}, u32[]{:S(2)}) copy-start(s32[2048]{0:T(1024)} %param.12) | copy-start | bytes 24580
  15.5 45.3 %copy-start.5 = (f32[2048]{0:T(1024)S(1)}, f32[2048]{0:T(1024)}, u32[]{:S(2)}) copy-start(f32[2048]{0:T(1024)} %param.8) | copy-start | bytes 24580
  67.4 3.4 %copy-start.1 = (f32[2048,384]{0,1:T(8,128)}, f32[2048,384]{0,1:T(8,128)S(1)}, u32[]{:S(2)}) copy-start(f32[2048,384]{0,1:T(8,128)S(1)} %fusion.3) | copy-start | bytes 9437188
  79.9 9.1 %slice-start = ((f32[2048,384]{0,1:T(8,128)}), f32[2048,256]{0,1:T(8,128)S(1)}, s32[]{:S(2)}) async-start(f32[2048,384]{0,1:T(8,128)} %copy-done.1), calls=%async_computation.4 | async-start | bytes 4194304 | tf_op jit(solution)/shard_map/slice | solution.py:174
  82.0 10.7 %collective-permute-start = (bf16[2048,128]{1,0:T(8,128)(2,1)}, bf16[2048,128]{1,0:T(8,128)(2,1)}, u32[]{:S(2)}, u32[]{:S(2)}) collective-permute-start(bf16[2048,128]{1,0:T(8,128)(2,1)} %pad_maximum_fusion), channel_id=1, source_target_pairs={{0,8},{8,16},{16,24},{24,32},{32,40},{40,48},{48,56},{56,64},{64,7... | collective-permute-start | bytes 1572872 | tf_op jit(solution)/shard_map/ppermute | solution.py:19
  90.4 2.3 copy-start.3
  159.6 59.2 %collective-permute-start.1 = (bf16[1,65,128]{2,0,1:T(2,128)(2,1)S(1)}, bf16[1,65,128]{2,0,1:T(2,128)(2,1)S(1)}, u32[]{:S(2)}, u32[]{:S(2)}) collective-permute-start(bf16[1,65,128]{2,0,1:T(2,128)(2,1)S(1)} %get-tuple-element.22), channel_id=1, source_target_pairs={{0,8},{8,16},{16,24},{24,32},{32,40},{40,48},{48,56},{56,64},{64,7... | collective-permute-start | bytes 49928 | tf_op jit(solution)/shard_map/ppermute | solution.py:24
  168.6 60.3 %collective-permute-start.14 = (bf16[1,65,128]{2,0,1:T(2,128)(2,1)S(1)}, bf16[1,65,128]{2,0,1:T(2,128)(2,1)S(1)}, u32[]{:S(2)}, u32[]{:S(2)}) collective-permute-start(bf16[1,65,128]{2,0,1:T(2,128)(2,1)S(1)} %get-tuple-element.26), channel_id=1, source_target_pairs={{0,112},{8,120},{16,0},{24,8},{32,16},{40,24},{48,32},{56,40},{64,... | collective-permute-start | bytes 49928 | tf_op jit(solution)/shard_map/ppermute | solution.py:24
  202.2 26.7 %collective-permute-start.15 = (bf16[1,65,128]{2,0,1:T(2,128)(2,1)S(1)}, bf16[1,65,128]{2,0,1:T(2,128)(2,1)S(1)}, u32[]{:S(2)}, u32[]{:S(2)}) collective-permute-start(bf16[1,65,128]{2,0,1:T(2,128)(2,1)S(1)} %get-tuple-element.20), channel_id=1, source_target_pairs={{0,120},{8,0},{16,8},{24,16},{32,24},{40,32},{48,40},{56,48},{64,5... | collective-permute-start | bytes 49928 | tf_op jit(solution)/shard_map/ppermute | solution.py:24
  203.0 26.0 %collective-permute-start.2 = (bf16[1,65,128]{2,0,1:T(2,128)(2,1)S(1)}, bf16[1,65,128]{2,0,1:T(2,128)(2,1)S(1)}, u32[]{:S(2)}, u32[]{:S(2)}) collective-permute-start(bf16[1,65,128]{2,0,1:T(2,128)(2,1)S(1)} %get-tuple-element.23), channel_id=1, source_target_pairs={{0,16},{8,24},{16,32},{24,40},{32,48},{40,56},{48,64},{56,72},{64,... | collective-permute-start | bytes 49928 | tf_op jit(solution)/shard_map/ppermute | solution.py:24
  210.6 98.6 %collective-permute-start.3 = (bf16[1,65,128]{2,0,1:T(2,128)(2,1)S(1)}, bf16[1,65,128]{2,0,1:T(2,128)(2,1)S(1)}, u32[]{:S(2)}, u32[]{:S(2)}) collective-permute-start(bf16[1,65,128]{2,0,1:T(2,128)(2,1)S(1)} %get-tuple-element.24), channel_id=1, source_target_pairs={{0,24},{8,32},{16,40},{24,48},{32,56},{40,64},{48,72},{56,80},{64,... | collective-permute-start | bytes 49928 | tf_op jit(solution)/shard_map/ppermute | solution.py:24
  218.8 90.9 %collective-permute-start.4 = (bf16[1,65,128]{2,0,1:T(2,128)(2,1)S(1)}, bf16[1,65,128]{2,0,1:T(2,128)(2,1)S(1)}, u32[]{:S(2)}, u32[]{:S(2)}) collective-permute-start(bf16[1,65,128]{2,0,1:T(2,128)(2,1)S(1)} %get-tuple-element.25), channel_id=1, source_target_pairs={{0,32},{8,40},{16,48},{24,56},{32,64},{40,72},{48,80},{56,88},{64,... | collective-permute-start | bytes 49928 | tf_op jit(solution)/shard_map/ppermute | solution.py:24
  228.9 84.1 %collective-permute-start.5 = (bf16[1,65,128]{2,0,1:T(2,128)(2,1)S(1)}, bf16[1,65,128]{2,0,1:T(2,128)(2,1)S(1)}, u32[]{:S(2)}, u32[]{:S(2)}) collective-permute-start(bf16[1,65,128]{2,0,1:T(2,128)(2,1)S(1)} %get-tuple-element.27), channel_id=1, source_target_pairs={{0,40},{8,48},{16,56},{24,64},{32,72},{40,80},{48,88},{56,96},{64,... | collective-permute-start | bytes 49928 | tf_op jit(solution)/shard_map/ppermute | solution.py:24
  228.9 84.1 %collective-permute-start.6 = (bf16[1,65,128]{2,0,1:T(2,128)(2,1)S(1)}, bf16[1,65,128]{2,0,1:T(2,128)(2,1)S(1)}, u32[]{:S(2)}, u32[]{:S(2)}) collective-permute-start(bf16[1,65,128]{2,0,1:T(2,128)(2,1)S(1)} %get-tuple-element.28), channel_id=1, source_target_pairs={{0,48},{8,56},{16,64},{24,72},{32,80},{40,88},{48,96},{56,104},{64... | collective-permute-start | bytes 49928 | tf_op jit(solution)/shard_map/ppermute | solution.py:24
  229.0 84.1 %collective-permute-start.7 = (bf16[1,65,128]{2,0,1:T(2,128)(2,1)S(1)}, bf16[1,65,128]{2,0,1:T(2,128)(2,1)S(1)}, u32[]{:S(2)}, u32[]{:S(2)}) collective-permute-start(bf16[1,65,128]{2,0,1:T(2,128)(2,1)S(1)} %get-tuple-element.29), channel_id=1, source_target_pairs={{0,56},{8,64},{16,72},{24,80},{32,88},{40,96},{48,104},{56,112},{6... | collective-permute-start | bytes 49928 | tf_op jit(solution)/shard_map/ppermute | solution.py:24
  309.2 7.7 %collective-permute-start.8 = (bf16[1,65,128]{2,0,1:T(2,128)(2,1)S(1)}, bf16[1,65,128]{2,0,1:T(2,128)(2,1)S(1)}, u32[]{:S(2)}, u32[]{:S(2)}) collective-permute-start(bf16[1,65,128]{2,0,1:T(2,128)(2,1)S(1)} %get-tuple-element.30), channel_id=1, source_target_pairs={{0,64},{8,72},{16,80},{24,88},{32,96},{40,104},{48,112},{56,120},{... | collective-permute-start | bytes 49928 | tf_op jit(solution)/shard_map/ppermute | solution.py:24
  309.8 8.4 %collective-permute-start.9 = (bf16[1,65,128]{2,0,1:T(2,128)(2,1)S(1)}, bf16[1,65,128]{2,0,1:T(2,128)(2,1)S(1)}, u32[]{:S(2)}, u32[]{:S(2)}) collective-permute-start(bf16[1,65,128]{2,0,1:T(2,128)(2,1)S(1)} %get-tuple-element.31), channel_id=1, source_target_pairs={{0,72},{8,80},{16,88},{24,96},{32,104},{40,112},{48,120},{56,0},{6... | collective-permute-start | bytes 49928 | tf_op jit(solution)/shard_map/ppermute | solution.py:24
  313.0 5.1 %collective-permute-start.10 = (bf16[1,65,128]{2,0,1:T(2,128)(2,1)S(1)}, bf16[1,65,128]{2,0,1:T(2,128)(2,1)S(1)}, u32[]{:S(2)}, u32[]{:S(2)}) collective-permute-start(bf16[1,65,128]{2,0,1:T(2,128)(2,1)S(1)} %get-tuple-element.33), channel_id=1, source_target_pairs={{0,80},{8,88},{16,96},{24,104},{32,112},{40,120},{48,0},{56,8},{64... | collective-permute-start | bytes 49928 | tf_op jit(solution)/shard_map/ppermute | solution.py:24
  313.0 5.7 %collective-permute-start.11 = (bf16[1,65,128]{2,0,1:T(2,128)(2,1)S(1)}, bf16[1,65,128]{2,0,1:T(2,128)(2,1)S(1)}, u32[]{:S(2)}, u32[]{:S(2)}) collective-permute-start(bf16[1,65,128]{2,0,1:T(2,128)(2,1)S(1)} %get-tuple-element.34), channel_id=1, source_target_pairs={{0,88},{8,96},{16,104},{24,112},{32,120},{40,0},{48,8},{56,16},{64... | collective-permute-start | bytes 49928 | tf_op jit(solution)/shard_map/ppermute | solution.py:24
  313.1 5.6 %collective-permute-start.12 = (bf16[1,65,128]{2,0,1:T(2,128)(2,1)S(1)}, bf16[1,65,128]{2,0,1:T(2,128)(2,1)S(1)}, u32[]{:S(2)}, u32[]{:S(2)}) collective-permute-start(bf16[1,65,128]{2,0,1:T(2,128)(2,1)S(1)} %get-tuple-element.35), channel_id=1, source_target_pairs={{0,96},{8,104},{16,112},{24,120},{32,0},{40,8},{48,16},{56,24},{64... | collective-permute-start | bytes 49928 | tf_op jit(solution)/shard_map/ppermute | solution.py:24
  316.9 4.8 %collective-permute-start.13 = (bf16[1,65,128]{2,0,1:T(2,128)(2,1)S(1)}, bf16[1,65,128]{2,0,1:T(2,128)(2,1)S(1)}, u32[]{:S(2)}, u32[]{:S(2)}) collective-permute-start(bf16[1,65,128]{2,0,1:T(2,128)(2,1)S(1)} %get-tuple-element.32), channel_id=1, source_target_pairs={{0,104},{8,112},{16,120},{24,0},{32,8},{40,16},{48,24},{56,32},{64... | collective-permute-start | bytes 49928 | tf_op jit(solution)/shard_map/ppermute | solution.py:24
  (3 other events, 2.4 us)
Sparse Core Ops, SparseCore 0:
  11.0 49.6 all-gather.2
  63.2 43.5 all-gather.4
  156.8 147.8 reduce-scatter.1

commit v6 on v4

--- a/solution.py
+++ b/solution.py
@@ -34,8 +34,8 @@
     )
 
 
-def flash_kernel(q_rows, tokens, first_ref, lowest_ref, q_ref, k_ref, v_ref, qs_ref, o_ref, m_sc, l_sc, acc_sc):
-    block = pl.program_id(0)
+def flash_kernel(q_rows, tokens, first_block, first_ref, lowest_ref, q_ref, k_ref, v_ref, qs_ref, o_ref, m_sc, l_sc, acc_sc):
+    block = pl.program_id(0) + first_block
     step = pl.program_id(1)
     rows = q_ref.shape[0]
     k_rows = k_ref.shape[0]
@@ -78,7 +78,7 @@
         o_ref[...] = (acc_sc[...] / l_sc[...]).astype(o_ref.dtype)
 
 
-def flash_attention(queries, keys, values, query_start, token_first):
+def flash_attention(queries, keys, values, query_start, token_first, first_block, count):
     tokens, heads, head_size = queries.shape
     q_rows = min(256, tokens)
     k_rows = 2 * q_rows
@@ -93,18 +93,18 @@
     rows = heads * q_rows
 
     def kv_map(i, j, first, low):
-        return (i * q_rows // k_rows + j, 0)
+        return ((i + first_block) * q_rows // k_rows + j, 0)
 
     out = pl.pallas_call(
-        functools.partial(flash_kernel, q_rows, tokens),
+        functools.partial(flash_kernel, q_rows, tokens, first_block),
         grid_spec=pltpu.PrefetchScalarGridSpec(
             num_scalar_prefetch=2,
-            grid=(blocks, steps),
+            grid=(count, steps),
             in_specs=[
-                pl.BlockSpec((rows, head_size), lambda i, j, first, low: (i, 0)),
+                pl.BlockSpec((rows, head_size), lambda i, j, first, low: (i + first_block, 0)),
                 pl.BlockSpec((k_rows, head_size), kv_map),
                 pl.BlockSpec((k_rows, head_size), kv_map),
-                pl.BlockSpec((rows, 1), lambda i, j, first, low: (i, 0)),
+                pl.BlockSpec((rows, 1), lambda i, j, first, low: (i + first_block, 0)),
             ],
             out_specs=pl.BlockSpec((rows, head_size), lambda i, j, first, low: (i, 0)),
             scratch_shapes=[
@@ -113,13 +113,13 @@
                 pltpu.VMEM((rows, head_size), jnp.float32),
             ],
         ),
-        out_shape=jax.ShapeDtypeStruct((blocks * rows, head_size), jnp.bfloat16),
+        out_shape=jax.ShapeDtypeStruct((count * rows, head_size), jnp.bfloat16),
         compiler_params=pltpu.CompilerParams(dimension_semantics=("arbitrary", "arbitrary")),
     )(token_first.reshape(1), lowest, stacked, keys, values, starts)
     return (
-        out.reshape(blocks, heads, q_rows, head_size)
+        out.reshape(count, heads, q_rows, head_size)
         .transpose(0, 2, 1, 3)
-        .reshape(tokens, heads * head_size)
+        .reshape(count * q_rows, heads * head_size)
     )
 
 
@@ -167,15 +167,26 @@
     keyval = jnp.concatenate([key_rows, value_rows], axis=1)
     earlier = from_behind(keyval, "seq", 1)
     window = jnp.concatenate([earlier, keyval], axis=0)
-    attended = flash_attention(
-        queries, window[:, :head_size], window[:, head_size:], query_start, token_first
-    )
-    partial_term = lax.dot_general(
-        attended, w_output, (((1,), (1,)), ((), ())), preferred_element_type=jnp.float32
-    )
-    layer_out = lax.psum_scatter(
-        partial_term.astype(jnp.bfloat16), "mp", scatter_dimension=1, tiled=True
-    )
+    halves = 2
+    blocks_all = tok_rows // min(256, tok_rows)
+    outputs = []
+    for part in range(halves):
+        attended = flash_attention(
+            queries,
+            window[:, :head_size],
+            window[:, head_size:],
+            query_start,
+            token_first,
+            part * blocks_all // halves,
+            blocks_all // halves,
+        )
+        partial_term = lax.dot_general(
+            attended, w_output, (((1,), (1,)), ((), ())), preferred_element_type=jnp.float32
+        )
+        outputs.append(
+            lax.psum_scatter(partial_term.astype(jnp.bfloat16), "mp", scatter_dimension=1, tiled=True)
+        )
+    layer_out = jnp.concatenate(outputs, axis=0)
     pages_dev = tok_rows // PAGE
     share_width = 2 * head_size // ratio
     share_index = mp_index % ratio

time: 320 us -> 292 us (0.912)
  the two profiles are of different devices: /device:TPU:1 before, /device:TPU:120 now
where the time goes in v6:
time: 292 us; the launch traced here: 287 us
  starting transfers between devices  90.7 us (31%)
  Pallas kernels  69.5 us (24%)
  waiting for transfers between devices  37.5 us (13%)
  local copies, waits for them, and re-layouts  27.7 us (9%)
  other arithmetic  23.4 us (8%)
  matrix products  14.9 us (5%)
  between operations  14.2 us (5%)
  blocking collectives  9.26 us (3%)
    ppermute x15, starting transfers between devices, shift_round(): return lax.ppermute(x, axis, [(i, (i + by) % peers) for i in range(peers)])  88.2 us
    pallas_call x2, Pallas kernels, flash_attention(): pl.pallas_call(functools.partial(flash_kernel, q_rows, tokens, first_bloc...  69.5 us
    all_gather x1, waiting for transfers between devices, body(): lax.all_gather(jnp.concatenate([q_weight, kv_own], axis=1), 'seq', axis=0...  24 us
    psum x1, blocking collectives, body(): seg_total = lax.psum(seg_hist, 'seq')  9.26 us
    another operation x4, other arithmetic  8.5 us
    unnamed x26, local copies, waits for them, and re-layouts  8.24 us
    dot_general x2, matrix products, body(): lax.dot_general(attended, w_output, (((1,), (1,)), ((), ())), preferred_e...  7.78 us
    dot_general x1, matrix products, body(): jnp.dot(normed, w_inputs, preferred_element_type=jnp.float32)  6.64 us
  transfers between devices with their start and end apart: 20, of which 5 were waited for; matrix products, arithmetic and copies ran while one was open for 20% of the time, Pallas kernels for 24%

profile of v6, /device:TPU:120, one launch (start us, length us, event | category | flops | bytes accessed | tf_op | source)
XLA Modules:
  0.0 287.1 jit_solution(5531923958732089241)
XLA Ops:
  11.2 9.3 %psum.7 = s32[32]{0:T(128)S(1)} all-reduce(s32[32]{0:T(128)S(1)} %convert_reduce_fusion), channel_id=1, replica_groups=mesh['seq'=16,'mp'=8] {'seq'}, use_global_device_ids=true, to_apply=%region_1.2 | all-reduce | flops 32 | bytes 256 | tf_op jit(solution)/shard_map/psum | solution.py:149
  20.5 5.2 %fusion = f32[2048]{0:T(1024)S(1)} fusion(bf16[2048,2048]{1,0:T(8,128)(2,1)} %param.7), kind=kLoop, calls=%fused_computation.2 | loop fusion | flops 12580864 | bytes 8396800 | tf_op jit(solution)/shard_map/reduce_sum | solution.py:143
  26.8 5.3 %reshape.179.qs_ref = s32[8192,1]{1,0:T(8,128)} reshape(s32[8,4,256]{2,1,0:T(4,128)S(1)} %broadcast_in_dim.26) | data formatting | bytes 65536 | tf_op jit(solution)/shard_map/reshape | solution.py:91
  32.1 24.0 %all-gather.3.cloned.1.call-done = bf16[2048,384]{1,0:T(8,128)(2,1)} async-done(((bf16[128,384]{1,0:T(8,128)(2,1)}), bf16[2048,384]{1,0:T(8,128)(2,1)}) %all-gather.3.cloned.1.call-update) | async-done | bytes 1572880 | tf_op jit(solution)/shard_map/all_gather | solution.py:138
  56.1 6.6 %fusion.3 = f32[2048,384]{0,1:T(8,128)S(1)} fusion(bf16[2048,384]{1,0:T(8,128)(2,1)} %all-gather.3.cloned.1.call-done, bf16[2048,2048]{1,0:T(8,128)(2,1)} %param.7, f32[2048]{0:T(1024)S(1)} %copy-done.7, f32[2048]{0:T(1024)S(1)} %add_rsqrt_fusion), kind=kOutput, calls=%fused_computation.5 | convolution fusion | flops 3238002688 | bytes 13123584 | tf_op jit(solution)/shard_map/dot_general | solution.py:161
  64.8 2.3 copy.58
  67.0 2.3 copy.57
  69.3 8.0 %subtract_convert_fusion = (bf16[2048,32]{1,0:T(8,128)(2,1)}, bf16[2048,32]{1,0:T(8,128)(2,1)}, f32[2048,32]{1,0:T(8,128)}, f32[2048,32]{1,0:T(8,128)}) fusion(f32[2048,32]{1,0:T(8,128)} %copy.58, f32[2048,32]{1,0:T(8,128)} %copy.57, f32[2048]{0:T(1024)S(1)} %subtract_convert_fusion.2, f32[32]{0:T(128)S(1)} %multiply_exponential_fusion), kind=kLoop, calls=%fused_computation.33 | loop fusion | flops 589824 | bytes 1319040 | tf_op jit(solution)/shard_map/convert.2
  82.4 2.3 collective-permute-start
  87.4 6.6 %collective-permute-done = bf16[2048,128]{1,0:T(8,128)(2,1)} collective-permute-done((bf16[2048,128]{1,0:T(8,128)(2,1)S(1)}, bf16[2048,128]{1,0:T(8,128)(2,1)}, u32[]{:S(2)}, u32[]{:S(2)}) %collective-permute-start) | collective-permute-done | bytes 524320 | tf_op jit(solution)/shard_map/ppermute | solution.py:19
  97.2 40.0 %shard_map.87 = bf16[4096,64]{1,0:T(8,128)(2,1)} custom-call(s32[1]{0:T(128)} %bitcast.first_ref, s32[8]{0:T(128)} %reduce_min.8.lowest_ref, bf16[8192,64]{1,0:T(8,128)(2,1)} %bitcast.49, bf16[4096,64]{1,0:T(8,128)(2,1)} %get-tuple-element.17.k_ref, bf16[4096,64]{1,0:T(8,128)(2,1)} %get-tuple-element.16.v_ref, s32[8192,1]{1,0:T(8,128)} %reshape.179.qs_ref), custom_call_target="tpu_custom_call" | custom-call | tf_op jit(solution)/shard_map/pallas_call | solution.py:98
  139.0 4.5 %convolution_convert_fusion = bf16[1024,2048]{1,0:T(8,128)(2,1)} fusion(bf16[1024,256]{0,1:T(8,128)(2,1)S(1)} %bitcast.54, bf16[2048,256]{1,0:T(8,128)(2,1)} %all-gather.5.cloned.1.call-done), kind=kOutput, calls=%fused_computation.8 | convolution fusion | flops 1075838976 | bytes 5767168 | tf_op jit(solution)/shard_map/dot_general | solution.py:183
  143.5 29.5 %shard_map.86 = bf16[4096,64]{1,0:T(8,128)(2,1)} custom-call(s32[1]{0:T(128)} %bitcast.first_ref, s32[8]{0:T(128)} %reduce_min.8.lowest_ref, bf16[8192,64]{1,0:T(8,128)(2,1)} %bitcast.50, bf16[4096,64]{1,0:T(8,128)(2,1)} %get-tuple-element.17.k_ref, bf16[4096,64]{1,0:T(8,128)(2,1)} %get-tuple-element.16.v_ref, s32[8192,1]{1,0:T(8,128)} %reshape.179.qs_ref), custom_call_target="tpu_custom_call" | custom-call | tf_op jit(solution)/shard_map/pallas_call | solution.py:98
  174.7 3.3 %convolution_convert_fusion.1 = bf16[1024,2048]{1,0:T(8,128)(2,1)} fusion(bf16[1024,256]{0,1:T(8,128)(2,1)S(1)} %bitcast.55, bf16[2048,256]{1,0:T(8,128)(2,1)S(1)} %copy-done.5), kind=kOutput, calls=%fused_computation.9 | convolution fusion | flops 1075838976 | bytes 5767168 | tf_op jit(solution)/shard_map/dot_general | solution.py:183
  179.9 27.9 %collective-permute-start.13 = (bf16[1,65,128]{2,0,1:T(2,128)(2,1)S(1)}, bf16[1,65,128]{2,0,1:T(2,128)(2,1)S(1)}, u32[]{:S(2)}, u32[]{:S(2)}) collective-permute-start(bf16[1,65,128]{2,0,1:T(2,128)(2,1)S(1)} %get-tuple-element.30), channel_id=1, source_target_pairs={{0,104},{8,112},{16,120},{24,0},{32,8},{40,16},{48,24},{56,32},{64... | collective-permute-start | bytes 49928 | tf_op jit(solution)/shard_map/ppermute | solution.py:24
  207.8 6.7 %collective-permute-start.12 = (bf16[1,65,128]{2,0,1:T(2,128)(2,1)S(1)}, bf16[1,65,128]{2,0,1:T(2,128)(2,1)S(1)}, u32[]{:S(2)}, u32[]{:S(2)}) collective-permute-start(bf16[1,65,128]{2,0,1:T(2,128)(2,1)S(1)} %get-tuple-element.33), channel_id=1, source_target_pairs={{0,96},{8,104},{16,112},{24,120},{32,0},{40,8},{48,16},{56,24},{64... | collective-permute-start | bytes 49928 | tf_op jit(solution)/shard_map/ppermute | solution.py:24
  216.8 6.0 %collective-permute-start.4 = (bf16[1,65,128]{2,0,1:T(2,128)(2,1)S(1)}, bf16[1,65,128]{2,0,1:T(2,128)(2,1)S(1)}, u32[]{:S(2)}, u32[]{:S(2)}) collective-permute-start(bf16[1,65,128]{2,0,1:T(2,128)(2,1)S(1)} %get-tuple-element.23), channel_id=1, source_target_pairs={{0,32},{8,40},{16,48},{24,56},{32,64},{40,72},{48,80},{56,88},{64,... | collective-permute-start | bytes 49928 | tf_op jit(solution)/shard_map/ppermute | solution.py:24
  224.4 3.2 %collective-permute-start.6 = (bf16[1,65,128]{2,0,1:T(2,128)(2,1)S(1)}, bf16[1,65,128]{2,0,1:T(2,128)(2,1)S(1)}, u32[]{:S(2)}, u32[]{:S(2)}) collective-permute-start(bf16[1,65,128]{2,0,1:T(2,128)(2,1)S(1)} %get-tuple-element.26), channel_id=1, source_target_pairs={{0,48},{8,56},{16,64},{24,72},{32,80},{40,88},{48,96},{56,104},{64... | collective-permute-start | bytes 49928 | tf_op jit(solution)/shard_map/ppermute | solution.py:24
  227.6 31.2 %collective-permute-start.7 = (bf16[1,65,128]{2,0,1:T(2,128)(2,1)S(1)}, bf16[1,65,128]{2,0,1:T(2,128)(2,1)S(1)}, u32[]{:S(2)}, u32[]{:S(2)}) collective-permute-start(bf16[1,65,128]{2,0,1:T(2,128)(2,1)S(1)} %get-tuple-element.27), channel_id=1, source_target_pairs={{0,56},{8,64},{16,72},{24,80},{32,88},{40,96},{48,104},{56,112},{6... | collective-permute-start | bytes 49928 | tf_op jit(solution)/shard_map/ppermute | solution.py:24
  258.8 10.0 %collective-permute-start.8 = (bf16[1,65,128]{2,0,1:T(2,128)(2,1)S(1)}, bf16[1,65,128]{2,0,1:T(2,128)(2,1)S(1)}, u32[]{:S(2)}, u32[]{:S(2)}) collective-permute-start(bf16[1,65,128]{2,0,1:T(2,128)(2,1)S(1)} %get-tuple-element.28), channel_id=1, source_target_pairs={{0,64},{8,72},{16,80},{24,88},{32,96},{40,104},{48,112},{56,120},{... | collective-permute-start | bytes 49928 | tf_op jit(solution)/shard_map/ppermute | solution.py:24
  268.8 2.2 collective-permute-done.8
  271.0 3.5 %collective-permute-done.9 = bf16[1,65,128]{2,0,1:T(2,128)(2,1)S(1)} collective-permute-done((bf16[1,65,128]{2,0,1:T(2,128)(2,1)S(1)}, bf16[1,65,128]{2,0,1:T(2,128)(2,1)S(1)}, u32[]{:S(2)}, u32[]{:S(2)}) %collective-permute-start.9) | collective-permute-done | bytes 16672 | tf_op jit(solution)/shard_map/ppermute | solution.py:24
  274.5 2.6 concatenate.38
  278.4 2.2 pad_maximum_fusion
  (100 shorter events, 28.2 us)
Async XLA Ops:
  7.2 48.9 %all-gather.3.cloned.1.call-start = ((), (), s32[]{:S(2)}) async-start(), calls=%async_computation.2 | async-start | bytes 1671168 | tf_op jit(solution)/shard_map/all_gather | solution.py:138
  9.6 129.4 %all-gather.5.cloned.1.call-start = ((), (), s32[]{:S(2)}) async-start(), calls=%async_computation.3 | async-start | bytes 1114112 | tf_op jit(solution)/shard_map/all_gather | solution.py:141
  10.3 268.0 %reduce-scatter.5.cloned.1.call-start = ((), (), s32[]{:S(2)}) async-start(), calls=%async_computation.5 | async-start | bytes 4718592 | tf_op jit(solution)/shard_map/reduce_scatter | solution.py:187
  25.7 30.4 %copy-start.7 = (f32[2048]{0:T(1024)S(1)}, f32[2048]{0:T(1024)}, u32[]{:S(2)}) copy-start(f32[2048]{0:T(1024)} %param.8) | copy-start | bytes 24580
  82.4 11.6 %collective-permute-start = (bf16[2048,128]{1,0:T(8,128)(2,1)S(1)}, bf16[2048,128]{1,0:T(8,128)(2,1)}, u32[]{:S(2)}, u32[]{:S(2)}) collective-permute-start(bf16[2048,128]{1,0:T(8,128)(2,1)S(1)} %pad_maximum_fusion.1), channel_id=1, source_target_pairs={{0,8},{8,16},{16,24},{24,32},{32,40},{40,48},{48,56},{56,64},{64,7... | collective-permute-start | bytes 1572872 | tf_op jit(solution)/shard_map/ppermute | solution.py:19
  85.1 8.9 %copy-start.2 = (bf16[2048,64]{1,0:T(8,128)(2,1)S(1)}, bf16[2048,64]{1,0:T(8,128)(2,1)}, u32[]{:S(2)}) copy-start(bf16[2048,64]{1,0:T(8,128)(2,1)} %copy.59) | copy-start | bytes 786436
  85.1 8.9 %copy-start.3 = (bf16[2048,32]{1,0:T(8,128)(2,1)S(1)}, bf16[2048,32]{1,0:T(8,128)(2,1)}, u32[]{:S(2)}) copy-start(bf16[2048,32]{1,0:T(8,128)(2,1)} %get-tuple-element.14) | copy-start | bytes 393220
  143.5 31.2 %copy-start.5 = (bf16[2048,256]{1,0:T(8,128)(2,1)S(1)}, bf16[2048,256]{1,0:T(8,128)(2,1)}, u32[]{:S(2)}) copy-start(bf16[2048,256]{1,0:T(8,128)(2,1)} %all-gather.5.cloned.1.call-done) | copy-start | bytes 3145732
  143.5 134.9 %reduce-scatter.3.cloned.1.call-start = ((), (), s32[]{:S(2)}) async-start(), calls=%async_computation.4 | async-start | bytes 4718592 | tf_op jit(solution)/shard_map/reduce_scatter | solution.py:187
  179.9 35.7 %collective-permute-start.13 = (bf16[1,65,128]{2,0,1:T(2,128)(2,1)S(1)}, bf16[1,65,128]{2,0,1:T(2,128)(2,1)S(1)}, u32[]{:S(2)}, u32[]{:S(2)}) collective-permute-start(bf16[1,65,128]{2,0,1:T(2,128)(2,1)S(1)} %get-tuple-element.30), channel_id=1, source_target_pairs={{0,104},{8,112},{16,120},{24,0},{32,8},{40,16},{48,24},{56,32},{64... | collective-permute-start | bytes 49928 | tf_op jit(solution)/shard_map/ppermute | solution.py:24
  207.8 7.9 %collective-permute-start.10 = (bf16[1,65,128]{2,0,1:T(2,128)(2,1)S(1)}, bf16[1,65,128]{2,0,1:T(2,128)(2,1)S(1)}, u32[]{:S(2)}, u32[]{:S(2)}) collective-permute-start(bf16[1,65,128]{2,0,1:T(2,128)(2,1)S(1)} %get-tuple-element.31), channel_id=1, source_target_pairs={{0,80},{8,88},{16,96},{24,104},{32,112},{40,120},{48,0},{56,8},{64... | collective-permute-start | bytes 49928 | tf_op jit(solution)/shard_map/ppermute | solution.py:24
  207.8 8.0 %collective-permute-start.11 = (bf16[1,65,128]{2,0,1:T(2,128)(2,1)S(1)}, bf16[1,65,128]{2,0,1:T(2,128)(2,1)S(1)}, u32[]{:S(2)}, u32[]{:S(2)}) collective-permute-start(bf16[1,65,128]{2,0,1:T(2,128)(2,1)S(1)} %get-tuple-element.32), channel_id=1, source_target_pairs={{0,88},{8,96},{16,104},{24,112},{32,120},{40,0},{48,8},{56,16},{64... | collective-permute-start | bytes 49928 | tf_op jit(solution)/shard_map/ppermute | solution.py:24
  207.8 9.0 %collective-permute-start.12 = (bf16[1,65,128]{2,0,1:T(2,128)(2,1)S(1)}, bf16[1,65,128]{2,0,1:T(2,128)(2,1)S(1)}, u32[]{:S(2)}, u32[]{:S(2)}) collective-permute-start(bf16[1,65,128]{2,0,1:T(2,128)(2,1)S(1)} %get-tuple-element.33), channel_id=1, source_target_pairs={{0,96},{8,104},{16,112},{24,120},{32,0},{40,8},{48,16},{56,24},{64... | collective-permute-start | bytes 49928 | tf_op jit(solution)/shard_map/ppermute | solution.py:24
  214.7 8.2 %collective-permute-start.15 = (bf16[1,65,128]{2,0,1:T(2,128)(2,1)S(1)}, bf16[1,65,128]{2,0,1:T(2,128)(2,1)S(1)}, u32[]{:S(2)}, u32[]{:S(2)}) collective-permute-start(bf16[1,65,128]{2,0,1:T(2,128)(2,1)S(1)} %get-tuple-element.18), channel_id=1, source_target_pairs={{0,120},{8,0},{16,8},{24,16},{32,24},{40,32},{48,40},{56,48},{64,5... | collective-permute-start | bytes 49928 | tf_op jit(solution)/shard_map/ppermute | solution.py:24
  215.6 7.2 %collective-permute-start.1 = (bf16[1,65,128]{2,0,1:T(2,128)(2,1)S(1)}, bf16[1,65,128]{2,0,1:T(2,128)(2,1)S(1)}, u32[]{:S(2)}, u32[]{:S(2)}) collective-permute-start(bf16[1,65,128]{2,0,1:T(2,128)(2,1)S(1)} %get-tuple-element.20), channel_id=1, source_target_pairs={{0,8},{8,16},{16,24},{24,32},{32,40},{40,48},{48,56},{56,64},{64,7... | collective-permute-start | bytes 49928 | tf_op jit(solution)/shard_map/ppermute | solution.py:24
  215.7 8.7 %collective-permute-start.2 = (bf16[1,65,128]{2,0,1:T(2,128)(2,1)S(1)}, bf16[1,65,128]{2,0,1:T(2,128)(2,1)S(1)}, u32[]{:S(2)}, u32[]{:S(2)}) collective-permute-start(bf16[1,65,128]{2,0,1:T(2,128)(2,1)S(1)} %get-tuple-element.21), channel_id=1, source_target_pairs={{0,16},{8,24},{16,32},{24,40},{32,48},{40,56},{48,64},{56,72},{64,... | collective-permute-start | bytes 49928 | tf_op jit(solution)/shard_map/ppermute | solution.py:24
  215.8 11.9 %collective-permute-start.3 = (bf16[1,65,128]{2,0,1:T(2,128)(2,1)S(1)}, bf16[1,65,128]{2,0,1:T(2,128)(2,1)S(1)}, u32[]{:S(2)}, u32[]{:S(2)}) collective-permute-start(bf16[1,65,128]{2,0,1:T(2,128)(2,1)S(1)} %get-tuple-element.22), channel_id=1, source_target_pairs={{0,24},{8,32},{16,40},{24,48},{32,56},{40,64},{48,72},{56,80},{64,... | collective-permute-start | bytes 49928 | tf_op jit(solution)/shard_map/ppermute | solution.py:24
  216.8 42.0 %collective-permute-start.4 = (bf16[1,65,128]{2,0,1:T(2,128)(2,1)S(1)}, bf16[1,65,128]{2,0,1:T(2,128)(2,1)S(1)}, u32[]{:S(2)}, u32[]{:S(2)}) collective-permute-start(bf16[1,65,128]{2,0,1:T(2,128)(2,1)S(1)} %get-tuple-element.23), channel_id=1, source_target_pairs={{0,32},{8,40},{16,48},{24,56},{32,64},{40,72},{48,80},{56,88},{64,... | collective-permute-start | bytes 49928 | tf_op jit(solution)/shard_map/ppermute | solution.py:24
  222.8 46.0 %collective-permute-start.14 = (bf16[1,65,128]{2,0,1:T(2,128)(2,1)S(1)}, bf16[1,65,128]{2,0,1:T(2,128)(2,1)S(1)}, u32[]{:S(2)}, u32[]{:S(2)}) collective-permute-start(bf16[1,65,128]{2,0,1:T(2,128)(2,1)S(1)} %get-tuple-element.24), channel_id=1, source_target_pairs={{0,112},{8,120},{16,0},{24,8},{32,16},{40,24},{48,32},{56,40},{64,... | collective-permute-start | bytes 49928 | tf_op jit(solution)/shard_map/ppermute | solution.py:24
  222.8 46.0 %collective-permute-start.5 = (bf16[1,65,128]{2,0,1:T(2,128)(2,1)S(1)}, bf16[1,65,128]{2,0,1:T(2,128)(2,1)S(1)}, u32[]{:S(2)}, u32[]{:S(2)}) collective-permute-start(bf16[1,65,128]{2,0,1:T(2,128)(2,1)S(1)} %get-tuple-element.25), channel_id=1, source_target_pairs={{0,40},{8,48},{16,56},{24,64},{32,72},{40,80},{48,88},{56,96},{64,... | collective-permute-start | bytes 49928 | tf_op jit(solution)/shard_map/ppermute | solution.py:24
  224.4 44.4 %collective-permute-start.6 = (bf16[1,65,128]{2,0,1:T(2,128)(2,1)S(1)}, bf16[1,65,128]{2,0,1:T(2,128)(2,1)S(1)}, u32[]{:S(2)}, u32[]{:S(2)}) collective-permute-start(bf16[1,65,128]{2,0,1:T(2,128)(2,1)S(1)} %get-tuple-element.26), channel_id=1, source_target_pairs={{0,48},{8,56},{16,64},{24,72},{32,80},{40,88},{48,96},{56,104},{64... | collective-permute-start | bytes 49928 | tf_op jit(solution)/shard_map/ppermute | solution.py:24
  227.6 41.2 %collective-permute-start.7 = (bf16[1,65,128]{2,0,1:T(2,128)(2,1)S(1)}, bf16[1,65,128]{2,0,1:T(2,128)(2,1)S(1)}, u32[]{:S(2)}, u32[]{:S(2)}) collective-permute-start(bf16[1,65,128]{2,0,1:T(2,128)(2,1)S(1)} %get-tuple-element.27), channel_id=1, source_target_pairs={{0,56},{8,64},{16,72},{24,80},{32,88},{40,96},{48,104},{56,112},{6... | collective-permute-start | bytes 49928 | tf_op jit(solution)/shard_map/ppermute | solution.py:24
  258.8 12.2 %collective-permute-start.8 = (bf16[1,65,128]{2,0,1:T(2,128)(2,1)S(1)}, bf16[1,65,128]{2,0,1:T(2,128)(2,1)S(1)}, u32[]{:S(2)}, u32[]{:S(2)}) collective-permute-start(bf16[1,65,128]{2,0,1:T(2,128)(2,1)S(1)} %get-tuple-element.28), channel_id=1, source_target_pairs={{0,64},{8,72},{16,80},{24,88},{32,96},{40,104},{48,112},{56,120},{... | collective-permute-start | bytes 49928 | tf_op jit(solution)/shard_map/ppermute | solution.py:24
  268.8 5.7 %collective-permute-start.9 = (bf16[1,65,128]{2,0,1:T(2,128)(2,1)S(1)}, bf16[1,65,128]{2,0,1:T(2,128)(2,1)S(1)}, u32[]{:S(2)}, u32[]{:S(2)}) collective-permute-start(bf16[1,65,128]{2,0,1:T(2,128)(2,1)S(1)} %get-tuple-element.29), channel_id=1, source_target_pairs={{0,72},{8,80},{16,88},{24,96},{32,104},{40,112},{48,120},{56,0},{6... | collective-permute-start | bytes 49928 | tf_op jit(solution)/shard_map/ppermute | solution.py:24
  (6 other events, 30.0 us)
Sparse Core Ops, SparseCore 0:
  11.0 45.0 all-gather.2
  58.6 45.3 all-gather.4
  143.6 61.3 reduce-scatter.4
  207.3 52.2 reduce-scatter.2

commit v7 on v6

--- a/solution.py
+++ b/solution.py
@@ -34,8 +34,8 @@
     )
 
 
-def flash_kernel(q_rows, tokens, first_block, first_ref, lowest_ref, q_ref, k_ref, v_ref, qs_ref, o_ref, m_sc, l_sc, acc_sc):
-    block = pl.program_id(0) + first_block
+def flash_kernel(q_rows, tokens, first_ref, lowest_ref, q_ref, k_ref, v_ref, qs_ref, o_ref, m_sc, l_sc, acc_sc):
+    block = pl.program_id(0) + first_ref[1]
     step = pl.program_id(1)
     rows = q_ref.shape[0]
     k_rows = k_ref.shape[0]
@@ -93,18 +93,18 @@
     rows = heads * q_rows
 
     def kv_map(i, j, first, low):
-        return ((i + first_block) * q_rows // k_rows + j, 0)
+        return ((i + first[1]) * q_rows // k_rows + j, 0)
 
     out = pl.pallas_call(
-        functools.partial(flash_kernel, q_rows, tokens, first_block),
+        functools.partial(flash_kernel, q_rows, tokens),
         grid_spec=pltpu.PrefetchScalarGridSpec(
             num_scalar_prefetch=2,
             grid=(count, steps),
             in_specs=[
-                pl.BlockSpec((rows, head_size), lambda i, j, first, low: (i + first_block, 0)),
+                pl.BlockSpec((rows, head_size), lambda i, j, first, low: (i + first[1], 0)),
                 pl.BlockSpec((k_rows, head_size), kv_map),
                 pl.BlockSpec((k_rows, head_size), kv_map),
-                pl.BlockSpec((rows, 1), lambda i, j, first, low: (i + first_block, 0)),
+                pl.BlockSpec((rows, 1), lambda i, j, first, low: (i + first[1], 0)),
             ],
             out_specs=pl.BlockSpec((rows, head_size), lambda i, j, first, low: (i, 0)),
             scratch_shapes=[
@@ -115,7 +115,7 @@
         ),
         out_shape=jax.ShapeDtypeStruct((count * rows, head_size), jnp.bfloat16),
         compiler_params=pltpu.CompilerParams(dimension_semantics=("arbitrary", "arbitrary")),
-    )(token_first.reshape(1), lowest, stacked, keys, values, starts)
+    )(jnp.stack([token_first, jnp.int32(first_block)]), lowest, stacked, keys, values, starts)
     return (
         out.reshape(count, heads, q_rows, head_size)
         .transpose(0, 2, 1, 3)
@@ -167,7 +167,7 @@
     keyval = jnp.concatenate([key_rows, value_rows], axis=1)
     earlier = from_behind(keyval, "seq", 1)
     window = jnp.concatenate([earlier, keyval], axis=0)
-    halves = 2
+    halves = 4
     blocks_all = tok_rows // min(256, tok_rows)
     outputs = []
     for part in range(halves):

time: 292 us -> 317 us (1.086)
  the two profiles are of different devices: /device:TPU:120 before, /device:TPU:1 now
where the time goes in v7:
time: 317 us; the launch traced here: 312 us
  Pallas kernels  87.4 us (28%)
  waiting for transfers between devices  77.7 us (25%)
  starting transfers between devices  49.1 us (15%)
  local copies, waits for them, and re-layouts  29.9 us (9%)
  other arithmetic  22.7 us (7%)
  matrix products  16.8 us (5%)
  between operations  14.5 us (5%)
  blocking collectives  13.7 us (4%)
    pallas_call x4, Pallas kernels, flash_attention(): pl.pallas_call(functools.partial(flash_kernel, q_rows, tokens), grid_spec...  87.4 us
    reduce_scatter x4, waiting for transfers between devices, body(): lax.psum_scatter(partial_term.astype(jnp.bfloat16), 'mp', scatter_dimensi...  45.5 us
    ppermute x15, starting transfers between devices, shift_round(): return lax.ppermute(x, axis, [(i, (i + by) % peers) for i in range(peers)])  45.4 us
    all_gather x1, waiting for transfers between devices, body(): lax.all_gather(jnp.concatenate([q_weight, kv_own], axis=1), 'seq', axis=0...  23.7 us
    psum x1, blocking collectives, body(): seg_total = lax.psum(seg_hist, 'seq')  13.7 us
    dot_general x4, matrix products, body(): lax.dot_general(attended, w_output, (((1,), (1,)), ((), ())), preferred_e...  9.65 us
    dot_general x1, matrix products, body(): jnp.dot(normed, w_inputs, preferred_element_type=jnp.float32)  6.64 us
    unnamed x28, local copies, waits for them, and re-layouts  6.44 us
  transfers between devices with their start and end apart: 22, of which 6 were waited for; matrix products, arithmetic and copies ran while one was open for 19% of the time, Pallas kernels for 28%

profile of v7, /device:TPU:1, one launch (start us, length us, event | category | flops | bytes accessed | tf_op | source)
XLA Modules:
  0.0 311.7 jit_solution(4167413465849883953)
XLA Ops:
  11.2 13.7 %psum.7 = s32[32]{0:T(128)S(1)} all-reduce(s32[32]{0:T(128)S(1)} %convert_reduce_fusion), channel_id=1, replica_groups=mesh['seq'=16,'mp'=8] {'seq'}, use_global_device_ids=true, to_apply=%region_1.2 | all-reduce | flops 32 | bytes 256 | tf_op jit(solution)/shard_map/psum | solution.py:149
  25.0 5.1 %fusion = f32[2048]{0:T(1024)S(1)} fusion(bf16[2048,2048]{1,0:T(8,128)(2,1)} %param.7), kind=kLoop, calls=%fused_computation.2 | loop fusion | flops 12580864 | bytes 8396800 | tf_op jit(solution)/shard_map/reduce_sum | solution.py:143
  31.2 5.3 %reshape.200.qs_ref = s32[8192,1]{1,0:T(8,128)} reshape(s32[8,4,256]{2,1,0:T(4,128)S(1)} %broadcast_in_dim.26) | data formatting | bytes 65536 | tf_op jit(solution)/shard_map/reshape | solution.py:91
  37.1 23.7 %all-gather.3.cloned.1.call-done = bf16[2048,384]{1,0:T(8,128)(2,1)} async-done(((bf16[128,384]{1,0:T(8,128)(2,1)}), bf16[2048,384]{1,0:T(8,128)(2,1)}) %all-gather.3.cloned.1.call-update) | async-done | bytes 1572880 | tf_op jit(solution)/shard_map/all_gather | solution.py:138
  60.8 6.6 %fusion.3 = f32[2048,384]{0,1:T(8,128)S(1)} fusion(bf16[2048,384]{1,0:T(8,128)(2,1)} %all-gather.3.cloned.1.call-done, bf16[2048,2048]{1,0:T(8,128)(2,1)} %param.7, f32[2048]{0:T(1024)S(1)} %copy-done.7, f32[2048]{0:T(1024)S(1)} %add_rsqrt_fusion), kind=kOutput, calls=%fused_computation.5 | convolution fusion | flops 3238002688 | bytes 13123584 | tf_op jit(solution)/shard_map/dot_general | solution.py:161
  72.8 5.6 %subtract_convert_fusion = (bf16[2048,32]{1,0:T(8,128)(2,1)S(1)}, bf16[2048,32]{1,0:T(8,128)(2,1)}, f32[2048,32]{1,0:T(8,128)}, f32[2048,32]{1,0:T(8,128)}) fusion(f32[2048,32]{1,0:T(8,128)S(1)} %copy.70, f32[2048,32]{1,0:T(8,128)S(1)} %copy.69, f32[2048]{0:T(1024)S(1)} %subtract_convert_fusion.2, f32[32]{0:T(128)S(1)} %multiply_exponential_fusion), kind=kLoop, calls=%fused_computation.35 | loop fusion | flops 589824 | bytes 1319040 | tf_op jit(solution)/shard_map/convert.2
  80.1 2.3 copy.52
  82.3 2.4 pad_maximum_fusion.1
  84.7 3.2 %collective-permute-start = (bf16[2048,128]{1,0:T(8,128)(2,1)}, bf16[2048,128]{1,0:T(8,128)(2,1)}, u32[]{:S(2)}, u32[]{:S(2)}) collective-permute-start(bf16[2048,128]{1,0:T(8,128)(2,1)} %pad_maximum_fusion.1), channel_id=1, source_target_pairs={{0,8},{8,16},{16,24},{24,32},{32,40},{40,48},{48,56},{56,64},{64,7... | collective-permute-start | bytes 1572872 | tf_op jit(solution)/shard_map/ppermute | solution.py:19
  90.7 4.2 %collective-permute-done = bf16[2048,128]{1,0:T(8,128)(2,1)} collective-permute-done((bf16[2048,128]{1,0:T(8,128)(2,1)}, bf16[2048,128]{1,0:T(8,128)(2,1)}, u32[]{:S(2)}, u32[]{:S(2)}) %collective-permute-start) | collective-permute-done | bytes 524320 | tf_op jit(solution)/shard_map/ppermute | solution.py:19
  98.1 26.1 %shard_map.87 = bf16[2048,64]{1,0:T(8,128)(2,1)} custom-call(s32[2]{0:T(128)} %get-tuple-element.39.first_ref, s32[8]{0:T(128)} %reduce_min.8.lowest_ref, bf16[8192,64]{1,0:T(8,128)(2,1)} %bitcast.67, bf16[4096,64]{1,0:T(8,128)(2,1)} %get-tuple-element.17.k_ref, bf16[4096,64]{1,0:T(8,128)(2,1)} %get-tuple-element.16.v_ref, s32[8192,1]{1,0:T(8,128)} %reshape.200.qs_ref), custom_call_target="tpu_custom_call" | custom-call | tf_op jit(solution)/shard_map/pallas_call | solution.py:98
  125.6 3.3 %convolution_convert_fusion.2 = bf16[512,2048]{1,0:T(8,128)(2,1)} fusion(bf16[512,256]{0,1:T(8,128)(2,1)S(1)} %bitcast.85, bf16[2048,256]{1,0:T(8,128)(2,1)} %all-gather.5.cloned.1.call-done), kind=kOutput, calls=%fused_computation.10 | convolution fusion | flops 537919488 | bytes 3407872 | tf_op jit(solution)/shard_map/dot_general | solution.py:183
  129.0 26.3 %shard_map.86 = bf16[2048,64]{1,0:T(8,128)(2,1)} custom-call(s32[2]{0:T(128)} %get-tuple-element.38.first_ref, s32[8]{0:T(128)} %reduce_min.8.lowest_ref, bf16[8192,64]{1,0:T(8,128)(2,1)} %bitcast.68, bf16[4096,64]{1,0:T(8,128)(2,1)} %get-tuple-element.17.k_ref, bf16[4096,64]{1,0:T(8,128)(2,1)} %get-tuple-element.16.v_ref, s32[8192,1]{1,0:T(8,128)} %reshape.200.qs_ref), custom_call_target="tpu_custom_call" | custom-call | tf_op jit(solution)/shard_map/pallas_call | solution.py:98
  159.7 15.5 %shard_map.88 = bf16[2048,64]{1,0:T(8,128)(2,1)} custom-call(s32[2]{0:T(128)} %get-tuple-element.40.first_ref, s32[8]{0:T(128)} %reduce_min.8.lowest_ref, bf16[8192,64]{1,0:T(8,128)(2,1)} %bitcast.69, bf16[4096,64]{1,0:T(8,128)(2,1)} %get-tuple-element.17.k_ref, bf16[4096,64]{1,0:T(8,128)(2,1)} %get-tuple-element.16.v_ref, s32[8192,1]{1,0:T(8,128)} %reshape.200.qs_ref), custom_call_target="tpu_custom_call" | custom-call | tf_op jit(solution)/shard_map/pallas_call | solution.py:98
  178.7 19.5 %shard_map.89 = bf16[2048,64]{1,0:T(8,128)(2,1)} custom-call(s32[2]{0:T(128)} %get-tuple-element.41.first_ref, s32[8]{0:T(128)} %reduce_min.8.lowest_ref, bf16[8192,64]{1,0:T(8,128)(2,1)} %bitcast.70, bf16[4096,64]{1,0:T(8,128)(2,1)} %get-tuple-element.17.k_ref, bf16[4096,64]{1,0:T(8,128)(2,1)} %get-tuple-element.16.v_ref, s32[8192,1]{1,0:T(8,128)} %reshape.200.qs_ref), custom_call_target="tpu_custom_call" | custom-call | tf_op jit(solution)/shard_map/pallas_call | solution.py:98
  204.0 22.3 %collective-permute-start.10 = (bf16[1,65,128]{2,0,1:T(2,128)(2,1)S(1)}, bf16[1,65,128]{2,0,1:T(2,128)(2,1)S(1)}, u32[]{:S(2)}, u32[]{:S(2)}) collective-permute-start(bf16[1,65,128]{2,0,1:T(2,128)(2,1)S(1)} %get-tuple-element.31), channel_id=1, source_target_pairs={{0,80},{8,88},{16,96},{24,104},{32,112},{40,120},{48,0},{56,8},{64... | collective-permute-start | bytes 49928 | tf_op jit(solution)/shard_map/ppermute | solution.py:24
  231.0 2.3 collective-permute-start.3
  233.3 4.7 %collective-permute-start.4 = (bf16[1,65,128]{2,0,1:T(2,128)(2,1)S(1)}, bf16[1,65,128]{2,0,1:T(2,128)(2,1)S(1)}, u32[]{:S(2)}, u32[]{:S(2)}) collective-permute-start(bf16[1,65,128]{2,0,1:T(2,128)(2,1)S(1)} %get-tuple-element.23), channel_id=1, source_target_pairs={{0,32},{8,40},{16,48},{24,56},{32,64},{40,72},{48,80},{56,88},{64,... | collective-permute-start | bytes 49928 | tf_op jit(solution)/shard_map/ppermute | solution.py:24
  238.0 4.5 %collective-permute-start.14 = (bf16[1,65,128]{2,0,1:T(2,128)(2,1)S(1)}, bf16[1,65,128]{2,0,1:T(2,128)(2,1)S(1)}, u32[]{:S(2)}, u32[]{:S(2)}) collective-permute-start(bf16[1,65,128]{2,0,1:T(2,128)(2,1)S(1)} %get-tuple-element.24), channel_id=1, source_target_pairs={{0,112},{8,120},{16,0},{24,8},{32,16},{40,24},{48,32},{56,40},{64,... | collective-permute-start | bytes 49928 | tf_op jit(solution)/shard_map/ppermute | solution.py:24
  242.6 2.6 collective-permute-start.7
  246.4 3.6 %collective-permute-start.9 = (bf16[1,65,128]{2,0,1:T(2,128)(2,1)S(1)}, bf16[1,65,128]{2,0,1:T(2,128)(2,1)S(1)}, u32[]{:S(2)}, u32[]{:S(2)}) collective-permute-start(bf16[1,65,128]{2,0,1:T(2,128)(2,1)S(1)} %get-tuple-element.29), channel_id=1, source_target_pairs={{0,72},{8,80},{16,88},{24,96},{32,104},{40,112},{48,120},{56,0},{6... | collective-permute-start | bytes 49928 | tf_op jit(solution)/shard_map/ppermute | solution.py:24
  250.0 3.2 %collective-permute-done.5 = bf16[1,65,128]{2,0,1:T(2,128)(2,1)S(1)} collective-permute-done((bf16[1,65,128]{2,0,1:T(2,128)(2,1)S(1)}, bf16[1,65,128]{2,0,1:T(2,128)(2,1)S(1)}, u32[]{:S(2)}, u32[]{:S(2)}) %collective-permute-start.5) | collective-permute-done | bytes 16672 | tf_op jit(solution)/shard_map/ppermute | solution.py:24
  253.3 2.7 concatenate.38
  258.3 44.4 %reduce-scatter.11.cloned.1.call-done = bf16[512,256]{1,0:T(8,128)(2,1)} async-done(((bf16[512,2048]{1,0:T(8,128)(2,1)}), bf16[512,256]{1,0:T(8,128)(2,1)}) %reduce-scatter.11.cloned.1.call-update) | async-done | bytes 262160 | tf_op jit(solution)/shard_map/reduce_scatter | solution.py:187
  (116 shorter events, 44.1 us)
Async XLA Ops:
  7.2 53.6 %all-gather.3.cloned.1.call-start = ((), (), s32[]{:S(2)}) async-start(), calls=%async_computation.4 | async-start | bytes 1671168 | tf_op jit(solution)/shard_map/all_gather | solution.py:138
  9.6 116.0 %all-gather.5.cloned.1.call-start = ((), (), s32[]{:S(2)}) async-start(), calls=%async_computation.5 | async-start | bytes 1114112 | tf_op jit(solution)/shard_map/all_gather | solution.py:141
  10.3 246.8 %reduce-scatter.7.cloned.1.call-start = ((), (), s32[]{:S(2)}) async-start(), calls=%async_computation.7 | async-start | bytes 2359296 | tf_op jit(solution)/shard_map/reduce_scatter | solution.py:187
  31.2 29.6 %copy-start.7 = (f32[2048]{0:T(1024)S(1)}, f32[2048]{0:T(1024)}, u32[]{:S(2)}) copy-start(f32[2048]{0:T(1024)} %param.8) | copy-start | bytes 24580
  84.7 10.2 %collective-permute-start = (bf16[2048,128]{1,0:T(8,128)(2,1)}, bf16[2048,128]{1,0:T(8,128)(2,1)}, u32[]{:S(2)}, u32[]{:S(2)}) collective-permute-start(bf16[2048,128]{1,0:T(8,128)(2,1)} %pad_maximum_fusion.1), channel_id=1, source_target_pairs={{0,8},{8,16},{16,24},{24,32},{32,40},{40,48},{48,56},{56,64},{64,7... | collective-permute-start | bytes 1572872 | tf_op jit(solution)/shard_map/ppermute | solution.py:19
  129.0 128.2 %reduce-scatter.5.cloned.1.call-start = ((), (), s32[]{:S(2)}) async-start(), calls=%async_computation.6 | async-start | bytes 2359296 | tf_op jit(solution)/shard_map/reduce_scatter | solution.py:187
  129.0 27.6 %copy-start.1 = (bf16[2048,256]{1,0:T(8,128)(2,1)S(1)}, bf16[2048,256]{1,0:T(8,128)(2,1)}, u32[]{:S(2)}) copy-start(bf16[2048,256]{1,0:T(8,128)(2,1)} %all-gather.5.cloned.1.call-done) | copy-start | bytes 3145732
  158.8 99.5 %reduce-scatter.9.cloned.1.call-start = ((), (), s32[]{:S(2)}) async-start(), calls=%async_computation.8 | async-start | bytes 2359296 | tf_op jit(solution)/shard_map/reduce_scatter | solution.py:187
  178.6 124.1 %reduce-scatter.11.cloned.1.call-start = ((), (), s32[]{:S(2)}) async-start(), calls=%async_computation.9 | async-start | bytes 2359296 | tf_op jit(solution)/shard_map/reduce_scatter | solution.py:187
  203.9 24.5 %collective-permute-start.13 = (bf16[1,65,128]{2,0,1:T(2,128)(2,1)S(1)}, bf16[1,65,128]{2,0,1:T(2,128)(2,1)S(1)}, u32[]{:S(2)}, u32[]{:S(2)}) collective-permute-start(bf16[1,65,128]{2,0,1:T(2,128)(2,1)S(1)} %get-tuple-element.30), channel_id=1, source_target_pairs={{0,104},{8,112},{16,120},{24,0},{32,8},{40,16},{48,24},{56,32},{64... | collective-permute-start | bytes 49928 | tf_op jit(solution)/shard_map/ppermute | solution.py:24
  204.0 26.2 %collective-permute-start.10 = (bf16[1,65,128]{2,0,1:T(2,128)(2,1)S(1)}, bf16[1,65,128]{2,0,1:T(2,128)(2,1)S(1)}, u32[]{:S(2)}, u32[]{:S(2)}) collective-permute-start(bf16[1,65,128]{2,0,1:T(2,128)(2,1)S(1)} %get-tuple-element.31), channel_id=1, source_target_pairs={{0,80},{8,88},{16,96},{24,104},{32,112},{40,120},{48,0},{56,8},{64... | collective-permute-start | bytes 49928 | tf_op jit(solution)/shard_map/ppermute | solution.py:24
  226.3 4.6 %collective-permute-start.11 = (bf16[1,65,128]{2,0,1:T(2,128)(2,1)S(1)}, bf16[1,65,128]{2,0,1:T(2,128)(2,1)S(1)}, u32[]{:S(2)}, u32[]{:S(2)}) collective-permute-start(bf16[1,65,128]{2,0,1:T(2,128)(2,1)S(1)} %get-tuple-element.32), channel_id=1, source_target_pairs={{0,88},{8,96},{16,104},{24,112},{32,120},{40,0},{48,8},{56,16},{64... | collective-permute-start | bytes 49928 | tf_op jit(solution)/shard_map/ppermute | solution.py:24
  226.4 6.9 %collective-permute-start.12 = (bf16[1,65,128]{2,0,1:T(2,128)(2,1)S(1)}, bf16[1,65,128]{2,0,1:T(2,128)(2,1)S(1)}, u32[]{:S(2)}, u32[]{:S(2)}) collective-permute-start(bf16[1,65,128]{2,0,1:T(2,128)(2,1)S(1)} %get-tuple-element.33), channel_id=1, source_target_pairs={{0,96},{8,104},{16,112},{24,120},{32,0},{40,8},{48,16},{56,24},{64... | collective-permute-start | bytes 49928 | tf_op jit(solution)/shard_map/ppermute | solution.py:24
  228.2 9.8 %collective-permute-start.15 = (bf16[1,65,128]{2,0,1:T(2,128)(2,1)S(1)}, bf16[1,65,128]{2,0,1:T(2,128)(2,1)S(1)}, u32[]{:S(2)}, u32[]{:S(2)}) collective-permute-start(bf16[1,65,128]{2,0,1:T(2,128)(2,1)S(1)} %get-tuple-element.18), channel_id=1, source_target_pairs={{0,120},{8,0},{16,8},{24,16},{32,24},{40,32},{48,40},{56,48},{64,5... | collective-permute-start | bytes 49928 | tf_op jit(solution)/shard_map/ppermute | solution.py:24
  228.4 14.0 %collective-permute-start.1 = (bf16[1,65,128]{2,0,1:T(2,128)(2,1)S(1)}, bf16[1,65,128]{2,0,1:T(2,128)(2,1)S(1)}, u32[]{:S(2)}, u32[]{:S(2)}) collective-permute-start(bf16[1,65,128]{2,0,1:T(2,128)(2,1)S(1)} %get-tuple-element.20), channel_id=1, source_target_pairs={{0,8},{8,16},{16,24},{24,32},{32,40},{40,48},{48,56},{56,64},{64,7... | collective-permute-start | bytes 49928 | tf_op jit(solution)/shard_map/ppermute | solution.py:24
  230.2 12.3 %collective-permute-start.2 = (bf16[1,65,128]{2,0,1:T(2,128)(2,1)S(1)}, bf16[1,65,128]{2,0,1:T(2,128)(2,1)S(1)}, u32[]{:S(2)}, u32[]{:S(2)}) collective-permute-start(bf16[1,65,128]{2,0,1:T(2,128)(2,1)S(1)} %get-tuple-element.21), channel_id=1, source_target_pairs={{0,16},{8,24},{16,32},{24,40},{32,48},{40,56},{48,64},{56,72},{64,... | collective-permute-start | bytes 49928 | tf_op jit(solution)/shard_map/ppermute | solution.py:24
  231.0 11.6 %collective-permute-start.3 = (bf16[1,65,128]{2,0,1:T(2,128)(2,1)S(1)}, bf16[1,65,128]{2,0,1:T(2,128)(2,1)S(1)}, u32[]{:S(2)}, u32[]{:S(2)}) collective-permute-start(bf16[1,65,128]{2,0,1:T(2,128)(2,1)S(1)} %get-tuple-element.22), channel_id=1, source_target_pairs={{0,24},{8,32},{16,40},{24,48},{32,56},{40,64},{48,72},{56,80},{64,... | collective-permute-start | bytes 49928 | tf_op jit(solution)/shard_map/ppermute | solution.py:24
  233.3 12.0 %collective-permute-start.4 = (bf16[1,65,128]{2,0,1:T(2,128)(2,1)S(1)}, bf16[1,65,128]{2,0,1:T(2,128)(2,1)S(1)}, u32[]{:S(2)}, u32[]{:S(2)}) collective-permute-start(bf16[1,65,128]{2,0,1:T(2,128)(2,1)S(1)} %get-tuple-element.23), channel_id=1, source_target_pairs={{0,32},{8,40},{16,48},{24,56},{32,64},{40,72},{48,80},{56,88},{64,... | collective-permute-start | bytes 49928 | tf_op jit(solution)/shard_map/ppermute | solution.py:24
  238.0 8.4 %collective-permute-start.14 = (bf16[1,65,128]{2,0,1:T(2,128)(2,1)S(1)}, bf16[1,65,128]{2,0,1:T(2,128)(2,1)S(1)}, u32[]{:S(2)}, u32[]{:S(2)}) collective-permute-start(bf16[1,65,128]{2,0,1:T(2,128)(2,1)S(1)} %get-tuple-element.24), channel_id=1, source_target_pairs={{0,112},{8,120},{16,0},{24,8},{32,16},{40,24},{48,32},{56,40},{64,... | collective-permute-start | bytes 49928 | tf_op jit(solution)/shard_map/ppermute | solution.py:24
  242.5 10.8 %collective-permute-start.5 = (bf16[1,65,128]{2,0,1:T(2,128)(2,1)S(1)}, bf16[1,65,128]{2,0,1:T(2,128)(2,1)S(1)}, u32[]{:S(2)}, u32[]{:S(2)}) collective-permute-start(bf16[1,65,128]{2,0,1:T(2,128)(2,1)S(1)} %get-tuple-element.25), channel_id=1, source_target_pairs={{0,40},{8,48},{16,56},{24,64},{32,72},{40,80},{48,88},{56,96},{64,... | collective-permute-start | bytes 49928 | tf_op jit(solution)/shard_map/ppermute | solution.py:24
  242.5 10.8 %collective-permute-start.6 = (bf16[1,65,128]{2,0,1:T(2,128)(2,1)S(1)}, bf16[1,65,128]{2,0,1:T(2,128)(2,1)S(1)}, u32[]{:S(2)}, u32[]{:S(2)}) collective-permute-start(bf16[1,65,128]{2,0,1:T(2,128)(2,1)S(1)} %get-tuple-element.26), channel_id=1, source_target_pairs={{0,48},{8,56},{16,64},{24,72},{32,80},{40,88},{48,96},{56,104},{64... | collective-permute-start | bytes 49928 | tf_op jit(solution)/shard_map/ppermute | solution.py:24
  242.6 10.7 %collective-permute-start.7 = (bf16[1,65,128]{2,0,1:T(2,128)(2,1)S(1)}, bf16[1,65,128]{2,0,1:T(2,128)(2,1)S(1)}, u32[]{:S(2)}, u32[]{:S(2)}) collective-permute-start(bf16[1,65,128]{2,0,1:T(2,128)(2,1)S(1)} %get-tuple-element.27), channel_id=1, source_target_pairs={{0,56},{8,64},{16,72},{24,80},{32,88},{40,96},{48,104},{56,112},{6... | collective-permute-start | bytes 49928 | tf_op jit(solution)/shard_map/ppermute | solution.py:24
  245.2 8.0 %collective-permute-start.8 = (bf16[1,65,128]{2,0,1:T(2,128)(2,1)S(1)}, bf16[1,65,128]{2,0,1:T(2,128)(2,1)S(1)}, u32[]{:S(2)}, u32[]{:S(2)}) collective-permute-start(bf16[1,65,128]{2,0,1:T(2,128)(2,1)S(1)} %get-tuple-element.28), channel_id=1, source_target_pairs={{0,64},{8,72},{16,80},{24,88},{32,96},{40,104},{48,112},{56,120},{... | collective-permute-start | bytes 49928 | tf_op jit(solution)/shard_map/ppermute | solution.py:24
  246.4 6.9 %collective-permute-start.9 = (bf16[1,65,128]{2,0,1:T(2,128)(2,1)S(1)}, bf16[1,65,128]{2,0,1:T(2,128)(2,1)S(1)}, u32[]{:S(2)}, u32[]{:S(2)}) collective-permute-start(bf16[1,65,128]{2,0,1:T(2,128)(2,1)S(1)} %get-tuple-element.29), channel_id=1, source_target_pairs={{0,72},{8,80},{16,88},{24,96},{32,104},{40,112},{48,120},{56,0},{6... | collective-permute-start | bytes 49928 | tf_op jit(solution)/shard_map/ppermute | solution.py:24
  (8 other events, 35.7 us)
Sparse Core Ops, SparseCore 0:
  11.0 49.6 all-gather.2
  63.2 43.5 all-gather.4
  129.1 41.1 reduce-scatter.6
  172.6 41.8 reduce-scatter.4
  216.7 41.5 reduce-scatter.8
  260.6 42.0 reduce-scatter.10

commit v8 on v6

--- a/solution.py
+++ b/solution.py
@@ -168,6 +168,7 @@
     earlier = from_behind(keyval, "seq", 1)
     window = jnp.concatenate([earlier, keyval], axis=0)
     halves = 2
+    out_groups = w_output.reshape(mp_count, -1, w_output.shape[1])
     blocks_all = tok_rows // min(256, tok_rows)
     outputs = []
     for part in range(halves):
@@ -180,13 +181,13 @@
             part * blocks_all // halves,
             blocks_all // halves,
         )
-        partial_term = lax.dot_general(
-            attended, w_output, (((1,), (1,)), ((), ())), preferred_element_type=jnp.float32
+        partial_term = jnp.einsum(
+            "tk,dck->dtc", attended, out_groups, preferred_element_type=jnp.float32
         )
         outputs.append(
-            lax.psum_scatter(partial_term.astype(jnp.bfloat16), "mp", scatter_dimension=1, tiled=True)
+            lax.psum_scatter(partial_term.astype(jnp.bfloat16), "mp", scatter_dimension=0, tiled=True)
         )
-    layer_out = jnp.concatenate(outputs, axis=0)
+    layer_out = jnp.concatenate(outputs, axis=1)[0]
     pages_dev = tok_rows // PAGE
     share_width = 2 * head_size // ratio
     share_index = mp_index % ratio

time: 292 us -> 293 us (level)
  the two profiles are of different devices: /device:TPU:120 before, /device:TPU:1 now
where the time goes in v8:
time: 293 us; the launch traced here: 292 us
  starting transfers between devices  95.4 us (33%)
  Pallas kernels  67.4 us (23%)
  waiting for transfers between devices  35.6 us (12%)
  local copies, waits for them, and re-layouts  27.1 us (9%)
  other arithmetic  23.3 us (8%)
  matrix products  14.9 us (5%)
  between operations  14.2 us (5%)
  blocking collectives  13.7 us (5%)
    ppermute x15, starting transfers between devices, shift_round(): return lax.ppermute(x, axis, [(i, (i + by) % peers) for i in range(peers)])  92 us
    pallas_call x2, Pallas kernels, flash_attention(): pl.pallas_call(functools.partial(flash_kernel, q_rows, tokens, first_bloc...  67.4 us
    all_gather x1, waiting for transfers between devices, body(): lax.all_gather(jnp.concatenate([q_weight, kv_own], axis=1), 'seq', axis=0...  24.3 us
    psum x1, blocking collectives, body(): seg_total = lax.psum(seg_hist, 'seq')  13.7 us
    another operation x4, other arithmetic  8.51 us
    dot_general x2, matrix products, body(): jnp.einsum('tk,dck->dtc', attended, out_groups, preferred_element_type=jn...  7.78 us
    unnamed x26, local copies, waits for them, and re-layouts  7.63 us
    dot_general x1, matrix products, body(): jnp.dot(normed, w_inputs, preferred_element_type=jnp.float32)  6.64 us
  transfers between devices with their start and end apart: 20, of which 8 were waited for; matrix products, arithmetic and copies ran while one was open for 19% of the time, Pallas kernels for 23%

profile of v8, /device:TPU:1, one launch (start us, length us, event | category | flops | bytes accessed | tf_op | source)
XLA Modules:
  0.0 291.6 jit_solution(3424166407916808370)
XLA Ops:
  11.2 13.7 %psum.7 = s32[32]{0:T(128)S(1)} all-reduce(s32[32]{0:T(128)S(1)} %convert_reduce_fusion), channel_id=1, replica_groups=mesh['seq'=16,'mp'=8] {'seq'}, use_global_device_ids=true, to_apply=%region_1.2 | all-reduce | flops 32 | bytes 256 | tf_op jit(solution)/shard_map/psum | solution.py:149
  25.0 5.1 %fusion = f32[2048]{0:T(1024)S(1)} fusion(bf16[2048,2048]{1,0:T(8,128)(2,1)} %param.7), kind=kLoop, calls=%fused_computation.2 | loop fusion | flops 12580864 | bytes 8396800 | tf_op jit(solution)/shard_map/reduce_sum | solution.py:143
  31.2 5.3 %reshape.185.qs_ref = s32[8192,1]{1,0:T(8,128)} reshape(s32[8,4,256]{2,1,0:T(4,128)S(1)} %broadcast_in_dim.26) | data formatting | bytes 65536 | tf_op jit(solution)/shard_map/reshape | solution.py:91
  36.4 24.3 %all-gather.3.cloned.1.call-done = bf16[2048,384]{1,0:T(8,128)(2,1)} async-done(((bf16[128,384]{1,0:T(8,128)(2,1)}), bf16[2048,384]{1,0:T(8,128)(2,1)}) %all-gather.3.cloned.1.call-update) | async-done | bytes 1572880 | tf_op jit(solution)/shard_map/all_gather | solution.py:138
  60.8 6.6 %fusion.3 = f32[2048,384]{0,1:T(8,128)S(1)} fusion(bf16[2048,384]{1,0:T(8,128)(2,1)} %all-gather.3.cloned.1.call-done, bf16[2048,2048]{1,0:T(8,128)(2,1)} %param.7, f32[2048]{0:T(1024)S(1)} %copy-done.7, f32[2048]{0:T(1024)S(1)} %add_rsqrt_fusion), kind=kOutput, calls=%fused_computation.5 | convolution fusion | flops 3238002688 | bytes 13123584 | tf_op jit(solution)/shard_map/dot_general | solution.py:161
  69.4 2.3 copy.70
  71.7 2.3 copy.69
  74.0 8.0 %subtract_convert_fusion = (bf16[2048,32]{1,0:T(8,128)(2,1)}, bf16[2048,32]{1,0:T(8,128)(2,1)}, f32[2048,32]{1,0:T(8,128)}, f32[2048,32]{1,0:T(8,128)}) fusion(f32[2048,32]{1,0:T(8,128)} %copy.70, f32[2048,32]{1,0:T(8,128)} %copy.69, f32[2048]{0:T(1024)S(1)} %subtract_convert_fusion.2, f32[32]{0:T(128)S(1)} %multiply_exponential_fusion), kind=kLoop, calls=%fused_computation.33 | loop fusion | flops 589824 | bytes 1319040 | tf_op jit(solution)/shard_map/convert.2
  85.2 1.9 pad_maximum_fusion
  87.1 3.2 %collective-permute-start = (bf16[2048,128]{1,0:T(8,128)(2,1)S(1)}, bf16[2048,128]{1,0:T(8,128)(2,1)}, u32[]{:S(2)}, u32[]{:S(2)}) collective-permute-start(bf16[2048,128]{1,0:T(8,128)(2,1)S(1)} %pad_maximum_fusion), channel_id=1, source_target_pairs={{0,8},{8,16},{16,24},{24,32},{32,40},{40,48},{48,56},{56,64},{64,7... | collective-permute-start | bytes 1572872 | tf_op jit(solution)/shard_map/ppermute | solution.py:19
  91.0 2.0 copy.52
  93.0 4.4 %collective-permute-done = bf16[2048,128]{1,0:T(8,128)(2,1)} collective-permute-done((bf16[2048,128]{1,0:T(8,128)(2,1)S(1)}, bf16[2048,128]{1,0:T(8,128)(2,1)}, u32[]{:S(2)}, u32[]{:S(2)}) %collective-permute-start) | collective-permute-done | bytes 524320 | tf_op jit(solution)/shard_map/ppermute | solution.py:19
  100.6 40.1 %shard_map.87 = bf16[4096,64]{1,0:T(8,128)(2,1)} custom-call(s32[1]{0:T(128)} %bitcast.first_ref, s32[8]{0:T(128)} %reduce_min.8.lowest_ref, bf16[8192,64]{1,0:T(8,128)(2,1)} %bitcast.60, bf16[4096,64]{1,0:T(8,128)(2,1)} %get-tuple-element.17.k_ref, bf16[4096,64]{1,0:T(8,128)(2,1)} %get-tuple-element.16.v_ref, s32[8192,1]{1,0:T(8,128)} %reshape.185.qs_ref), custom_call_target="tpu_custom_call" | custom-call | tf_op jit(solution)/shard_map/pallas_call | solution.py:98
  142.3 4.5 %convert_bitcast_fusion = bf16[8,1024,256]{2,1,0:T(8,128)(2,1)} fusion(bf16[8,256,256]{2,1,0:T(8,128)(2,1)} %bitcast.65, bf16[1024,256]{0,1:T(8,128)(2,1)S(1)} %bitcast.74), kind=kOutput, calls=%fused_computation.8 | convolution fusion | flops 1075838976 | bytes 5767168 | tf_op jit(solution)/shard_map/tk,dck->dtc/dot_general | solution.py:184
  146.9 27.3 %shard_map.86 = bf16[4096,64]{1,0:T(8,128)(2,1)} custom-call(s32[1]{0:T(128)} %bitcast.first_ref, s32[8]{0:T(128)} %reduce_min.8.lowest_ref, bf16[8192,64]{1,0:T(8,128)(2,1)} %bitcast.61, bf16[4096,64]{1,0:T(8,128)(2,1)} %get-tuple-element.17.k_ref, bf16[4096,64]{1,0:T(8,128)(2,1)} %get-tuple-element.16.v_ref, s32[8192,1]{1,0:T(8,128)} %reshape.185.qs_ref), custom_call_target="tpu_custom_call" | custom-call | tf_op jit(solution)/shard_map/pallas_call | solution.py:98
  175.9 3.3 %convert_bitcast_fusion.1 = bf16[8,1024,256]{2,1,0:T(8,128)(2,1)} fusion(bf16[8,256,256]{2,1,0:T(8,128)(2,1)S(1)} %bitcast.66, bf16[1024,256]{0,1:T(8,128)(2,1)S(1)} %bitcast.75), kind=kOutput, calls=%fused_computation.9 | convolution fusion | flops 1075838976 | bytes 5767168 | tf_op jit(solution)/shard_map/tk,dck->dtc/dot_general | solution.py:184
  180.5 35.0 %collective-permute-start.13 = (bf16[1,65,128]{2,0,1:T(2,128)(2,1)S(1)}, bf16[1,65,128]{2,0,1:T(2,128)(2,1)S(1)}, u32[]{:S(2)}, u32[]{:S(2)}) collective-permute-start(bf16[1,65,128]{2,0,1:T(2,128)(2,1)S(1)} %get-tuple-element.30), channel_id=1, source_target_pairs={{0,104},{8,112},{16,120},{24,0},{32,8},{40,16},{48,24},{56,32},{64... | collective-permute-start | bytes 49928 | tf_op jit(solution)/shard_map/ppermute | solution.py:24
  215.5 3.5 %collective-permute-start.12 = (bf16[1,65,128]{2,0,1:T(2,128)(2,1)S(1)}, bf16[1,65,128]{2,0,1:T(2,128)(2,1)S(1)}, u32[]{:S(2)}, u32[]{:S(2)}) collective-permute-start(bf16[1,65,128]{2,0,1:T(2,128)(2,1)S(1)} %get-tuple-element.33), channel_id=1, source_target_pairs={{0,96},{8,104},{16,112},{24,120},{32,0},{40,8},{48,16},{56,24},{64... | collective-permute-start | bytes 49928 | tf_op jit(solution)/shard_map/ppermute | solution.py:24
  219.1 3.5 %collective-permute-start.15 = (bf16[1,65,128]{2,0,1:T(2,128)(2,1)S(1)}, bf16[1,65,128]{2,0,1:T(2,128)(2,1)S(1)}, u32[]{:S(2)}, u32[]{:S(2)}) collective-permute-start(bf16[1,65,128]{2,0,1:T(2,128)(2,1)S(1)} %get-tuple-element.18), channel_id=1, source_target_pairs={{0,120},{8,0},{16,8},{24,16},{32,24},{40,32},{48,40},{56,48},{64,5... | collective-permute-start | bytes 49928 | tf_op jit(solution)/shard_map/ppermute | solution.py:24
  224.4 42.5 %collective-permute-start.4 = (bf16[1,65,128]{2,0,1:T(2,128)(2,1)S(1)}, bf16[1,65,128]{2,0,1:T(2,128)(2,1)S(1)}, u32[]{:S(2)}, u32[]{:S(2)}) collective-permute-start(bf16[1,65,128]{2,0,1:T(2,128)(2,1)S(1)} %get-tuple-element.23), channel_id=1, source_target_pairs={{0,32},{8,40},{16,48},{24,56},{32,64},{40,72},{48,80},{56,88},{64,... | collective-permute-start | bytes 49928 | tf_op jit(solution)/shard_map/ppermute | solution.py:24
  268.3 5.7 %collective-permute-start.7 = (bf16[1,65,128]{2,0,1:T(2,128)(2,1)S(1)}, bf16[1,65,128]{2,0,1:T(2,128)(2,1)S(1)}, u32[]{:S(2)}, u32[]{:S(2)}) collective-permute-start(bf16[1,65,128]{2,0,1:T(2,128)(2,1)S(1)} %get-tuple-element.27), channel_id=1, source_target_pairs={{0,56},{8,64},{16,72},{24,80},{32,88},{40,96},{48,104},{56,112},{6... | collective-permute-start | bytes 49928 | tf_op jit(solution)/shard_map/ppermute | solution.py:24
  275.1 3.2 %collective-permute-done.8 = bf16[1,65,128]{2,0,1:T(2,128)(2,1)S(1)} collective-permute-done((bf16[1,65,128]{2,0,1:T(2,128)(2,1)S(1)}, bf16[1,65,128]{2,0,1:T(2,128)(2,1)S(1)}, u32[]{:S(2)}, u32[]{:S(2)}) %collective-permute-start.8) | collective-permute-done | bytes 16672 | tf_op jit(solution)/shard_map/ppermute | solution.py:24
  279.0 2.6 concatenate.38
  282.9 2.2 maximum_bitcast_fusion.1
  (100 shorter events, 24.9 us)
Async XLA Ops:
  7.2 53.6 %all-gather.3.cloned.1.call-start = ((), (), s32[]{:S(2)}) async-start(), calls=%async_computation.2 | async-start | bytes 1671168 | tf_op jit(solution)/shard_map/all_gather | solution.py:138
  9.6 132.7 %all-gather.5.cloned.1.call-start = ((), (), s32[]{:S(2)}) async-start(), calls=%async_computation.3 | async-start | bytes 1114112 | tf_op jit(solution)/shard_map/all_gather | solution.py:141
  10.3 272.5 %reduce-scatter.5.cloned.1.call-start = ((), (), s32[]{:S(2)}) async-start(), calls=%async_computation.5 | async-start | bytes 4718592 | tf_op jit(solution)/shard_map/reduce_scatter | solution.py:188
  30.1 30.7 %copy-start.7 = (f32[2048]{0:T(1024)S(1)}, f32[2048]{0:T(1024)}, u32[]{:S(2)}) copy-start(f32[2048]{0:T(1024)} %param.8) | copy-start | bytes 24580
  82.0 8.3 %slice-start = ((f32[2048,384]{0,1:T(8,128)}), f32[2048,256]{0,1:T(8,128)S(1)}, s32[]{:S(2)}) async-start(f32[2048,384]{0,1:T(8,128)} %copy-done.1), calls=%async_computation.6 | async-start | bytes 4194304 | tf_op jit(solution)/shard_map/slice | solution.py:162
  87.1 10.3 %collective-permute-start = (bf16[2048,128]{1,0:T(8,128)(2,1)S(1)}, bf16[2048,128]{1,0:T(8,128)(2,1)}, u32[]{:S(2)}, u32[]{:S(2)}) collective-permute-start(bf16[2048,128]{1,0:T(8,128)(2,1)S(1)} %pad_maximum_fusion), channel_id=1, source_target_pairs={{0,8},{8,16},{16,24},{24,32},{32,40},{40,48},{48,56},{56,64},{64,7... | collective-permute-start | bytes 1572872 | tf_op jit(solution)/shard_map/ppermute | solution.py:19
  90.6 6.7 %copy-start.2 = (bf16[2048,64]{1,0:T(8,128)(2,1)S(1)}, bf16[2048,64]{1,0:T(8,128)(2,1)}, u32[]{:S(2)}) copy-start(bf16[2048,64]{1,0:T(8,128)(2,1)} %copy.71) | copy-start | bytes 786436
  146.8 29.0 %copy-start.5 = (bf16[2048,256]{1,0:T(8,128)(2,1)S(1)}, bf16[2048,256]{1,0:T(8,128)(2,1)}, u32[]{:S(2)}) copy-start(bf16[2048,256]{1,0:T(8,128)(2,1)} %all-gather.5.cloned.1.call-done) | copy-start | bytes 3145732
  146.9 136.0 %reduce-scatter.3.cloned.1.call-start = ((), (), s32[]{:S(2)}) async-start(), calls=%async_computation.4 | async-start | bytes 4718592 | tf_op jit(solution)/shard_map/reduce_scatter | solution.py:188
  180.5 42.3 %collective-permute-start.13 = (bf16[1,65,128]{2,0,1:T(2,128)(2,1)S(1)}, bf16[1,65,128]{2,0,1:T(2,128)(2,1)S(1)}, u32[]{:S(2)}, u32[]{:S(2)}) collective-permute-start(bf16[1,65,128]{2,0,1:T(2,128)(2,1)S(1)} %get-tuple-element.30), channel_id=1, source_target_pairs={{0,104},{8,112},{16,120},{24,0},{32,8},{40,16},{48,24},{56,32},{64... | collective-permute-start | bytes 49928 | tf_op jit(solution)/shard_map/ppermute | solution.py:24
  215.5 7.4 %collective-permute-start.10 = (bf16[1,65,128]{2,0,1:T(2,128)(2,1)S(1)}, bf16[1,65,128]{2,0,1:T(2,128)(2,1)S(1)}, u32[]{:S(2)}, u32[]{:S(2)}) collective-permute-start(bf16[1,65,128]{2,0,1:T(2,128)(2,1)S(1)} %get-tuple-element.31), channel_id=1, source_target_pairs={{0,80},{8,88},{16,96},{24,104},{32,112},{40,120},{48,0},{56,8},{64... | collective-permute-start | bytes 49928 | tf_op jit(solution)/shard_map/ppermute | solution.py:24
  215.5 8.3 %collective-permute-start.11 = (bf16[1,65,128]{2,0,1:T(2,128)(2,1)S(1)}, bf16[1,65,128]{2,0,1:T(2,128)(2,1)S(1)}, u32[]{:S(2)}, u32[]{:S(2)}) collective-permute-start(bf16[1,65,128]{2,0,1:T(2,128)(2,1)S(1)} %get-tuple-element.32), channel_id=1, source_target_pairs={{0,88},{8,96},{16,104},{24,112},{32,120},{40,0},{48,8},{56,16},{64... | collective-permute-start | bytes 49928 | tf_op jit(solution)/shard_map/ppermute | solution.py:24
  215.5 8.9 %collective-permute-start.12 = (bf16[1,65,128]{2,0,1:T(2,128)(2,1)S(1)}, bf16[1,65,128]{2,0,1:T(2,128)(2,1)S(1)}, u32[]{:S(2)}, u32[]{:S(2)}) collective-permute-start(bf16[1,65,128]{2,0,1:T(2,128)(2,1)S(1)} %get-tuple-element.33), channel_id=1, source_target_pairs={{0,96},{8,104},{16,112},{24,120},{32,0},{40,8},{48,16},{56,24},{64... | collective-permute-start | bytes 49928 | tf_op jit(solution)/shard_map/ppermute | solution.py:24
  219.1 47.8 %collective-permute-start.15 = (bf16[1,65,128]{2,0,1:T(2,128)(2,1)S(1)}, bf16[1,65,128]{2,0,1:T(2,128)(2,1)S(1)}, u32[]{:S(2)}, u32[]{:S(2)}) collective-permute-start(bf16[1,65,128]{2,0,1:T(2,128)(2,1)S(1)} %get-tuple-element.18), channel_id=1, source_target_pairs={{0,120},{8,0},{16,8},{24,16},{32,24},{40,32},{48,40},{56,48},{64,5... | collective-permute-start | bytes 49928 | tf_op jit(solution)/shard_map/ppermute | solution.py:24
  222.8 44.1 %collective-permute-start.1 = (bf16[1,65,128]{2,0,1:T(2,128)(2,1)S(1)}, bf16[1,65,128]{2,0,1:T(2,128)(2,1)S(1)}, u32[]{:S(2)}, u32[]{:S(2)}) collective-permute-start(bf16[1,65,128]{2,0,1:T(2,128)(2,1)S(1)} %get-tuple-element.20), channel_id=1, source_target_pairs={{0,8},{8,16},{16,24},{24,32},{32,40},{40,48},{48,56},{56,64},{64,7... | collective-permute-start | bytes 49928 | tf_op jit(solution)/shard_map/ppermute | solution.py:24
  222.9 45.3 %collective-permute-start.2 = (bf16[1,65,128]{2,0,1:T(2,128)(2,1)S(1)}, bf16[1,65,128]{2,0,1:T(2,128)(2,1)S(1)}, u32[]{:S(2)}, u32[]{:S(2)}) collective-permute-start(bf16[1,65,128]{2,0,1:T(2,128)(2,1)S(1)} %get-tuple-element.21), channel_id=1, source_target_pairs={{0,16},{8,24},{16,32},{24,40},{32,48},{40,56},{48,64},{56,72},{64,... | collective-permute-start | bytes 49928 | tf_op jit(solution)/shard_map/ppermute | solution.py:24
  223.8 44.5 %collective-permute-start.3 = (bf16[1,65,128]{2,0,1:T(2,128)(2,1)S(1)}, bf16[1,65,128]{2,0,1:T(2,128)(2,1)S(1)}, u32[]{:S(2)}, u32[]{:S(2)}) collective-permute-start(bf16[1,65,128]{2,0,1:T(2,128)(2,1)S(1)} %get-tuple-element.22), channel_id=1, source_target_pairs={{0,24},{8,32},{16,40},{24,48},{32,56},{40,64},{48,72},{56,80},{64,... | collective-permute-start | bytes 49928 | tf_op jit(solution)/shard_map/ppermute | solution.py:24
  224.4 49.6 %collective-permute-start.4 = (bf16[1,65,128]{2,0,1:T(2,128)(2,1)S(1)}, bf16[1,65,128]{2,0,1:T(2,128)(2,1)S(1)}, u32[]{:S(2)}, u32[]{:S(2)}) collective-permute-start(bf16[1,65,128]{2,0,1:T(2,128)(2,1)S(1)} %get-tuple-element.23), channel_id=1, source_target_pairs={{0,32},{8,40},{16,48},{24,56},{32,64},{40,72},{48,80},{56,88},{64,... | collective-permute-start | bytes 49928 | tf_op jit(solution)/shard_map/ppermute | solution.py:24
  266.9 7.1 %collective-permute-start.14 = (bf16[1,65,128]{2,0,1:T(2,128)(2,1)S(1)}, bf16[1,65,128]{2,0,1:T(2,128)(2,1)S(1)}, u32[]{:S(2)}, u32[]{:S(2)}) collective-permute-start(bf16[1,65,128]{2,0,1:T(2,128)(2,1)S(1)} %get-tuple-element.24), channel_id=1, source_target_pairs={{0,112},{8,120},{16,0},{24,8},{32,16},{40,24},{48,32},{56,40},{64,... | collective-permute-start | bytes 49928 | tf_op jit(solution)/shard_map/ppermute | solution.py:24
  266.9 7.3 %collective-permute-start.5 = (bf16[1,65,128]{2,0,1:T(2,128)(2,1)S(1)}, bf16[1,65,128]{2,0,1:T(2,128)(2,1)S(1)}, u32[]{:S(2)}, u32[]{:S(2)}) collective-permute-start(bf16[1,65,128]{2,0,1:T(2,128)(2,1)S(1)} %get-tuple-element.25), channel_id=1, source_target_pairs={{0,40},{8,48},{16,56},{24,64},{32,72},{40,80},{48,88},{56,96},{64,... | collective-permute-start | bytes 49928 | tf_op jit(solution)/shard_map/ppermute | solution.py:24
  268.2 6.0 %collective-permute-start.6 = (bf16[1,65,128]{2,0,1:T(2,128)(2,1)S(1)}, bf16[1,65,128]{2,0,1:T(2,128)(2,1)S(1)}, u32[]{:S(2)}, u32[]{:S(2)}) collective-permute-start(bf16[1,65,128]{2,0,1:T(2,128)(2,1)S(1)} %get-tuple-element.26), channel_id=1, source_target_pairs={{0,48},{8,56},{16,64},{24,72},{32,80},{40,88},{48,96},{56,104},{64... | collective-permute-start | bytes 49928 | tf_op jit(solution)/shard_map/ppermute | solution.py:24
  268.3 6.8 %collective-permute-start.7 = (bf16[1,65,128]{2,0,1:T(2,128)(2,1)S(1)}, bf16[1,65,128]{2,0,1:T(2,128)(2,1)S(1)}, u32[]{:S(2)}, u32[]{:S(2)}) collective-permute-start(bf16[1,65,128]{2,0,1:T(2,128)(2,1)S(1)} %get-tuple-element.27), channel_id=1, source_target_pairs={{0,56},{8,64},{16,72},{24,80},{32,88},{40,96},{48,104},{56,112},{6... | collective-permute-start | bytes 49928 | tf_op jit(solution)/shard_map/ppermute | solution.py:24
  274.0 4.3 %collective-permute-start.8 = (bf16[1,65,128]{2,0,1:T(2,128)(2,1)S(1)}, bf16[1,65,128]{2,0,1:T(2,128)(2,1)S(1)}, u32[]{:S(2)}, u32[]{:S(2)}) collective-permute-start(bf16[1,65,128]{2,0,1:T(2,128)(2,1)S(1)} %get-tuple-element.28), channel_id=1, source_target_pairs={{0,64},{8,72},{16,80},{24,88},{32,96},{40,104},{48,112},{56,120},{... | collective-permute-start | bytes 49928 | tf_op jit(solution)/shard_map/ppermute | solution.py:24
  274.1 5.0 %collective-permute-start.9 = (bf16[1,65,128]{2,0,1:T(2,128)(2,1)S(1)}, bf16[1,65,128]{2,0,1:T(2,128)(2,1)S(1)}, u32[]{:S(2)}, u32[]{:S(2)}) collective-permute-start(bf16[1,65,128]{2,0,1:T(2,128)(2,1)S(1)} %get-tuple-element.29), channel_id=1, source_target_pairs={{0,72},{8,80},{16,88},{24,96},{32,104},{40,112},{48,120},{56,0},{6... | collective-permute-start | bytes 49928 | tf_op jit(solution)/shard_map/ppermute | solution.py:24
  (6 other events, 29.6 us)
Sparse Core Ops, SparseCore 0:
  11.0 49.6 all-gather.2
  63.2 43.5 all-gather.4
  147.0 62.0 reduce-scatter.4
  211.3 52.1 reduce-scatter.2

commit v9 on v6

--- a/solution.py
+++ b/solution.py
@@ -135,8 +135,9 @@
     own_head = mp_index // ratio
     kv_own = lax.dynamic_index_in_dim(kv_weight, own_head, 0, keepdims=False)
     q_columns = q_weight.shape[1]
+    kv_columns = kv_own.shape[1]
     w_inputs = lax.all_gather(
-        jnp.concatenate([q_weight, kv_own], axis=1), "seq", axis=0, tiled=True
+        jnp.concatenate([kv_own, q_weight], axis=1), "seq", axis=0, tiled=True
     )
     w_output = lax.all_gather(out_weight, "seq", axis=0, tiled=True)
     inputs = tokens_in.astype(jnp.float32)
@@ -155,17 +156,16 @@
     half = head_size // 2
     freqs = jnp.exp(jnp.arange(half, dtype=jnp.float32) * (-2.0 * math.log(10000.0) / head_size))
     angles = positions.astype(jnp.float32)[:, None] * freqs[None, :]
-    cosine = jnp.cos(angles)
-    sine_table = jnp.sin(angles)
+    cosine, sine_table = lax.optimization_barrier((jnp.cos(angles), jnp.sin(angles)))
     local_heads = q_columns // head_size
-    projected_all = jnp.dot(normed, w_inputs, preferred_element_type=jnp.float32)
-    queries = projected_all[:, :q_columns].reshape(tok_rows, local_heads, head_size)
-    queries = rotate_half(queries, cosine[:, None, :], sine_table[:, None, :]).astype(jnp.bfloat16)
-    projected = projected_all[:, q_columns:]
+    projected = jnp.dot(normed, w_inputs[:, :kv_columns], preferred_element_type=jnp.float32)
     key_rows = rotate_half(projected[:, :head_size], cosine, sine_table).astype(jnp.bfloat16)
     value_rows = projected[:, head_size:].astype(jnp.bfloat16)
     keyval = jnp.concatenate([key_rows, value_rows], axis=1)
     earlier = from_behind(keyval, "seq", 1)
+    queries = jnp.dot(normed, w_inputs[:, kv_columns:], preferred_element_type=jnp.float32)
+    queries = queries.reshape(tok_rows, local_heads, head_size)
+    queries = rotate_half(queries, cosine[:, None, :], sine_table[:, None, :]).astype(jnp.bfloat16)
     window = jnp.concatenate([earlier, keyval], axis=0)
     halves = 2
     blocks_all = tok_rows // min(256, tok_rows)

time: 292 us -> 273 us (0.935)
  the two profiles are of different devices: /device:TPU:120 before, /device:TPU:1 now
where the time goes in v9:
time: 273 us; the launch traced here: 272 us
  Pallas kernels  79.6 us (29%)
  waiting for transfers between devices  56.9 us (21%)
  starting transfers between devices  51.1 us (19%)
  local copies, waits for them, and re-layouts  20.2 us (7%)
  matrix products  18.5 us (7%)
  other arithmetic  17.8 us (7%)
  between operations  14.1 us (5%)
  blocking collectives  13.7 us (5%)
    pallas_call x2, Pallas kernels, flash_attention(): pl.pallas_call(functools.partial(flash_kernel, q_rows, tokens, first_bloc...  79.6 us
    ppermute x15, starting transfers between devices, shift_round(): return lax.ppermute(x, axis, [(i, (i + by) % peers) for i in range(peers)])  47.4 us
    ppermute x15, waiting for transfers between devices, shift_round(): return lax.ppermute(x, axis, [(i, (i + by) % peers) for i in range(peers)])  36.8 us
    all_gather x1, waiting for transfers between devices, body(): lax.all_gather(jnp.concatenate([kv_own, q_weight], axis=1), 'seq', axis=0...  19.3 us
    psum x1, blocking collectives, body(): seg_total = lax.psum(seg_hist, 'seq')  13.7 us
    dot_general x2, matrix products, body(): lax.dot_general(attended, w_output, (((1,), (1,)), ((), ())), preferred_e...  7.78 us
  transfers between devices with their start and end apart: 20, of which 3 were waited for; matrix products, arithmetic and copies ran while one was open for 17% of the time, Pallas kernels for 29%

profile of v9, /device:TPU:1, one launch (start us, length us, event | category | flops | bytes accessed | tf_op | source)
XLA Modules:
  0.0 272.1 jit_solution(3135710435879749897)
XLA Ops:
  11.2 13.7 %psum.7 = s32[32]{0:T(128)S(1)} all-reduce(s32[32]{0:T(128)S(1)} %convert_reduce_fusion), channel_id=1, replica_groups=mesh['seq'=16,'mp'=8] {'seq'}, use_global_device_ids=true, to_apply=%region_1.2 | all-reduce | flops 32 | bytes 256 | tf_op jit(solution)/shard_map/psum | solution.py:150
  25.0 5.1 %fusion = f32[2048]{0:T(1024)S(1)} fusion(bf16[2048,2048]{1,0:T(8,128)(2,1)} %param.7), kind=kLoop, calls=%fused_computation.2 | loop fusion | flops 12580864 | bytes 8396800 | tf_op jit(solution)/shard_map/reduce_sum | solution.py:144
  30.5 3.7 %multiply_sine_fusion = (f32[2048,32]{1,0:T(8,128)S(1)}, f32[2048,32]{1,0:T(8,128)S(1)}) fusion(f32[32]{0:T(128)S(1)} %multiply_exponential_fusion, f32[2048]{0:T(1024)S(1)} %subtract_convert_fusion.2), kind=kLoop, calls=%fused_computation.24 | loop fusion | flops 65536 | bytes 532608 | tf_op jit(solution)/shard_map/sin | solution.py:159
  36.1 5.3 %reshape.134.qs_ref = s32[8192,1]{1,0:T(8,128)} reshape(s32[8,4,256]{2,1,0:T(4,128)S(1)} %broadcast_in_dim.26) | data formatting | bytes 65536 | tf_op jit(solution)/shard_map/reshape | solution.py:91
  41.4 19.3 %all-gather.3.cloned.1.call-done = bf16[2048,384]{1,0:T(8,128)(2,1)} async-done(((bf16[128,384]{1,0:T(8,128)(2,1)}), bf16[2048,384]{1,0:T(8,128)(2,1)}) %all-gather.3.cloned.1.call-update) | async-done | bytes 1572880 | tf_op jit(solution)/shard_map/all_gather | solution.py:139
  60.8 4.9 %fusion.3 = f32[2048,128]{1,0:T(8,128)S(1)} fusion(bf16[2048,2048]{1,0:T(8,128)(2,1)} %param.7, f32[2048]{0:T(1024)S(1)} %copy-done.7, f32[2048]{0:T(1024)S(1)} %add_rsqrt_fusion, bf16[2048,384]{1,0:T(8,128)(2,1)} %all-gather.3.cloned.1.call-done), kind=kOutput, calls=%fused_computation.7 | convolution fusion | flops 1090519040 | bytes 9977856 | tf_op jit(solution)/shard_map/dot_general | solution.py:161
  68.0 3.4 %collective-permute-start = (bf16[2048,128]{1,0:T(8,128)(2,1)}, bf16[2048,128]{1,0:T(8,128)(2,1)S(1)}, u32[]{:S(2)}, u32[]{:S(2)}) collective-permute-start(bf16[2048,128]{1,0:T(8,128)(2,1)} %pad_maximum_fusion.1), channel_id=1, source_target_pairs={{0,8},{8,16},{16,24},{24,32},{32,40},{40,48},{48,56},{56,64},{64,7... | collective-permute-start | bytes 1572872 | tf_op jit(solution)/shard_map/ppermute | solution.py:19
  71.4 5.3 %fusion.5 = f32[2048,256]{0,1:T(8,128)S(1)} fusion(bf16[2048,2048]{1,0:T(8,128)(2,1)} %param.7, f32[2048]{0:T(1024)S(1)} %copy-done.7, f32[2048]{0:T(1024)S(1)} %add_rsqrt_fusion, bf16[2048,384]{1,0:T(8,128)(2,1)S(1)} %copy-done.6), kind=kOutput, calls=%fused_computation.8 | convolution fusion | flops 2164260864 | bytes 11550720 | tf_op jit(solution)/shard_map/dot_general | solution.py:166
  77.4 2.0 copy.32
  81.6 39.5 %shard_map.87 = bf16[4096,64]{1,0:T(8,128)(2,1)} custom-call(s32[1]{0:T(128)} %bitcast.first_ref, s32[8]{0:T(128)} %reduce_min.8.lowest_ref, bf16[8192,64]{1,0:T(8,128)(2,1)} %bitcast.48, bf16[4096,64]{1,0:T(8,128)(2,1)} %get-tuple-element.17.k_ref, bf16[4096,64]{1,0:T(8,128)(2,1)} %get-tuple-element.16.v_ref, s32[8192,1]{1,0:T(8,128)} %reshape.134.qs_ref), custom_call_target="tpu_custom_call" | custom-call | tf_op jit(solution)/shard_map/pallas_call | solution.py:98
  122.7 4.5 %convolution_convert_fusion = bf16[1024,2048]{1,0:T(8,128)(2,1)} fusion(bf16[1024,256]{0,1:T(8,128)(2,1)S(1)} %bitcast.52, bf16[2048,256]{1,0:T(8,128)(2,1)} %all-gather.5.cloned.1.call-done), kind=kOutput, calls=%fused_computation.5 | convolution fusion | flops 1075838976 | bytes 5767168 | tf_op jit(solution)/shard_map/dot_general | solution.py:183
  127.5 40.1 %shard_map.86 = bf16[4096,64]{1,0:T(8,128)(2,1)} custom-call(s32[1]{0:T(128)} %bitcast.first_ref, s32[8]{0:T(128)} %reduce_min.8.lowest_ref, bf16[8192,64]{1,0:T(8,128)(2,1)} %bitcast.49, bf16[4096,64]{1,0:T(8,128)(2,1)} %get-tuple-element.17.k_ref, bf16[4096,64]{1,0:T(8,128)(2,1)} %get-tuple-element.16.v_ref, s32[8192,1]{1,0:T(8,128)} %reshape.134.qs_ref), custom_call_target="tpu_custom_call" | custom-call | tf_op jit(solution)/shard_map/pallas_call | solution.py:98
  169.3 3.3 %convolution_convert_fusion.1 = bf16[1024,2048]{1,0:T(8,128)(2,1)} fusion(bf16[1024,256]{0,1:T(8,128)(2,1)S(1)} %bitcast.53, bf16[2048,256]{1,0:T(8,128)(2,1)S(1)} %copy-done.3), kind=kOutput, calls=%fused_computation.6 | convolution fusion | flops 1075838976 | bytes 5767168 | tf_op jit(solution)/shard_map/dot_general | solution.py:183
  175.0 19.1 %collective-permute-start.10 = (bf16[1,65,128]{2,0,1:T(2,128)(2,1)S(1)}, bf16[1,65,128]{2,0,1:T(2,128)(2,1)S(1)}, u32[]{:S(2)}, u32[]{:S(2)}) collective-permute-start(bf16[1,65,128]{2,0,1:T(2,128)(2,1)S(1)} %get-tuple-element.31), channel_id=1, source_target_pairs={{0,80},{8,88},{16,96},{24,104},{32,112},{40,120},{48,0},{56,8},{64... | collective-permute-start | bytes 49928 | tf_op jit(solution)/shard_map/ppermute | solution.py:24
  194.1 6.3 %collective-permute-start.11 = (bf16[1,65,128]{2,0,1:T(2,128)(2,1)S(1)}, bf16[1,65,128]{2,0,1:T(2,128)(2,1)S(1)}, u32[]{:S(2)}, u32[]{:S(2)}) collective-permute-start(bf16[1,65,128]{2,0,1:T(2,128)(2,1)S(1)} %get-tuple-element.32), channel_id=1, source_target_pairs={{0,88},{8,96},{16,104},{24,112},{32,120},{40,0},{48,8},{56,16},{64... | collective-permute-start | bytes 49928 | tf_op jit(solution)/shard_map/ppermute | solution.py:24
  202.7 1.8 collective-permute-start.1
  205.0 35.5 %collective-permute-done.11 = bf16[1,65,128]{2,0,1:T(2,128)(2,1)S(1)} collective-permute-done((bf16[1,65,128]{2,0,1:T(2,128)(2,1)S(1)}, bf16[1,65,128]{2,0,1:T(2,128)(2,1)S(1)}, u32[]{:S(2)}, u32[]{:S(2)}) %collective-permute-start.11) | collective-permute-done | bytes 16672 | tf_op jit(solution)/shard_map/ppermute | solution.py:24
  240.5 3.1 %collective-permute-start.3 = (bf16[1,65,128]{2,0,1:T(2,128)(2,1)S(1)}, bf16[1,65,128]{2,0,1:T(2,128)(2,1)S(1)}, u32[]{:S(2)}, u32[]{:S(2)}) collective-permute-start(bf16[1,65,128]{2,0,1:T(2,128)(2,1)S(1)} %get-tuple-element.22), channel_id=1, source_target_pairs={{0,24},{8,32},{16,40},{24,48},{32,56},{40,64},{48,72},{56,80},{64,... | collective-permute-start | bytes 49928 | tf_op jit(solution)/shard_map/ppermute | solution.py:24
  243.7 4.1 %collective-permute-start.14 = (bf16[1,65,128]{2,0,1:T(2,128)(2,1)S(1)}, bf16[1,65,128]{2,0,1:T(2,128)(2,1)S(1)}, u32[]{:S(2)}, u32[]{:S(2)}) collective-permute-start(bf16[1,65,128]{2,0,1:T(2,128)(2,1)S(1)} %get-tuple-element.24), channel_id=1, source_target_pairs={{0,112},{8,120},{16,0},{24,8},{32,16},{40,24},{48,32},{56,40},{64,... | collective-permute-start | bytes 49928 | tf_op jit(solution)/shard_map/ppermute | solution.py:24
  247.8 3.5 %collective-permute-start.6 = (bf16[1,65,128]{2,0,1:T(2,128)(2,1)S(1)}, bf16[1,65,128]{2,0,1:T(2,128)(2,1)S(1)}, u32[]{:S(2)}, u32[]{:S(2)}) collective-permute-start(bf16[1,65,128]{2,0,1:T(2,128)(2,1)S(1)} %get-tuple-element.26), channel_id=1, source_target_pairs={{0,48},{8,56},{16,64},{24,72},{32,80},{40,88},{48,96},{56,104},{64... | collective-permute-start | bytes 49928 | tf_op jit(solution)/shard_map/ppermute | solution.py:24
  251.3 3.3 %collective-permute-start.8 = (bf16[1,65,128]{2,0,1:T(2,128)(2,1)S(1)}, bf16[1,65,128]{2,0,1:T(2,128)(2,1)S(1)}, u32[]{:S(2)}, u32[]{:S(2)}) collective-permute-start(bf16[1,65,128]{2,0,1:T(2,128)(2,1)S(1)} %get-tuple-element.28), channel_id=1, source_target_pairs={{0,64},{8,72},{16,80},{24,88},{32,96},{40,104},{48,112},{56,120},{... | collective-permute-start | bytes 49928 | tf_op jit(solution)/shard_map/ppermute | solution.py:24
  254.7 3.6 %collective-permute-start.9 = (bf16[1,65,128]{2,0,1:T(2,128)(2,1)S(1)}, bf16[1,65,128]{2,0,1:T(2,128)(2,1)S(1)}, u32[]{:S(2)}, u32[]{:S(2)}) collective-permute-start(bf16[1,65,128]{2,0,1:T(2,128)(2,1)S(1)} %get-tuple-element.29), channel_id=1, source_target_pairs={{0,72},{8,80},{16,88},{24,96},{32,104},{40,112},{48,120},{56,0},{6... | collective-permute-start | bytes 49928 | tf_op jit(solution)/shard_map/ppermute | solution.py:24
  259.5 2.6 concatenate.38
  263.3 2.2 pad_maximum_fusion
  (96 shorter events, 22.5 us)
Async XLA Ops:
  7.2 23.2 %copy-start.5 = (s32[2048]{0:T(1024)S(1)}, s32[2048]{0:T(1024)}, u32[]{:S(2)}) copy-start(s32[2048]{0:T(1024)} %param.12) | copy-start | bytes 24580
  7.2 53.6 %all-gather.3.cloned.1.call-start = ((), (), s32[]{:S(2)}) async-start(), calls=%async_computation.2 | async-start | bytes 1671168 | tf_op jit(solution)/shard_map/all_gather | solution.py:139
  9.6 113.1 %all-gather.5.cloned.1.call-start = ((), (), s32[]{:S(2)}) async-start(), calls=%async_computation.3 | async-start | bytes 1114112 | tf_op jit(solution)/shard_map/all_gather | solution.py:142
  10.3 253.0 %reduce-scatter.5.cloned.1.call-start = ((), (), s32[]{:S(2)}) async-start(), calls=%async_computation.5 | async-start | bytes 4718592 | tf_op jit(solution)/shard_map/reduce_scatter | solution.py:187
  25.0 35.8 %copy-start.7 = (f32[2048]{0:T(1024)S(1)}, f32[2048]{0:T(1024)}, u32[]{:S(2)}) copy-start(f32[2048]{0:T(1024)} %param.8) | copy-start | bytes 24580
  68.0 8.7 %copy-start.4 = (f32[2048,32]{0,1:T(8,128)S(1)}, f32[2048,32]{0,1:T(8,128)}, u32[]{:S(2)}) copy-start(f32[2048,32]{0,1:T(8,128)} %copy.31) | copy-start | bytes 786436
  68.0 11.3 %collective-permute-start = (bf16[2048,128]{1,0:T(8,128)(2,1)}, bf16[2048,128]{1,0:T(8,128)(2,1)S(1)}, u32[]{:S(2)}, u32[]{:S(2)}) collective-permute-start(bf16[2048,128]{1,0:T(8,128)(2,1)} %pad_maximum_fusion.1), channel_id=1, source_target_pairs={{0,8},{8,16},{16,24},{24,32},{32,40},{40,48},{48,56},{56,64},{64,7... | collective-permute-start | bytes 1572872 | tf_op jit(solution)/shard_map/ppermute | solution.py:19
  127.2 42.1 %copy-start.3 = (bf16[2048,256]{1,0:T(8,128)(2,1)S(1)}, bf16[2048,256]{1,0:T(8,128)(2,1)}, u32[]{:S(2)}) copy-start(bf16[2048,256]{1,0:T(8,128)(2,1)} %all-gather.5.cloned.1.call-done) | copy-start | bytes 3145732
  127.2 136.1 %reduce-scatter.3.cloned.1.call-start = ((), (), s32[]{:S(2)}) async-start(), calls=%async_computation.4 | async-start | bytes 4718592 | tf_op jit(solution)/shard_map/reduce_scatter | solution.py:187
  174.9 27.7 %collective-permute-start.13 = (bf16[1,65,128]{2,0,1:T(2,128)(2,1)S(1)}, bf16[1,65,128]{2,0,1:T(2,128)(2,1)S(1)}, u32[]{:S(2)}, u32[]{:S(2)}) collective-permute-start(bf16[1,65,128]{2,0,1:T(2,128)(2,1)S(1)} %get-tuple-element.30), channel_id=1, source_target_pairs={{0,104},{8,112},{16,120},{24,0},{32,8},{40,16},{48,24},{56,32},{64... | collective-permute-start | bytes 49928 | tf_op jit(solution)/shard_map/ppermute | solution.py:24
  175.0 29.4 %collective-permute-start.10 = (bf16[1,65,128]{2,0,1:T(2,128)(2,1)S(1)}, bf16[1,65,128]{2,0,1:T(2,128)(2,1)S(1)}, u32[]{:S(2)}, u32[]{:S(2)}) collective-permute-start(bf16[1,65,128]{2,0,1:T(2,128)(2,1)S(1)} %get-tuple-element.31), channel_id=1, source_target_pairs={{0,80},{8,88},{16,96},{24,104},{32,112},{40,120},{48,0},{56,8},{64... | collective-permute-start | bytes 49928 | tf_op jit(solution)/shard_map/ppermute | solution.py:24
  194.1 46.4 %collective-permute-start.11 = (bf16[1,65,128]{2,0,1:T(2,128)(2,1)S(1)}, bf16[1,65,128]{2,0,1:T(2,128)(2,1)S(1)}, u32[]{:S(2)}, u32[]{:S(2)}) collective-permute-start(bf16[1,65,128]{2,0,1:T(2,128)(2,1)S(1)} %get-tuple-element.32), channel_id=1, source_target_pairs={{0,88},{8,96},{16,104},{24,112},{32,120},{40,0},{48,8},{56,16},{64... | collective-permute-start | bytes 49928 | tf_op jit(solution)/shard_map/ppermute | solution.py:24
  200.5 43.2 %collective-permute-start.12 = (bf16[1,65,128]{2,0,1:T(2,128)(2,1)S(1)}, bf16[1,65,128]{2,0,1:T(2,128)(2,1)S(1)}, u32[]{:S(2)}, u32[]{:S(2)}) collective-permute-start(bf16[1,65,128]{2,0,1:T(2,128)(2,1)S(1)} %get-tuple-element.33), channel_id=1, source_target_pairs={{0,96},{8,104},{16,112},{24,120},{32,0},{40,8},{48,16},{56,24},{64... | collective-permute-start | bytes 49928 | tf_op jit(solution)/shard_map/ppermute | solution.py:24
  202.4 41.3 %collective-permute-start.15 = (bf16[1,65,128]{2,0,1:T(2,128)(2,1)S(1)}, bf16[1,65,128]{2,0,1:T(2,128)(2,1)S(1)}, u32[]{:S(2)}, u32[]{:S(2)}) collective-permute-start(bf16[1,65,128]{2,0,1:T(2,128)(2,1)S(1)} %get-tuple-element.18), channel_id=1, source_target_pairs={{0,120},{8,0},{16,8},{24,16},{32,24},{40,32},{48,40},{56,48},{64,5... | collective-permute-start | bytes 49928 | tf_op jit(solution)/shard_map/ppermute | solution.py:24
  202.7 45.2 %collective-permute-start.1 = (bf16[1,65,128]{2,0,1:T(2,128)(2,1)S(1)}, bf16[1,65,128]{2,0,1:T(2,128)(2,1)S(1)}, u32[]{:S(2)}, u32[]{:S(2)}) collective-permute-start(bf16[1,65,128]{2,0,1:T(2,128)(2,1)S(1)} %get-tuple-element.20), channel_id=1, source_target_pairs={{0,8},{8,16},{16,24},{24,32},{32,40},{40,48},{48,56},{56,64},{64,7... | collective-permute-start | bytes 49928 | tf_op jit(solution)/shard_map/ppermute | solution.py:24
  204.5 43.4 %collective-permute-start.2 = (bf16[1,65,128]{2,0,1:T(2,128)(2,1)S(1)}, bf16[1,65,128]{2,0,1:T(2,128)(2,1)S(1)}, u32[]{:S(2)}, u32[]{:S(2)}) collective-permute-start(bf16[1,65,128]{2,0,1:T(2,128)(2,1)S(1)} %get-tuple-element.21), channel_id=1, source_target_pairs={{0,16},{8,24},{16,32},{24,40},{32,48},{40,56},{48,64},{56,72},{64,... | collective-permute-start | bytes 49928 | tf_op jit(solution)/shard_map/ppermute | solution.py:24
  240.5 10.7 %collective-permute-start.3 = (bf16[1,65,128]{2,0,1:T(2,128)(2,1)S(1)}, bf16[1,65,128]{2,0,1:T(2,128)(2,1)S(1)}, u32[]{:S(2)}, u32[]{:S(2)}) collective-permute-start(bf16[1,65,128]{2,0,1:T(2,128)(2,1)S(1)} %get-tuple-element.22), channel_id=1, source_target_pairs={{0,24},{8,32},{16,40},{24,48},{32,56},{40,64},{48,72},{56,80},{64,... | collective-permute-start | bytes 49928 | tf_op jit(solution)/shard_map/ppermute | solution.py:24
  243.6 7.6 %collective-permute-start.4 = (bf16[1,65,128]{2,0,1:T(2,128)(2,1)S(1)}, bf16[1,65,128]{2,0,1:T(2,128)(2,1)S(1)}, u32[]{:S(2)}, u32[]{:S(2)}) collective-permute-start(bf16[1,65,128]{2,0,1:T(2,128)(2,1)S(1)} %get-tuple-element.23), channel_id=1, source_target_pairs={{0,32},{8,40},{16,48},{24,56},{32,64},{40,72},{48,80},{56,88},{64,... | collective-permute-start | bytes 49928 | tf_op jit(solution)/shard_map/ppermute | solution.py:24
  243.7 11.0 %collective-permute-start.14 = (bf16[1,65,128]{2,0,1:T(2,128)(2,1)S(1)}, bf16[1,65,128]{2,0,1:T(2,128)(2,1)S(1)}, u32[]{:S(2)}, u32[]{:S(2)}) collective-permute-start(bf16[1,65,128]{2,0,1:T(2,128)(2,1)S(1)} %get-tuple-element.24), channel_id=1, source_target_pairs={{0,112},{8,120},{16,0},{24,8},{32,16},{40,24},{48,32},{56,40},{64,... | collective-permute-start | bytes 49928 | tf_op jit(solution)/shard_map/ppermute | solution.py:24
  247.8 10.4 %collective-permute-start.5 = (bf16[1,65,128]{2,0,1:T(2,128)(2,1)S(1)}, bf16[1,65,128]{2,0,1:T(2,128)(2,1)S(1)}, u32[]{:S(2)}, u32[]{:S(2)}) collective-permute-start(bf16[1,65,128]{2,0,1:T(2,128)(2,1)S(1)} %get-tuple-element.25), channel_id=1, source_target_pairs={{0,40},{8,48},{16,56},{24,64},{32,72},{40,80},{48,88},{56,96},{64,... | collective-permute-start | bytes 49928 | tf_op jit(solution)/shard_map/ppermute | solution.py:24
  247.8 10.4 %collective-permute-start.6 = (bf16[1,65,128]{2,0,1:T(2,128)(2,1)S(1)}, bf16[1,65,128]{2,0,1:T(2,128)(2,1)S(1)}, u32[]{:S(2)}, u32[]{:S(2)}) collective-permute-start(bf16[1,65,128]{2,0,1:T(2,128)(2,1)S(1)} %get-tuple-element.26), channel_id=1, source_target_pairs={{0,48},{8,56},{16,64},{24,72},{32,80},{40,88},{48,96},{56,104},{64... | collective-permute-start | bytes 49928 | tf_op jit(solution)/shard_map/ppermute | solution.py:24
  251.3 7.0 %collective-permute-start.7 = (bf16[1,65,128]{2,0,1:T(2,128)(2,1)S(1)}, bf16[1,65,128]{2,0,1:T(2,128)(2,1)S(1)}, u32[]{:S(2)}, u32[]{:S(2)}) collective-permute-start(bf16[1,65,128]{2,0,1:T(2,128)(2,1)S(1)} %get-tuple-element.27), channel_id=1, source_target_pairs={{0,56},{8,64},{16,72},{24,80},{32,88},{40,96},{48,104},{56,112},{6... | collective-permute-start | bytes 49928 | tf_op jit(solution)/shard_map/ppermute | solution.py:24
  251.3 7.0 %collective-permute-start.8 = (bf16[1,65,128]{2,0,1:T(2,128)(2,1)S(1)}, bf16[1,65,128]{2,0,1:T(2,128)(2,1)S(1)}, u32[]{:S(2)}, u32[]{:S(2)}) collective-permute-start(bf16[1,65,128]{2,0,1:T(2,128)(2,1)S(1)} %get-tuple-element.28), channel_id=1, source_target_pairs={{0,64},{8,72},{16,80},{24,88},{32,96},{40,104},{48,112},{56,120},{... | collective-permute-start | bytes 49928 | tf_op jit(solution)/shard_map/ppermute | solution.py:24
  254.7 4.8 %collective-permute-start.9 = (bf16[1,65,128]{2,0,1:T(2,128)(2,1)S(1)}, bf16[1,65,128]{2,0,1:T(2,128)(2,1)S(1)}, u32[]{:S(2)}, u32[]{:S(2)}) collective-permute-start(bf16[1,65,128]{2,0,1:T(2,128)(2,1)S(1)} %get-tuple-element.29), channel_id=1, source_target_pairs={{0,72},{8,80},{16,88},{24,96},{32,104},{40,112},{48,120},{56,0},{6... | collective-permute-start | bytes 49928 | tf_op jit(solution)/shard_map/ppermute | solution.py:24
  (5 other events, 15.0 us)
Sparse Core Ops, SparseCore 0:
  11.1 49.6 all-gather.2
  63.2 45.0 all-gather.4
  127.3 60.7 reduce-scatter.4
  190.4 52.3 reduce-scatter.2

commit v10 on v9

--- a/solution.py
+++ b/solution.py
@@ -58,15 +58,15 @@
     def _():
         scores = lax.dot_general(
             q_ref[...], k_ref[...], (((1,), (1,)), ((), ())), preferred_element_type=jnp.float32
-        ) * (1.0 / math.sqrt(head_size))
-        key_index = key_first + lax.broadcasted_iota(jnp.int32, (rows, k_rows), 1)
-        query_index = query_first + lax.broadcasted_iota(jnp.int32, (rows, k_rows), 0) % q_rows
-        keep = (key_index >= qs_ref[...]) & (key_index <= query_index)
-        keep = keep & (query_index - key_index < W)
-        masked = jnp.where(keep, scores, -1e30)
+        )
+        column = lax.broadcasted_iota(jnp.int32, (1, k_rows), 1)
+        row_ahead = (query_first - key_first) + lax.broadcasted_iota(jnp.int32, (rows, 1), 0) % q_rows
+        ahead = (row_ahead - column).astype(jnp.uint32)
+        keep = (ahead < jnp.uint32(W)) & (column >= qs_ref[...] - key_first)
+        masked = jnp.where(keep, scores, -jnp.inf)
         best = m_sc[...]
         new_best = jnp.maximum(best, jnp.max(masked, axis=1, keepdims=True))
-        weights = jnp.where(keep, jnp.exp(masked - new_best), 0.0)
+        weights = jnp.exp(masked - new_best)
         factor = jnp.exp(best - new_best)
         l_sc[...] = l_sc[...] * factor + jnp.sum(weights, axis=1, keepdims=True)
         mixed = jnp.dot(weights.astype(jnp.bfloat16), v_ref[...], preferred_element_type=jnp.float32)
@@ -84,7 +84,8 @@
     k_rows = 2 * q_rows
     blocks = tokens // q_rows
     steps = (W + q_rows) // k_rows + 1
-    stacked = queries.reshape(blocks, q_rows, heads, head_size).transpose(0, 2, 1, 3)
+    scaled = queries * jnp.asarray(1.0 / math.sqrt(head_size), queries.dtype)
+    stacked = scaled.reshape(blocks, q_rows, heads, head_size).transpose(0, 2, 1, 3)
     stacked = stacked.reshape(blocks * heads * q_rows, head_size)
     starts = jnp.broadcast_to(
         query_start.reshape(blocks, 1, q_rows), (blocks, heads, q_rows)

time: 273 us -> 263 us (0.963)
  Pallas kernels: 79.6 us -> 72.1 us
  starting transfers between devices: 51.1 us -> 44.2 us
    pallas_call x2, Pallas kernels: 79.6 us -> 72.1 us  [flash_attention(): pl.pallas_call(functools.partial(flash_kernel, q_rows, tokens, first_bloc...]
    ppermute x15, starting transfers between devices: 47.4 us -> 40.4 us  [shift_round(): return lax.ppermute(x, axis, [(i, (i + by) % peers) for i in range(peers)])]
  transfers between devices with their start and end apart: 20 -> 20, of which waited for: 3 -> 3; matrix products, arithmetic and copies ran while one was open for 17% -> 18% of each run, Pallas kernels for 29% -> 28%
where the time goes in v10:
time: 263 us; the launch traced here: 260 us
  Pallas kernels  72.1 us (27%)
  waiting for transfers between devices  58.8 us (22%)
  starting transfers between devices  44.2 us (17%)
  local copies, waits for them, and re-layouts  20.2 us (8%)
  matrix products  18.5 us (7%)
  other arithmetic  17.9 us (7%)
  between operations  14.1 us (5%)
  blocking collectives  13.7 us (5%)
    pallas_call x2, Pallas kernels, flash_attention(): pl.pallas_call(functools.partial(flash_kernel, q_rows, tokens, first_bloc...  72.1 us
    ppermute x15, starting transfers between devices, shift_round(): return lax.ppermute(x, axis, [(i, (i + by) % peers) for i in range(peers)])  40.4 us
    ppermute x15, waiting for transfers between devices, shift_round(): return lax.ppermute(x, axis, [(i, (i + by) % peers) for i in range(peers)])  38.7 us
    all_gather x1, waiting for transfers between devices, body(): lax.all_gather(jnp.concatenate([kv_own, q_weight], axis=1), 'seq', axis=0...  19.3 us
    psum x1, blocking collectives, body(): seg_total = lax.psum(seg_hist, 'seq')  13.7 us
    dot_general x2, matrix products, body(): lax.dot_general(attended, w_output, (((1,), (1,)), ((), ())), preferred_e...  7.78 us
    dot_general x1, matrix products, body(): jnp.dot(normed, w_inputs[:, kv_columns:], preferred_element_type=jnp.floa...  5.3 us
    reshape x1, local copies, waits for them, and re-layouts, flash_attention(): starts = jnp.broadcast_to(query_start.reshape(blocks, 1, q_rows), (blocks...  5.29 us
  transfers between devices with their start and end apart: 20, of which 3 were waited for; matrix products, arithmetic and copies ran while one was open for 18% of the time, Pallas kernels for 28%

profile of v10, /device:TPU:1, one launch (start us, length us, event | category | flops | bytes accessed | tf_op | source)
XLA Modules:
  0.0 259.6 jit_solution(498447912578988599)
XLA Ops:
  11.2 13.7 %psum.7 = s32[32]{0:T(128)S(1)} all-reduce(s32[32]{0:T(128)S(1)} %convert_reduce_fusion), channel_id=1, replica_groups=mesh['seq'=16,'mp'=8] {'seq'}, use_global_device_ids=true, to_apply=%region_1.2 | all-reduce | flops 32 | bytes 256 | tf_op jit(solution)/shard_map/psum | solution.py:151
  25.0 5.1 %fusion = f32[2048]{0:T(1024)S(1)} fusion(bf16[2048,2048]{1,0:T(8,128)(2,1)} %param.7), kind=kLoop, calls=%fused_computation.2 | loop fusion | flops 12580864 | bytes 8396800 | tf_op jit(solution)/shard_map/reduce_sum | solution.py:145
  30.5 3.7 %multiply_sine_fusion = (f32[2048,32]{1,0:T(8,128)S(1)}, f32[2048,32]{1,0:T(8,128)S(1)}) fusion(f32[32]{0:T(128)S(1)} %multiply_exponential_fusion, f32[2048]{0:T(1024)S(1)} %subtract_convert_fusion.2), kind=kLoop, calls=%fused_computation.24 | loop fusion | flops 65536 | bytes 532608 | tf_op jit(solution)/shard_map/sin | solution.py:160
  36.1 5.3 %reshape.134.qs_ref = s32[8192,1]{1,0:T(8,128)} reshape(s32[8,4,256]{2,1,0:T(4,128)S(1)} %broadcast_in_dim.26) | data formatting | bytes 65536 | tf_op jit(solution)/shard_map/reshape | solution.py:92
  41.4 19.3 %all-gather.3.cloned.1.call-done = bf16[2048,384]{1,0:T(8,128)(2,1)} async-done(((bf16[128,384]{1,0:T(8,128)(2,1)}), bf16[2048,384]{1,0:T(8,128)(2,1)}) %all-gather.3.cloned.1.call-update) | async-done | bytes 1572880 | tf_op jit(solution)/shard_map/all_gather | solution.py:140
  60.8 4.9 %fusion.3 = f32[2048,128]{1,0:T(8,128)S(1)} fusion(bf16[2048,2048]{1,0:T(8,128)(2,1)} %param.7, f32[2048]{0:T(1024)S(1)} %copy-done.7, f32[2048]{0:T(1024)S(1)} %add_rsqrt_fusion, bf16[2048,384]{1,0:T(8,128)(2,1)} %all-gather.3.cloned.1.call-done), kind=kOutput, calls=%fused_computation.7 | convolution fusion | flops 1090519040 | bytes 9977856 | tf_op jit(solution)/shard_map/dot_general | solution.py:162
  68.0 3.4 %collective-permute-start = (bf16[2048,128]{1,0:T(8,128)(2,1)}, bf16[2048,128]{1,0:T(8,128)(2,1)S(1)}, u32[]{:S(2)}, u32[]{:S(2)}) collective-permute-start(bf16[2048,128]{1,0:T(8,128)(2,1)} %pad_maximum_fusion.1), channel_id=1, source_target_pairs={{0,8},{8,16},{16,24},{24,32},{32,40},{40,48},{48,56},{56,64},{64,7... | collective-permute-start | bytes 1572872 | tf_op jit(solution)/shard_map/ppermute | solution.py:19
  71.4 5.3 %fusion.5 = f32[2048,256]{0,1:T(8,128)S(1)} fusion(bf16[2048,2048]{1,0:T(8,128)(2,1)} %param.7, f32[2048]{0:T(1024)S(1)} %copy-done.7, f32[2048]{0:T(1024)S(1)} %add_rsqrt_fusion, bf16[2048,384]{1,0:T(8,128)(2,1)S(1)} %copy-done.6), kind=kOutput, calls=%fused_computation.8 | convolution fusion | flops 2164260864 | bytes 11550720 | tf_op jit(solution)/shard_map/dot_general | solution.py:167
  77.4 2.0 copy.32
  79.9 1.7 fusion.38
  81.6 35.8 %shard_map.87 = bf16[4096,64]{1,0:T(8,128)(2,1)} custom-call(s32[1]{0:T(128)} %bitcast.first_ref, s32[8]{0:T(128)} %reduce_min.8.lowest_ref, bf16[8192,64]{1,0:T(8,128)(2,1)} %bitcast.48, bf16[4096,64]{1,0:T(8,128)(2,1)} %get-tuple-element.17.k_ref, bf16[4096,64]{1,0:T(8,128)(2,1)} %get-tuple-element.16.v_ref, s32[8192,1]{1,0:T(8,128)} %reshape.134.qs_ref), custom_call_target="tpu_custom_call" | custom-call | tf_op jit(solution)/shard_map/pallas_call | solution.py:99
  119.0 4.5 %convolution_convert_fusion = bf16[1024,2048]{1,0:T(8,128)(2,1)} fusion(bf16[1024,256]{0,1:T(8,128)(2,1)S(1)} %bitcast.52, bf16[2048,256]{1,0:T(8,128)(2,1)} %all-gather.5.cloned.1.call-done), kind=kOutput, calls=%fused_computation.5 | convolution fusion | flops 1075838976 | bytes 5767168 | tf_op jit(solution)/shard_map/dot_general | solution.py:184
  123.8 36.4 %shard_map.86 = bf16[4096,64]{1,0:T(8,128)(2,1)} custom-call(s32[1]{0:T(128)} %bitcast.first_ref, s32[8]{0:T(128)} %reduce_min.8.lowest_ref, bf16[8192,64]{1,0:T(8,128)(2,1)} %bitcast.49, bf16[4096,64]{1,0:T(8,128)(2,1)} %get-tuple-element.17.k_ref, bf16[4096,64]{1,0:T(8,128)(2,1)} %get-tuple-element.16.v_ref, s32[8192,1]{1,0:T(8,128)} %reshape.134.qs_ref), custom_call_target="tpu_custom_call" | custom-call | tf_op jit(solution)/shard_map/pallas_call | solution.py:99
  161.9 3.3 %convolution_convert_fusion.1 = bf16[1024,2048]{1,0:T(8,128)(2,1)} fusion(bf16[1024,256]{0,1:T(8,128)(2,1)S(1)} %bitcast.53, bf16[2048,256]{1,0:T(8,128)(2,1)S(1)} %copy-done.3), kind=kOutput, calls=%fused_computation.6 | convolution fusion | flops 1075838976 | bytes 5767168 | tf_op jit(solution)/shard_map/dot_general | solution.py:184
  167.5 10.7 %collective-permute-start.13 = (bf16[1,65,128]{2,0,1:T(2,128)(2,1)S(1)}, bf16[1,65,128]{2,0,1:T(2,128)(2,1)S(1)}, u32[]{:S(2)}, u32[]{:S(2)}) collective-permute-start(bf16[1,65,128]{2,0,1:T(2,128)(2,1)S(1)} %get-tuple-element.30), channel_id=1, source_target_pairs={{0,104},{8,112},{16,120},{24,0},{32,8},{40,16},{48,24},{56,32},{64... | collective-permute-start | bytes 49928 | tf_op jit(solution)/shard_map/ppermute | solution.py:24
  178.2 5.3 %collective-permute-start.10 = (bf16[1,65,128]{2,0,1:T(2,128)(2,1)S(1)}, bf16[1,65,128]{2,0,1:T(2,128)(2,1)S(1)}, u32[]{:S(2)}, u32[]{:S(2)}) collective-permute-start(bf16[1,65,128]{2,0,1:T(2,128)(2,1)S(1)} %get-tuple-element.31), channel_id=1, source_target_pairs={{0,80},{8,88},{16,96},{24,104},{32,112},{40,120},{48,0},{56,8},{64... | collective-permute-start | bytes 49928 | tf_op jit(solution)/shard_map/ppermute | solution.py:24
  183.5 3.3 %collective-permute-start.11 = (bf16[1,65,128]{2,0,1:T(2,128)(2,1)S(1)}, bf16[1,65,128]{2,0,1:T(2,128)(2,1)S(1)}, u32[]{:S(2)}, u32[]{:S(2)}) collective-permute-start(bf16[1,65,128]{2,0,1:T(2,128)(2,1)S(1)} %get-tuple-element.32), channel_id=1, source_target_pairs={{0,88},{8,96},{16,104},{24,112},{32,120},{40,0},{48,8},{56,16},{64... | collective-permute-start | bytes 49928 | tf_op jit(solution)/shard_map/ppermute | solution.py:24
  189.8 5.1 %collective-permute-start.3 = (bf16[1,65,128]{2,0,1:T(2,128)(2,1)S(1)}, bf16[1,65,128]{2,0,1:T(2,128)(2,1)S(1)}, u32[]{:S(2)}, u32[]{:S(2)}) collective-permute-start(bf16[1,65,128]{2,0,1:T(2,128)(2,1)S(1)} %get-tuple-element.22), channel_id=1, source_target_pairs={{0,24},{8,32},{16,40},{24,48},{32,56},{40,64},{48,72},{56,80},{64,... | collective-permute-start | bytes 49928 | tf_op jit(solution)/shard_map/ppermute | solution.py:24
  196.2 4.5 %collective-permute-start.14 = (bf16[1,65,128]{2,0,1:T(2,128)(2,1)S(1)}, bf16[1,65,128]{2,0,1:T(2,128)(2,1)S(1)}, u32[]{:S(2)}, u32[]{:S(2)}) collective-permute-start(bf16[1,65,128]{2,0,1:T(2,128)(2,1)S(1)} %get-tuple-element.24), channel_id=1, source_target_pairs={{0,112},{8,120},{16,0},{24,8},{32,16},{40,24},{48,32},{56,40},{64,... | collective-permute-start | bytes 49928 | tf_op jit(solution)/shard_map/ppermute | solution.py:24
  200.8 2.6 collective-permute-start.7
  203.4 37.7 %collective-permute-done.4 = bf16[1,65,128]{2,0,1:T(2,128)(2,1)S(1)} collective-permute-done((bf16[1,65,128]{2,0,1:T(2,128)(2,1)S(1)}, bf16[1,65,128]{2,0,1:T(2,128)(2,1)S(1)}, u32[]{:S(2)}, u32[]{:S(2)}) %collective-permute-start.4) | collective-permute-done | bytes 16672 | tf_op jit(solution)/shard_map/ppermute | solution.py:24
  241.7 4.3 %collective-permute-start.9 = (bf16[1,65,128]{2,0,1:T(2,128)(2,1)S(1)}, bf16[1,65,128]{2,0,1:T(2,128)(2,1)S(1)}, u32[]{:S(2)}, u32[]{:S(2)}) collective-permute-start(bf16[1,65,128]{2,0,1:T(2,128)(2,1)S(1)} %get-tuple-element.29), channel_id=1, source_target_pairs={{0,72},{8,80},{16,88},{24,96},{32,104},{40,112},{48,120},{56,0},{6... | collective-permute-start | bytes 49928 | tf_op jit(solution)/shard_map/ppermute | solution.py:24
  247.0 2.6 %concatenate.38 = bf16[16,65,128]{2,0,1:T(8,128)(2,1)S(1)} concatenate(bf16[1,65,128]{2,0,1:T(2,128)(2,1)S(1)} %get-tuple-element.19, bf16[1,65,128]{2,0,1:T(2,128)(2,1)S(1)} %collective-permute-done.1, bf16[1,65,128]{2,0,1:T(2,128)(2,1)S(1)} %collective-permute-done.2, bf16[1,65,128]{2,0,1:T(2,128)(2,1)S(1)} %collective-permute-done.3, ...), dimensions={0} | concatenate | bytes 532480 | tf_op jit(solution)/shard_map/concatenate | solution.py:216
  250.8 2.2 pad_maximum_fusion
  (96 shorter events, 22.9 us)
Async XLA Ops:
  7.2 23.2 %copy-start.5 = (s32[2048]{0:T(1024)S(1)}, s32[2048]{0:T(1024)}, u32[]{:S(2)}) copy-start(s32[2048]{0:T(1024)} %param.12) | copy-start | bytes 24580
  7.2 53.6 %all-gather.3.cloned.1.call-start = ((), (), s32[]{:S(2)}) async-start(), calls=%async_computation.2 | async-start | bytes 1671168 | tf_op jit(solution)/shard_map/all_gather | solution.py:140
  9.6 109.4 %all-gather.5.cloned.1.call-start = ((), (), s32[]{:S(2)}) async-start(), calls=%async_computation.3 | async-start | bytes 1114112 | tf_op jit(solution)/shard_map/all_gather | solution.py:143
  10.3 240.4 %reduce-scatter.5.cloned.1.call-start = ((), (), s32[]{:S(2)}) async-start(), calls=%async_computation.5 | async-start | bytes 4718592 | tf_op jit(solution)/shard_map/reduce_scatter | solution.py:188
  25.0 35.8 %copy-start.7 = (f32[2048]{0:T(1024)S(1)}, f32[2048]{0:T(1024)}, u32[]{:S(2)}) copy-start(f32[2048]{0:T(1024)} %param.8) | copy-start | bytes 24580
  68.0 8.7 %copy-start.4 = (f32[2048,32]{0,1:T(8,128)S(1)}, f32[2048,32]{0,1:T(8,128)}, u32[]{:S(2)}) copy-start(f32[2048,32]{0,1:T(8,128)} %copy.31) | copy-start | bytes 786436
  68.0 11.4 %collective-permute-start = (bf16[2048,128]{1,0:T(8,128)(2,1)}, bf16[2048,128]{1,0:T(8,128)(2,1)S(1)}, u32[]{:S(2)}, u32[]{:S(2)}) collective-permute-start(bf16[2048,128]{1,0:T(8,128)(2,1)} %pad_maximum_fusion.1), channel_id=1, source_target_pairs={{0,8},{8,16},{16,24},{24,32},{32,40},{40,48},{48,56},{56,64},{64,7... | collective-permute-start | bytes 1572872 | tf_op jit(solution)/shard_map/ppermute | solution.py:19
  123.5 38.3 %copy-start.3 = (bf16[2048,256]{1,0:T(8,128)(2,1)S(1)}, bf16[2048,256]{1,0:T(8,128)(2,1)}, u32[]{:S(2)}) copy-start(bf16[2048,256]{1,0:T(8,128)(2,1)} %all-gather.5.cloned.1.call-done) | copy-start | bytes 3145732
  123.5 127.2 %reduce-scatter.3.cloned.1.call-start = ((), (), s32[]{:S(2)}) async-start(), calls=%async_computation.4 | async-start | bytes 4718592 | tf_op jit(solution)/shard_map/reduce_scatter | solution.py:188
  167.5 20.0 %collective-permute-start.13 = (bf16[1,65,128]{2,0,1:T(2,128)(2,1)S(1)}, bf16[1,65,128]{2,0,1:T(2,128)(2,1)S(1)}, u32[]{:S(2)}, u32[]{:S(2)}) collective-permute-start(bf16[1,65,128]{2,0,1:T(2,128)(2,1)S(1)} %get-tuple-element.30), channel_id=1, source_target_pairs={{0,104},{8,112},{16,120},{24,0},{32,8},{40,16},{48,24},{56,32},{64... | collective-permute-start | bytes 49928 | tf_op jit(solution)/shard_map/ppermute | solution.py:24
  178.2 10.8 %collective-permute-start.10 = (bf16[1,65,128]{2,0,1:T(2,128)(2,1)S(1)}, bf16[1,65,128]{2,0,1:T(2,128)(2,1)S(1)}, u32[]{:S(2)}, u32[]{:S(2)}) collective-permute-start(bf16[1,65,128]{2,0,1:T(2,128)(2,1)S(1)} %get-tuple-element.31), channel_id=1, source_target_pairs={{0,80},{8,88},{16,96},{24,104},{32,112},{40,120},{48,0},{56,8},{64... | collective-permute-start | bytes 49928 | tf_op jit(solution)/shard_map/ppermute | solution.py:24
  183.5 6.3 %collective-permute-start.11 = (bf16[1,65,128]{2,0,1:T(2,128)(2,1)S(1)}, bf16[1,65,128]{2,0,1:T(2,128)(2,1)S(1)}, u32[]{:S(2)}, u32[]{:S(2)}) collective-permute-start(bf16[1,65,128]{2,0,1:T(2,128)(2,1)S(1)} %get-tuple-element.32), channel_id=1, source_target_pairs={{0,88},{8,96},{16,104},{24,112},{32,120},{40,0},{48,8},{56,16},{64... | collective-permute-start | bytes 49928 | tf_op jit(solution)/shard_map/ppermute | solution.py:24
  186.8 8.2 %collective-permute-start.12 = (bf16[1,65,128]{2,0,1:T(2,128)(2,1)S(1)}, bf16[1,65,128]{2,0,1:T(2,128)(2,1)S(1)}, u32[]{:S(2)}, u32[]{:S(2)}) collective-permute-start(bf16[1,65,128]{2,0,1:T(2,128)(2,1)S(1)} %get-tuple-element.33), channel_id=1, source_target_pairs={{0,96},{8,104},{16,112},{24,120},{32,0},{40,8},{48,16},{56,24},{64... | collective-permute-start | bytes 49928 | tf_op jit(solution)/shard_map/ppermute | solution.py:24
  186.9 9.3 %collective-permute-start.15 = (bf16[1,65,128]{2,0,1:T(2,128)(2,1)S(1)}, bf16[1,65,128]{2,0,1:T(2,128)(2,1)S(1)}, u32[]{:S(2)}, u32[]{:S(2)}) collective-permute-start(bf16[1,65,128]{2,0,1:T(2,128)(2,1)S(1)} %get-tuple-element.18), channel_id=1, source_target_pairs={{0,120},{8,0},{16,8},{24,16},{32,24},{40,32},{48,40},{56,48},{64,5... | collective-permute-start | bytes 49928 | tf_op jit(solution)/shard_map/ppermute | solution.py:24
  187.6 13.1 %collective-permute-start.1 = (bf16[1,65,128]{2,0,1:T(2,128)(2,1)S(1)}, bf16[1,65,128]{2,0,1:T(2,128)(2,1)S(1)}, u32[]{:S(2)}, u32[]{:S(2)}) collective-permute-start(bf16[1,65,128]{2,0,1:T(2,128)(2,1)S(1)} %get-tuple-element.20), channel_id=1, source_target_pairs={{0,8},{8,16},{16,24},{24,32},{32,40},{40,48},{48,56},{56,64},{64,7... | collective-permute-start | bytes 49928 | tf_op jit(solution)/shard_map/ppermute | solution.py:24
  189.0 11.7 %collective-permute-start.2 = (bf16[1,65,128]{2,0,1:T(2,128)(2,1)S(1)}, bf16[1,65,128]{2,0,1:T(2,128)(2,1)S(1)}, u32[]{:S(2)}, u32[]{:S(2)}) collective-permute-start(bf16[1,65,128]{2,0,1:T(2,128)(2,1)S(1)} %get-tuple-element.21), channel_id=1, source_target_pairs={{0,16},{8,24},{16,32},{24,40},{32,48},{40,56},{48,64},{56,72},{64,... | collective-permute-start | bytes 49928 | tf_op jit(solution)/shard_map/ppermute | solution.py:24
  189.8 11.0 %collective-permute-start.3 = (bf16[1,65,128]{2,0,1:T(2,128)(2,1)S(1)}, bf16[1,65,128]{2,0,1:T(2,128)(2,1)S(1)}, u32[]{:S(2)}, u32[]{:S(2)}) collective-permute-start(bf16[1,65,128]{2,0,1:T(2,128)(2,1)S(1)} %get-tuple-element.22), channel_id=1, source_target_pairs={{0,24},{8,32},{16,40},{24,48},{32,56},{40,64},{48,72},{56,80},{64,... | collective-permute-start | bytes 49928 | tf_op jit(solution)/shard_map/ppermute | solution.py:24
  194.9 46.1 %collective-permute-start.4 = (bf16[1,65,128]{2,0,1:T(2,128)(2,1)S(1)}, bf16[1,65,128]{2,0,1:T(2,128)(2,1)S(1)}, u32[]{:S(2)}, u32[]{:S(2)}) collective-permute-start(bf16[1,65,128]{2,0,1:T(2,128)(2,1)S(1)} %get-tuple-element.23), channel_id=1, source_target_pairs={{0,32},{8,40},{16,48},{24,56},{32,64},{40,72},{48,80},{56,88},{64,... | collective-permute-start | bytes 49928 | tf_op jit(solution)/shard_map/ppermute | solution.py:24
  196.2 45.4 %collective-permute-start.14 = (bf16[1,65,128]{2,0,1:T(2,128)(2,1)S(1)}, bf16[1,65,128]{2,0,1:T(2,128)(2,1)S(1)}, u32[]{:S(2)}, u32[]{:S(2)}) collective-permute-start(bf16[1,65,128]{2,0,1:T(2,128)(2,1)S(1)} %get-tuple-element.24), channel_id=1, source_target_pairs={{0,112},{8,120},{16,0},{24,8},{32,16},{40,24},{48,32},{56,40},{64,... | collective-permute-start | bytes 49928 | tf_op jit(solution)/shard_map/ppermute | solution.py:24
  200.7 45.3 %collective-permute-start.5 = (bf16[1,65,128]{2,0,1:T(2,128)(2,1)S(1)}, bf16[1,65,128]{2,0,1:T(2,128)(2,1)S(1)}, u32[]{:S(2)}, u32[]{:S(2)}) collective-permute-start(bf16[1,65,128]{2,0,1:T(2,128)(2,1)S(1)} %get-tuple-element.25), channel_id=1, source_target_pairs={{0,40},{8,48},{16,56},{24,64},{32,72},{40,80},{48,88},{56,96},{64,... | collective-permute-start | bytes 49928 | tf_op jit(solution)/shard_map/ppermute | solution.py:24
  200.7 45.3 %collective-permute-start.6 = (bf16[1,65,128]{2,0,1:T(2,128)(2,1)S(1)}, bf16[1,65,128]{2,0,1:T(2,128)(2,1)S(1)}, u32[]{:S(2)}, u32[]{:S(2)}) collective-permute-start(bf16[1,65,128]{2,0,1:T(2,128)(2,1)S(1)} %get-tuple-element.26), channel_id=1, source_target_pairs={{0,48},{8,56},{16,64},{24,72},{32,80},{40,88},{48,96},{56,104},{64... | collective-permute-start | bytes 49928 | tf_op jit(solution)/shard_map/ppermute | solution.py:24
  200.8 45.2 %collective-permute-start.7 = (bf16[1,65,128]{2,0,1:T(2,128)(2,1)S(1)}, bf16[1,65,128]{2,0,1:T(2,128)(2,1)S(1)}, u32[]{:S(2)}, u32[]{:S(2)}) collective-permute-start(bf16[1,65,128]{2,0,1:T(2,128)(2,1)S(1)} %get-tuple-element.27), channel_id=1, source_target_pairs={{0,56},{8,64},{16,72},{24,80},{32,88},{40,96},{48,104},{56,112},{6... | collective-permute-start | bytes 49928 | tf_op jit(solution)/shard_map/ppermute | solution.py:24
  241.0 4.9 %collective-permute-start.8 = (bf16[1,65,128]{2,0,1:T(2,128)(2,1)S(1)}, bf16[1,65,128]{2,0,1:T(2,128)(2,1)S(1)}, u32[]{:S(2)}, u32[]{:S(2)}) collective-permute-start(bf16[1,65,128]{2,0,1:T(2,128)(2,1)S(1)} %get-tuple-element.28), channel_id=1, source_target_pairs={{0,64},{8,72},{16,80},{24,88},{32,96},{40,104},{48,112},{56,120},{... | collective-permute-start | bytes 49928 | tf_op jit(solution)/shard_map/ppermute | solution.py:24
  241.7 5.3 %collective-permute-start.9 = (bf16[1,65,128]{2,0,1:T(2,128)(2,1)S(1)}, bf16[1,65,128]{2,0,1:T(2,128)(2,1)S(1)}, u32[]{:S(2)}, u32[]{:S(2)}) collective-permute-start(bf16[1,65,128]{2,0,1:T(2,128)(2,1)S(1)} %get-tuple-element.29), channel_id=1, source_target_pairs={{0,72},{8,80},{16,88},{24,96},{32,104},{40,112},{48,120},{56,0},{6... | collective-permute-start | bytes 49928 | tf_op jit(solution)/shard_map/ppermute | solution.py:24
  (5 other events, 15.1 us)
Sparse Core Ops, SparseCore 0:
  11.1 49.6 all-gather.2
  63.2 45.0 all-gather.4
  123.7 59.6 reduce-scatter.4
  185.6 51.8 reduce-scatter.2

commit v11 on v10

--- a/solution.py
+++ b/solution.py
@@ -34,7 +34,7 @@
     )
 
 
-def flash_kernel(q_rows, tokens, first_block, first_ref, lowest_ref, q_ref, k_ref, v_ref, qs_ref, o_ref, m_sc, l_sc, acc_sc):
+def flash_kernel(q_rows, tokens, first_block, first_ref, lowest_ref, q_ref, k_ref, v_ref, qs_ref, o_ref, m_sc, acc_sc):
     block = pl.program_id(0) + first_block
     step = pl.program_id(1)
     rows = q_ref.shape[0]
@@ -44,7 +44,6 @@
     @pl.when(step == 0)
     def _():
         m_sc[...] = jnp.full(m_sc.shape, -1e30, jnp.float32)
-        l_sc[...] = jnp.zeros(l_sc.shape, jnp.float32)
         acc_sc[...] = jnp.zeros(acc_sc.shape, jnp.float32)
 
     token_first = first_ref[0]
@@ -68,14 +67,15 @@
         new_best = jnp.maximum(best, jnp.max(masked, axis=1, keepdims=True))
         weights = jnp.exp(masked - new_best)
         factor = jnp.exp(best - new_best)
-        l_sc[...] = l_sc[...] * factor + jnp.sum(weights, axis=1, keepdims=True)
         mixed = jnp.dot(weights.astype(jnp.bfloat16), v_ref[...], preferred_element_type=jnp.float32)
         acc_sc[...] = acc_sc[...] * factor + mixed
         m_sc[...] = new_best
 
     @pl.when(step == pl.num_programs(1) - 1)
     def _():
-        o_ref[...] = (acc_sc[...] / l_sc[...]).astype(o_ref.dtype)
+        head_size = o_ref.shape[1]
+        totals = acc_sc[:, head_size:head_size + 1]
+        o_ref[...] = (acc_sc[:, :head_size] / totals).astype(o_ref.dtype)
 
 
 def flash_attention(queries, keys, values, query_start, token_first, first_block, count):
@@ -92,6 +92,8 @@
     ).reshape(blocks * heads * q_rows, 1)
     lowest = jnp.min(query_start.reshape(blocks, q_rows), axis=1)
     rows = heads * q_rows
+    counted = jnp.zeros((values.shape[0], head_size), values.dtype).at[:, 0].set(1)
+    values = jnp.concatenate([values, counted], axis=1)
 
     def kv_map(i, j, first, low):
         return ((i + first_block) * q_rows // k_rows + j, 0)
@@ -104,14 +106,13 @@
             in_specs=[
                 pl.BlockSpec((rows, head_size), lambda i, j, first, low: (i + first_block, 0)),
                 pl.BlockSpec((k_rows, head_size), kv_map),
-                pl.BlockSpec((k_rows, head_size), kv_map),
+                pl.BlockSpec((k_rows, 2 * head_size), kv_map),
                 pl.BlockSpec((rows, 1), lambda i, j, first, low: (i + first_block, 0)),
             ],
             out_specs=pl.BlockSpec((rows, head_size), lambda i, j, first, low: (i, 0)),
             scratch_shapes=[
                 pltpu.VMEM((rows, 1), jnp.float32),
-                pltpu.VMEM((rows, 1), jnp.float32),
-                pltpu.VMEM((rows, head_size), jnp.float32),
+                pltpu.VMEM((rows, 2 * head_size), jnp.float32),
             ],
         ),
         out_shape=jax.ShapeDtypeStruct((count * rows, head_size), jnp.bfloat16),

time: 263 us -> 268 us (1.019)
  starting transfers between devices: 44.2 us -> 100 us
  waiting for transfers between devices: 58.8 us -> 19.8 us
  Pallas kernels: 72.1 us -> 58.5 us
    ppermute x15, starting transfers between devices: 40.4 us -> 96.4 us  [shift_round(): return lax.ppermute(x, axis, [(i, (i + by) % peers) for i in range(peers)])]
    ppermute x15, waiting for transfers between devices: 38.7 us -> 1.21 us  [shift_round(): return lax.ppermute(x, axis, [(i, (i + by) % peers) for i in range(peers)])]
    pallas_call x2, Pallas kernels: 72.1 us -> 58.5 us  [flash_attention(): pl.pallas_call(functools.partial(flash_kernel, q_rows, tokens, first_bloc...]
  transfers between devices with their start and end apart: 20 -> 20, of which waited for: 3 -> 3; matrix products, arithmetic and copies ran while one was open for 18% -> 18% of each run, Pallas kernels for 28% -> 22%
where the time goes in v11:
time: 268 us; the launch traced here: 266 us
  starting transfers between devices  100 us (37%)
  Pallas kernels  58.5 us (22%)
  local copies, waits for them, and re-layouts  20.5 us (8%)
  other arithmetic  20 us (7%)
  waiting for transfers between devices  19.8 us (7%)
  matrix products  18.5 us (7%)
  between operations  14.8 us (6%)
  blocking collectives  13.7 us (5%)
    ppermute x15, starting transfers between devices, shift_round(): return lax.ppermute(x, axis, [(i, (i + by) % peers) for i in range(peers)])  96.4 us
    pallas_call x2, Pallas kernels, flash_attention(): pl.pallas_call(functools.partial(flash_kernel, q_rows, tokens, first_bloc...  58.5 us
    all_gather x1, waiting for transfers between devices, body(): lax.all_gather(jnp.concatenate([kv_own, q_weight], axis=1), 'seq', axis=0...  17.8 us
    psum x1, blocking collectives, body(): seg_total = lax.psum(seg_hist, 'seq')  13.7 us
    dot_general x2, matrix products, body(): lax.dot_general(attended, w_output, (((1,), (1,)), ((), ())), preferred_e...  7.78 us
  transfers between devices with their start and end apart: 20, of which 3 were waited for; matrix products, arithmetic and copies ran while one was open for 18% of the time, Pallas kernels for 22%

profile of v11, /device:TPU:1, one launch (start us, length us, event | category | flops | bytes accessed | tf_op | source)
XLA Modules:
  0.0 266.0 jit_solution(6071128629766988362)
XLA Ops:
  12.6 13.7 %psum.7 = s32[32]{0:T(128)S(1)} all-reduce(s32[32]{0:T(128)S(1)} %convert_reduce_fusion), channel_id=1, replica_groups=mesh['seq'=16,'mp'=8] {'seq'}, use_global_device_ids=true, to_apply=%region_1.2 | all-reduce | flops 32 | bytes 256 | tf_op jit(solution)/shard_map/psum | solution.py:152
  26.3 5.1 %fusion = f32[2048]{0:T(1024)S(1)} fusion(bf16[2048,2048]{1,0:T(8,128)(2,1)} %param.11), kind=kLoop, calls=%fused_computation.2 | loop fusion | flops 12580864 | bytes 8396800 | tf_op jit(solution)/shard_map/reduce_sum | solution.py:146
  31.9 3.7 %multiply_sine_fusion = (f32[2048,32]{1,0:T(8,128)S(1)}, f32[2048,32]{1,0:T(8,128)S(1)}) fusion(f32[32]{0:T(128)S(1)} %multiply_exponential_fusion, f32[2048]{0:T(1024)S(1)} %subtract_convert_fusion.2), kind=kLoop, calls=%fused_computation.24 | loop fusion | flops 65536 | bytes 532608 | tf_op jit(solution)/shard_map/sin | solution.py:161
  37.6 5.3 %reshape.172.qs_ref = s32[8192,1]{1,0:T(8,128)} reshape(s32[8,4,256]{2,1,0:T(4,128)S(1)} %broadcast_in_dim.26) | data formatting | bytes 65536 | tf_op jit(solution)/shard_map/reshape | solution.py:92
  42.9 17.8 %all-gather.3.cloned.1.call-done = bf16[2048,384]{1,0:T(8,128)(2,1)} async-done(((bf16[128,384]{1,0:T(8,128)(2,1)}), bf16[2048,384]{1,0:T(8,128)(2,1)}) %all-gather.3.cloned.1.call-update) | async-done | bytes 1572880 | tf_op jit(solution)/shard_map/all_gather | solution.py:141
  60.8 5.0 %fusion.3 = f32[2048,128]{1,0:T(8,128)S(1)} fusion(bf16[2048,2048]{1,0:T(8,128)(2,1)} %param.11, f32[2048]{0:T(1024)S(1)} %copy-done.7, f32[2048]{0:T(1024)S(1)} %add_rsqrt_fusion, bf16[2048,384]{1,0:T(8,128)(2,1)} %all-gather.3.cloned.1.call-done), kind=kOutput, calls=%fused_computation.7 | convolution fusion | flops 1090519040 | bytes 9977856 | tf_op jit(solution)/shard_map/dot_general | solution.py:163
  68.0 3.4 %collective-permute-start = (bf16[2048,128]{1,0:T(8,128)(2,1)}, bf16[2048,128]{1,0:T(8,128)(2,1)S(1)}, u32[]{:S(2)}, u32[]{:S(2)}) collective-permute-start(bf16[2048,128]{1,0:T(8,128)(2,1)} %pad_maximum_fusion.2), channel_id=1, source_target_pairs={{0,8},{8,16},{16,24},{24,32},{32,40},{40,48},{48,56},{56,64},{64,7... | collective-permute-start | bytes 1572872 | tf_op jit(solution)/shard_map/ppermute | solution.py:19
  71.4 5.3 %fusion.5 = f32[2048,256]{0,1:T(8,128)S(1)} fusion(bf16[2048,2048]{1,0:T(8,128)(2,1)} %param.11, f32[2048]{0:T(1024)S(1)} %copy-done.8, f32[2048]{0:T(1024)S(1)} %add_rsqrt_fusion, bf16[2048,384]{1,0:T(8,128)(2,1)S(1)} %copy-done.6), kind=kOutput, calls=%fused_computation.8 | convolution fusion | flops 2164260864 | bytes 11550720 | tf_op jit(solution)/shard_map/dot_general | solution.py:168
  77.4 2.0 copy.32
  82.5 30.9 %shard_map.87 = bf16[4096,64]{1,0:T(8,128)(2,1)} custom-call(s32[1]{0:T(128)} %bitcast.first_ref, s32[8]{0:T(128)} %reduce_min.8.lowest_ref, bf16[8192,64]{1,0:T(8,128)(2,1)} %bitcast.49, bf16[4096,64]{1,0:T(8,128)(2,1)} %get-tuple-element.37.k_ref, bf16[4096,128]{1,0:T(8,128)(2,1)} %pad_maximum_fusion.v_ref, s32[8192,1]{1,0:T(8,128)} %reshape.172.qs_ref), custom_call_target="tpu_custom_call" | custom-call | tf_op jit(solution)/shard_map/pallas_call | solution.py:101
  115.1 4.5 %convolution_convert_fusion = bf16[1024,2048]{1,0:T(8,128)(2,1)} fusion(bf16[1024,256]{0,1:T(8,128)(2,1)S(1)} %bitcast.53, bf16[2048,256]{1,0:T(8,128)(2,1)} %all-gather.5.cloned.1.call-done), kind=kOutput, calls=%fused_computation.5 | convolution fusion | flops 1075838976 | bytes 5767168 | tf_op jit(solution)/shard_map/dot_general | solution.py:185
  119.9 27.6 %shard_map.86 = bf16[4096,64]{1,0:T(8,128)(2,1)} custom-call(s32[1]{0:T(128)} %bitcast.first_ref, s32[8]{0:T(128)} %reduce_min.8.lowest_ref, bf16[8192,64]{1,0:T(8,128)(2,1)} %bitcast.50, bf16[4096,64]{1,0:T(8,128)(2,1)} %get-tuple-element.37.k_ref, bf16[4096,128]{1,0:T(8,128)(2,1)} %pad_maximum_fusion.v_ref, s32[8192,1]{1,0:T(8,128)} %reshape.172.qs_ref), custom_call_target="tpu_custom_call" | custom-call | tf_op jit(solution)/shard_map/pallas_call | solution.py:101
  149.2 3.3 %convolution_convert_fusion.1 = bf16[1024,2048]{1,0:T(8,128)(2,1)} fusion(bf16[1024,256]{0,1:T(8,128)(2,1)S(1)} %bitcast.54, bf16[2048,256]{1,0:T(8,128)(2,1)S(1)} %copy-done.3), kind=kOutput, calls=%fused_computation.6 | convolution fusion | flops 1075838976 | bytes 5767168 | tf_op jit(solution)/shard_map/dot_general | solution.py:185
  155.4 7.3 %collective-permute-start.13 = (bf16[1,65,128]{2,0,1:T(2,128)(2,1)S(1)}, bf16[1,65,128]{2,0,1:T(2,128)(2,1)S(1)}, u32[]{:S(2)}, u32[]{:S(2)}) collective-permute-start(bf16[1,65,128]{2,0,1:T(2,128)(2,1)S(1)} %get-tuple-element.50), channel_id=1, source_target_pairs={{0,104},{8,112},{16,120},{24,0},{32,8},{40,16},{48,24},{56,32},{64... | collective-permute-start | bytes 49928 | tf_op jit(solution)/shard_map/ppermute | solution.py:24
  162.7 31.4 %collective-permute-start.10 = (bf16[1,65,128]{2,0,1:T(2,128)(2,1)S(1)}, bf16[1,65,128]{2,0,1:T(2,128)(2,1)S(1)}, u32[]{:S(2)}, u32[]{:S(2)}) collective-permute-start(bf16[1,65,128]{2,0,1:T(2,128)(2,1)S(1)} %get-tuple-element.51), channel_id=1, source_target_pairs={{0,80},{8,88},{16,96},{24,104},{32,112},{40,120},{48,0},{56,8},{64... | collective-permute-start | bytes 49928 | tf_op jit(solution)/shard_map/ppermute | solution.py:24
  196.1 1.8 collective-permute-start.1
  198.6 2.3 collective-permute-start.3
  201.0 4.7 %collective-permute-start.4 = (bf16[1,65,128]{2,0,1:T(2,128)(2,1)S(1)}, bf16[1,65,128]{2,0,1:T(2,128)(2,1)S(1)}, u32[]{:S(2)}, u32[]{:S(2)}) collective-permute-start(bf16[1,65,128]{2,0,1:T(2,128)(2,1)S(1)} %get-tuple-element.43), channel_id=1, source_target_pairs={{0,32},{8,40},{16,48},{24,56},{32,64},{40,72},{48,80},{56,88},{64,... | collective-permute-start | bytes 49928 | tf_op jit(solution)/shard_map/ppermute | solution.py:24
  205.7 4.5 %collective-permute-start.14 = (bf16[1,65,128]{2,0,1:T(2,128)(2,1)S(1)}, bf16[1,65,128]{2,0,1:T(2,128)(2,1)S(1)}, u32[]{:S(2)}, u32[]{:S(2)}) collective-permute-start(bf16[1,65,128]{2,0,1:T(2,128)(2,1)S(1)} %get-tuple-element.44), channel_id=1, source_target_pairs={{0,112},{8,120},{16,0},{24,8},{32,16},{40,24},{48,32},{56,40},{64,... | collective-permute-start | bytes 49928 | tf_op jit(solution)/shard_map/ppermute | solution.py:24
  210.2 35.0 %collective-permute-start.6 = (bf16[1,65,128]{2,0,1:T(2,128)(2,1)S(1)}, bf16[1,65,128]{2,0,1:T(2,128)(2,1)S(1)}, u32[]{:S(2)}, u32[]{:S(2)}) collective-permute-start(bf16[1,65,128]{2,0,1:T(2,128)(2,1)S(1)} %get-tuple-element.46), channel_id=1, source_target_pairs={{0,48},{8,56},{16,64},{24,72},{32,80},{40,88},{48,96},{56,104},{64... | collective-permute-start | bytes 49928 | tf_op jit(solution)/shard_map/ppermute | solution.py:24
  245.2 1.9 collective-permute-start.7
  248.1 4.3 %collective-permute-start.9 = (bf16[1,65,128]{2,0,1:T(2,128)(2,1)S(1)}, bf16[1,65,128]{2,0,1:T(2,128)(2,1)S(1)}, u32[]{:S(2)}, u32[]{:S(2)}) collective-permute-start(bf16[1,65,128]{2,0,1:T(2,128)(2,1)S(1)} %get-tuple-element.49), channel_id=1, source_target_pairs={{0,72},{8,80},{16,88},{24,96},{32,104},{40,112},{48,120},{56,0},{6... | collective-permute-start | bytes 49928 | tf_op jit(solution)/shard_map/ppermute | solution.py:24
  253.4 2.6 concatenate.46
  257.3 2.2 pad_maximum_fusion.1
  (101 shorter events, 25.5 us)
Async XLA Ops:
  7.2 53.6 %all-gather.3.cloned.1.call-start = ((), (), s32[]{:S(2)}) async-start(), calls=%async_computation.2 | async-start | bytes 1671168 | tf_op jit(solution)/shard_map/all_gather | solution.py:141
  9.6 105.5 %all-gather.5.cloned.1.call-start = ((), (), s32[]{:S(2)}) async-start(), calls=%async_computation.3 | async-start | bytes 1114112 | tf_op jit(solution)/shard_map/all_gather | solution.py:144
  10.3 246.9 %reduce-scatter.5.cloned.1.call-start = ((), (), s32[]{:S(2)}) async-start(), calls=%async_computation.5 | async-start | bytes 4718592 | tf_op jit(solution)/shard_map/reduce_scatter | solution.py:189
  31.9 28.9 %copy-start.7 = (f32[2048]{0:T(1024)S(1)}, f32[2048]{0:T(1024)}, u32[]{:S(2)}) copy-start(f32[2048]{0:T(1024)} %param.12) | copy-start | bytes 24580
  65.7 5.7 %copy-start.6 = (bf16[2048,384]{1,0:T(8,128)(2,1)S(1)}, bf16[2048,384]{1,0:T(8,128)(2,1)}, u32[]{:S(2)}) copy-start(bf16[2048,384]{1,0:T(8,128)(2,1)} %all-gather.3.cloned.1.call-done) | copy-start | bytes 4718596
  68.0 8.7 %copy-start.4 = (f32[2048,32]{0,1:T(8,128)S(1)}, f32[2048,32]{0,1:T(8,128)}, u32[]{:S(2)}) copy-start(f32[2048,32]{0,1:T(8,128)} %copy.31) | copy-start | bytes 786436
  68.0 11.4 %collective-permute-start = (bf16[2048,128]{1,0:T(8,128)(2,1)}, bf16[2048,128]{1,0:T(8,128)(2,1)S(1)}, u32[]{:S(2)}, u32[]{:S(2)}) collective-permute-start(bf16[2048,128]{1,0:T(8,128)(2,1)} %pad_maximum_fusion.2), channel_id=1, source_target_pairs={{0,8},{8,16},{16,24},{24,32},{32,40},{40,48},{48,56},{56,64},{64,7... | collective-permute-start | bytes 1572872 | tf_op jit(solution)/shard_map/ppermute | solution.py:19
  119.6 29.5 %copy-start.3 = (bf16[2048,256]{1,0:T(8,128)(2,1)S(1)}, bf16[2048,256]{1,0:T(8,128)(2,1)}, u32[]{:S(2)}) copy-start(bf16[2048,256]{1,0:T(8,128)(2,1)} %all-gather.5.cloned.1.call-done) | copy-start | bytes 3145732
  119.6 137.6 %reduce-scatter.3.cloned.1.call-start = ((), (), s32[]{:S(2)}) async-start(), calls=%async_computation.4 | async-start | bytes 4718592 | tf_op jit(solution)/shard_map/reduce_scatter | solution.py:189
  155.4 40.7 %collective-permute-start.13 = (bf16[1,65,128]{2,0,1:T(2,128)(2,1)S(1)}, bf16[1,65,128]{2,0,1:T(2,128)(2,1)S(1)}, u32[]{:S(2)}, u32[]{:S(2)}) collective-permute-start(bf16[1,65,128]{2,0,1:T(2,128)(2,1)S(1)} %get-tuple-element.50), channel_id=1, source_target_pairs={{0,104},{8,112},{16,120},{24,0},{32,8},{40,16},{48,24},{56,32},{64... | collective-permute-start | bytes 49928 | tf_op jit(solution)/shard_map/ppermute | solution.py:24
  162.7 35.3 %collective-permute-start.10 = (bf16[1,65,128]{2,0,1:T(2,128)(2,1)S(1)}, bf16[1,65,128]{2,0,1:T(2,128)(2,1)S(1)}, u32[]{:S(2)}, u32[]{:S(2)}) collective-permute-start(bf16[1,65,128]{2,0,1:T(2,128)(2,1)S(1)} %get-tuple-element.51), channel_id=1, source_target_pairs={{0,80},{8,88},{16,96},{24,104},{32,112},{40,120},{48,0},{56,8},{64... | collective-permute-start | bytes 49928 | tf_op jit(solution)/shard_map/ppermute | solution.py:24
  194.1 4.6 %collective-permute-start.11 = (bf16[1,65,128]{2,0,1:T(2,128)(2,1)S(1)}, bf16[1,65,128]{2,0,1:T(2,128)(2,1)S(1)}, u32[]{:S(2)}, u32[]{:S(2)}) collective-permute-start(bf16[1,65,128]{2,0,1:T(2,128)(2,1)S(1)} %get-tuple-element.52), channel_id=1, source_target_pairs={{0,88},{8,96},{16,104},{24,112},{32,120},{40,0},{48,8},{56,16},{64... | collective-permute-start | bytes 49928 | tf_op jit(solution)/shard_map/ppermute | solution.py:24
  195.0 5.9 %collective-permute-start.12 = (bf16[1,65,128]{2,0,1:T(2,128)(2,1)S(1)}, bf16[1,65,128]{2,0,1:T(2,128)(2,1)S(1)}, u32[]{:S(2)}, u32[]{:S(2)}) collective-permute-start(bf16[1,65,128]{2,0,1:T(2,128)(2,1)S(1)} %get-tuple-element.53), channel_id=1, source_target_pairs={{0,96},{8,104},{16,112},{24,120},{32,0},{40,8},{48,16},{56,24},{64... | collective-permute-start | bytes 49928 | tf_op jit(solution)/shard_map/ppermute | solution.py:24
  195.9 9.8 %collective-permute-start.15 = (bf16[1,65,128]{2,0,1:T(2,128)(2,1)S(1)}, bf16[1,65,128]{2,0,1:T(2,128)(2,1)S(1)}, u32[]{:S(2)}, u32[]{:S(2)}) collective-permute-start(bf16[1,65,128]{2,0,1:T(2,128)(2,1)S(1)} %get-tuple-element.38), channel_id=1, source_target_pairs={{0,120},{8,0},{16,8},{24,16},{32,24},{40,32},{48,40},{56,48},{64,5... | collective-permute-start | bytes 49928 | tf_op jit(solution)/shard_map/ppermute | solution.py:24
  196.1 14.0 %collective-permute-start.1 = (bf16[1,65,128]{2,0,1:T(2,128)(2,1)S(1)}, bf16[1,65,128]{2,0,1:T(2,128)(2,1)S(1)}, u32[]{:S(2)}, u32[]{:S(2)}) collective-permute-start(bf16[1,65,128]{2,0,1:T(2,128)(2,1)S(1)} %get-tuple-element.40), channel_id=1, source_target_pairs={{0,8},{8,16},{16,24},{24,32},{32,40},{40,48},{48,56},{56,64},{64,7... | collective-permute-start | bytes 49928 | tf_op jit(solution)/shard_map/ppermute | solution.py:24
  197.9 12.3 %collective-permute-start.2 = (bf16[1,65,128]{2,0,1:T(2,128)(2,1)S(1)}, bf16[1,65,128]{2,0,1:T(2,128)(2,1)S(1)}, u32[]{:S(2)}, u32[]{:S(2)}) collective-permute-start(bf16[1,65,128]{2,0,1:T(2,128)(2,1)S(1)} %get-tuple-element.41), channel_id=1, source_target_pairs={{0,16},{8,24},{16,32},{24,40},{32,48},{40,56},{48,64},{56,72},{64,... | collective-permute-start | bytes 49928 | tf_op jit(solution)/shard_map/ppermute | solution.py:24
  198.6 46.6 %collective-permute-start.3 = (bf16[1,65,128]{2,0,1:T(2,128)(2,1)S(1)}, bf16[1,65,128]{2,0,1:T(2,128)(2,1)S(1)}, u32[]{:S(2)}, u32[]{:S(2)}) collective-permute-start(bf16[1,65,128]{2,0,1:T(2,128)(2,1)S(1)} %get-tuple-element.42), channel_id=1, source_target_pairs={{0,24},{8,32},{16,40},{24,48},{32,56},{40,64},{48,72},{56,80},{64,... | collective-permute-start | bytes 49928 | tf_op jit(solution)/shard_map/ppermute | solution.py:24
  201.0 46.2 %collective-permute-start.4 = (bf16[1,65,128]{2,0,1:T(2,128)(2,1)S(1)}, bf16[1,65,128]{2,0,1:T(2,128)(2,1)S(1)}, u32[]{:S(2)}, u32[]{:S(2)}) collective-permute-start(bf16[1,65,128]{2,0,1:T(2,128)(2,1)S(1)} %get-tuple-element.43), channel_id=1, source_target_pairs={{0,32},{8,40},{16,48},{24,56},{32,64},{40,72},{48,80},{56,88},{64,... | collective-permute-start | bytes 49928 | tf_op jit(solution)/shard_map/ppermute | solution.py:24
  205.7 42.4 %collective-permute-start.14 = (bf16[1,65,128]{2,0,1:T(2,128)(2,1)S(1)}, bf16[1,65,128]{2,0,1:T(2,128)(2,1)S(1)}, u32[]{:S(2)}, u32[]{:S(2)}) collective-permute-start(bf16[1,65,128]{2,0,1:T(2,128)(2,1)S(1)} %get-tuple-element.44), channel_id=1, source_target_pairs={{0,112},{8,120},{16,0},{24,8},{32,16},{40,24},{48,32},{56,40},{64,... | collective-permute-start | bytes 49928 | tf_op jit(solution)/shard_map/ppermute | solution.py:24
  210.2 42.2 %collective-permute-start.5 = (bf16[1,65,128]{2,0,1:T(2,128)(2,1)S(1)}, bf16[1,65,128]{2,0,1:T(2,128)(2,1)S(1)}, u32[]{:S(2)}, u32[]{:S(2)}) collective-permute-start(bf16[1,65,128]{2,0,1:T(2,128)(2,1)S(1)} %get-tuple-element.45), channel_id=1, source_target_pairs={{0,40},{8,48},{16,56},{24,64},{32,72},{40,80},{48,88},{56,96},{64,... | collective-permute-start | bytes 49928 | tf_op jit(solution)/shard_map/ppermute | solution.py:24
  210.2 42.2 %collective-permute-start.6 = (bf16[1,65,128]{2,0,1:T(2,128)(2,1)S(1)}, bf16[1,65,128]{2,0,1:T(2,128)(2,1)S(1)}, u32[]{:S(2)}, u32[]{:S(2)}) collective-permute-start(bf16[1,65,128]{2,0,1:T(2,128)(2,1)S(1)} %get-tuple-element.46), channel_id=1, source_target_pairs={{0,48},{8,56},{16,64},{24,72},{32,80},{40,88},{48,96},{56,104},{64... | collective-permute-start | bytes 49928 | tf_op jit(solution)/shard_map/ppermute | solution.py:24
  245.2 7.2 %collective-permute-start.7 = (bf16[1,65,128]{2,0,1:T(2,128)(2,1)S(1)}, bf16[1,65,128]{2,0,1:T(2,128)(2,1)S(1)}, u32[]{:S(2)}, u32[]{:S(2)}) collective-permute-start(bf16[1,65,128]{2,0,1:T(2,128)(2,1)S(1)} %get-tuple-element.47), channel_id=1, source_target_pairs={{0,56},{8,64},{16,72},{24,80},{32,88},{40,96},{48,104},{56,112},{6... | collective-permute-start | bytes 49928 | tf_op jit(solution)/shard_map/ppermute | solution.py:24
  247.2 5.3 %collective-permute-start.8 = (bf16[1,65,128]{2,0,1:T(2,128)(2,1)S(1)}, bf16[1,65,128]{2,0,1:T(2,128)(2,1)S(1)}, u32[]{:S(2)}, u32[]{:S(2)}) collective-permute-start(bf16[1,65,128]{2,0,1:T(2,128)(2,1)S(1)} %get-tuple-element.48), channel_id=1, source_target_pairs={{0,64},{8,72},{16,80},{24,88},{32,96},{40,104},{48,112},{56,120},{... | collective-permute-start | bytes 49928 | tf_op jit(solution)/shard_map/ppermute | solution.py:24
  248.1 5.4 %collective-permute-start.9 = (bf16[1,65,128]{2,0,1:T(2,128)(2,1)S(1)}, bf16[1,65,128]{2,0,1:T(2,128)(2,1)S(1)}, u32[]{:S(2)}, u32[]{:S(2)}) collective-permute-start(bf16[1,65,128]{2,0,1:T(2,128)(2,1)S(1)} %get-tuple-element.49), channel_id=1, source_target_pairs={{0,72},{8,80},{16,88},{24,96},{32,104},{40,112},{48,120},{56,0},{6... | collective-permute-start | bytes 49928 | tf_op jit(solution)/shard_map/ppermute | solution.py:24
  (6 other events, 15.8 us)
Sparse Core Ops, SparseCore 0:
  11.0 49.6 all-gather.2
  63.2 45.0 all-gather.4
  119.7 68.1 reduce-scatter.4
  190.1 51.9 reduce-scatter.2

commit v12 on v11

--- a/solution.py
+++ b/solution.py
@@ -169,26 +169,6 @@
     queries = queries.reshape(tok_rows, local_heads, head_size)
     queries = rotate_half(queries, cosine[:, None, :], sine_table[:, None, :]).astype(jnp.bfloat16)
     window = jnp.concatenate([earlier, keyval], axis=0)
-    halves = 2
-    blocks_all = tok_rows // min(256, tok_rows)
-    outputs = []
-    for part in range(halves):
-        attended = flash_attention(
-            queries,
-            window[:, :head_size],
-            window[:, head_size:],
-            query_start,
-            token_first,
-            part * blocks_all // halves,
-            blocks_all // halves,
-        )
-        partial_term = lax.dot_general(
-            attended, w_output, (((1,), (1,)), ((), ())), preferred_element_type=jnp.float32
-        )
-        outputs.append(
-            lax.psum_scatter(partial_term.astype(jnp.bfloat16), "mp", scatter_dimension=1, tiled=True)
-        )
-    layer_out = jnp.concatenate(outputs, axis=0)
     pages_dev = tok_rows // PAGE
     share_width = 2 * head_size // ratio
     share_index = mp_index % ratio
@@ -217,6 +197,28 @@
     landed = jnp.concatenate(arrived, axis=0)
     incoming = landed[:, :share_width]
     tags = landed[:, share_width, 0].astype(jnp.int32)
+    halves = 2
+    blocks_all = tok_rows // min(256, tok_rows)
+    outputs = []
+    for part in range(halves):
+        if part == 1:
+            queries, landed = lax.optimization_barrier((queries, landed))
+        attended = flash_attention(
+            queries,
+            window[:, :head_size],
+            window[:, head_size:],
+            query_start,
+            token_first,
+            part * blocks_all // halves,
+            blocks_all // halves,
+        )
+        partial_term = lax.dot_general(
+            attended, w_output, (((1,), (1,)), ((), ())), preferred_element_type=jnp.float32
+        )
+        outputs.append(
+            lax.psum_scatter(partial_term.astype(jnp.bfloat16), "mp", scatter_dimension=1, tiled=True)
+        )
+    layer_out = jnp.concatenate(outputs, axis=0)
     placement = (tags[None, :] == (page_order + 1)[:, None]).astype(jnp.bfloat16)
     kv_cache = jnp.einsum(
         "ps,sfk->pfk", placement, incoming, preferred_element_type=jnp.float32

time: 268 us -> 292 us (1.090)
  waiting for transfers between devices: 19.8 us -> 110 us
  starting transfers between devices: 100 us -> 30.1 us
  other arithmetic: 20 us -> 24.4 us
  local copies, waits for them, and re-layouts: 20.5 us -> 23.7 us
  Pallas kernels: 58.5 us -> 55.4 us
    reduce_scatter x2, waiting for transfers between devices: 0.01 us -> 90.9 us  [body(): lax.psum_scatter(partial_term.astype(jnp.bfloat16), 'mp', scatter_dimensi...]
    ppermute x15, starting transfers between devices: 96.4 us -> 28 us  [shift_round(): return lax.ppermute(x, axis, [(i, (i + by) % peers) for i in range(peers)])]
    pallas_call x2, Pallas kernels: 58.5 us -> 55.4 us  [flash_attention(): pl.pallas_call(functools.partial(flash_kernel, q_rows, tokens, first_bloc...]
  transfers between devices with their start and end apart: 20 -> 20, of which waited for: 3 -> 6; matrix products, arithmetic and copies ran while one was open for 18% -> 20% of each run, Pallas kernels for 22% -> 19%
where the time goes in v12:
time: 292 us; the launch traced here: 291 us
  waiting for transfers between devices  110 us (38%)
  Pallas kernels  55.4 us (19%)
  starting transfers between devices  30.1 us (10%)
  other arithmetic  24.4 us (8%)
  local copies, waits for them, and re-layouts  23.7 us (8%)
  matrix products  18.8 us (6%)
  between operations  14.9 us (5%)
  blocking collectives  13.7 us (5%)
    reduce_scatter x2, waiting for transfers between devices, body(): lax.psum_scatter(partial_term.astype(jnp.bfloat16), 'mp', scatter_dimensi...  90.9 us
    pallas_call x2, Pallas kernels, flash_attention(): pl.pallas_call(functools.partial(flash_kernel, q_rows, tokens, first_bloc...  55.4 us
    ppermute x15, starting transfers between devices, shift_round(): return lax.ppermute(x, axis, [(i, (i + by) % peers) for i in range(peers)])  28 us
    all_gather x1, waiting for transfers between devices, body(): lax.all_gather(jnp.concatenate([kv_own, q_weight], axis=1), 'seq', axis=0...  16.3 us
    psum x1, blocking collectives, body(): seg_total = lax.psum(seg_hist, 'seq')  13.7 us
    dot_general x2, matrix products, body(): lax.dot_general(attended, w_output, (((1,), (1,)), ((), ())), preferred_e...  7.79 us
  transfers between devices with their start and end apart: 20, of which 6 were waited for; matrix products, arithmetic and copies ran while one was open for 20% of the time, Pallas kernels for 19%

profile of v12, /device:TPU:1, one launch (start us, length us, event | category | flops | bytes accessed | tf_op | source)
XLA Modules:
  0.0 290.7 jit_solution(2159302345713388565)
XLA Ops:
  12.6 13.7 %psum.7 = s32[32]{0:T(128)S(1)} all-reduce(s32[32]{0:T(128)S(1)} %convert_reduce_fusion), channel_id=1, replica_groups=mesh['seq'=16,'mp'=8] {'seq'}, use_global_device_ids=true, to_apply=%region_1.2 | all-reduce | flops 32 | bytes 256 | tf_op jit(solution)/shard_map/psum | solution.py:152
  27.9 5.1 %fusion = f32[2048]{0:T(1024)S(1)} fusion(bf16[2048,2048]{1,0:T(8,128)(2,1)} %param.11), kind=kLoop, calls=%fused_computation.2 | loop fusion | flops 12580864 | bytes 8396800 | tf_op jit(solution)/shard_map/reduce_sum | solution.py:146
  33.5 3.7 %multiply_sine_fusion = (f32[2048,32]{1,0:T(8,128)S(1)}, f32[2048,32]{1,0:T(8,128)S(1)}) fusion(f32[32]{0:T(128)S(1)} %multiply_exponential_fusion, f32[2048]{0:T(1024)S(1)} %subtract_convert_fusion.2), kind=kLoop, calls=%fused_computation.24 | loop fusion | flops 65536 | bytes 532608 | tf_op jit(solution)/shard_map/sin | solution.py:161
  39.2 5.2 %reshape.178.qs_ref = s32[8192,1]{1,0:T(8,128)} reshape(s32[8,4,256]{2,1,0:T(4,128)S(1)} %broadcast_in_dim.26) | data formatting | bytes 65536 | tf_op jit(solution)/shard_map/reshape | solution.py:92
  44.4 16.3 %all-gather.3.cloned.1.call-done = bf16[2048,384]{1,0:T(8,128)(2,1)} async-done(((bf16[128,384]{1,0:T(8,128)(2,1)}), bf16[2048,384]{1,0:T(8,128)(2,1)}) %all-gather.3.cloned.1.call-update) | async-done | bytes 1572880 | tf_op jit(solution)/shard_map/all_gather | solution.py:141
  60.8 5.0 %fusion.3 = f32[2048,128]{1,0:T(8,128)S(1)} fusion(bf16[2048,2048]{1,0:T(8,128)(2,1)} %param.11, f32[2048]{0:T(1024)S(1)} %copy-done.22, f32[2048]{0:T(1024)S(1)} %add_rsqrt_fusion, bf16[2048,384]{1,0:T(8,128)(2,1)} %all-gather.3.cloned.1.call-done), kind=kOutput, calls=%fused_computation.7 | convolution fusion | flops 1090519040 | bytes 9977856 | tf_op jit(solution)/shard_map/dot_general | solution.py:163
  68.7 2.4 collective-permute-start.13
  71.1 5.1 %collective-permute-start.11 = (bf16[1,65,128]{2,0,1:T(2,128)(2,1)S(1)}, bf16[1,65,128]{2,0,1:T(2,128)(2,1)S(1)}, u32[]{:S(2)}, u32[]{:S(2)}) collective-permute-start(bf16[1,65,128]{2,0,1:T(2,128)(2,1)S(1)} %get-tuple-element.54), channel_id=1, source_target_pairs={{0,88},{8,96},{16,104},{24,112},{32,120},{40,0},{48,8},{56,16},{64... | collective-permute-start | bytes 49928 | tf_op jit(solution)/shard_map/ppermute | solution.py:24
  78.0 5.6 %fusion.5 = f32[2048,256]{0,1:T(8,128)S(1)} fusion(bf16[2048,2048]{1,0:T(8,128)(2,1)} %param.11, f32[2048]{0:T(1024)S(1)} %copy-done.23, f32[2048]{0:T(1024)S(1)} %add_rsqrt_fusion, bf16[2048,384]{1,0:T(8,128)(2,1)} %all-gather.3.cloned.1.call-done), kind=kOutput, calls=%fused_computation.8 | convolution fusion | flops 2164260864 | bytes 11550720 | tf_op jit(solution)/shard_map/dot_general | solution.py:168
  85.1 2.0 collective-permute-start.3
  87.1 3.9 %collective-permute-start.4 = (bf16[1,65,128]{2,0,1:T(2,128)(2,1)S(1)}, bf16[1,65,128]{2,0,1:T(2,128)(2,1)S(1)}, u32[]{:S(2)}, u32[]{:S(2)}) collective-permute-start(bf16[1,65,128]{2,0,1:T(2,128)(2,1)S(1)} %get-tuple-element.45), channel_id=1, source_target_pairs={{0,32},{8,40},{16,48},{24,56},{32,64},{40,72},{48,80},{56,88},{64,... | collective-permute-start | bytes 49928 | tf_op jit(solution)/shard_map/ppermute | solution.py:24
  91.0 4.4 %collective-permute-start.14 = (bf16[1,65,128]{2,0,1:T(2,128)(2,1)S(1)}, bf16[1,65,128]{2,0,1:T(2,128)(2,1)S(1)}, u32[]{:S(2)}, u32[]{:S(2)}) collective-permute-start(bf16[1,65,128]{2,0,1:T(2,128)(2,1)S(1)} %get-tuple-element.46), channel_id=1, source_target_pairs={{0,112},{8,120},{16,0},{24,8},{32,16},{40,24},{48,32},{56,40},{64,... | collective-permute-start | bytes 49928 | tf_op jit(solution)/shard_map/ppermute | solution.py:24
  97.7 3.5 %collective-permute-start.6 = (bf16[1,65,128]{2,0,1:T(2,128)(2,1)S(1)}, bf16[1,65,128]{2,0,1:T(2,128)(2,1)S(1)}, u32[]{:S(2)}, u32[]{:S(2)}) collective-permute-start(bf16[1,65,128]{2,0,1:T(2,128)(2,1)S(1)} %get-tuple-element.48), channel_id=1, source_target_pairs={{0,48},{8,56},{16,64},{24,72},{32,80},{40,88},{48,96},{56,104},{64... | collective-permute-start | bytes 49928 | tf_op jit(solution)/shard_map/ppermute | solution.py:24
  102.8 2.9 collective-permute-start.9
  108.3 2.9 %concatenate.49 = bf16[16,65,128]{2,0,1:T(8,128)(2,1)S(1)} concatenate(bf16[1,65,128]{2,0,1:T(2,128)(2,1)} %get-tuple-element.41, bf16[1,65,128]{2,0,1:T(2,128)(2,1)} %copy-done.10, bf16[1,65,128]{2,0,1:T(2,128)(2,1)} %copy-done.11, bf16[1,65,128]{2,0,1:T(2,128)(2,1)} %copy-done.12, bf16[1,65,128]{2,0,1:T(2,128)(2,1)} %copy-done.13, bf16[1,65,128]{2,0,1:T(2,128)(2,1)} %copy-done.15, ...), dimensions={0} | concatenate | bytes 532480 | tf_op jit(solution)/shard_map/concatenate | solution.py:197
  113.9 2.9 %copy.40 = bf16[8,4,256,64]{3,2,1,0:T(8,128)(2,1)} copy(bf16[8,4,256,64]{2,0,3,1:T(8,128)(2,1)} %bitcast.63) | data formatting | bytes 2097152 | tf_op jit(solution)/shard_map/transpose | solution.py:88
  120.9 27.5 %shard_map.87 = bf16[4096,64]{1,0:T(8,128)(2,1)} custom-call(s32[1]{0:T(128)} %bitcast.first_ref, s32[8]{0:T(128)} %reduce_min.8.lowest_ref, bf16[8192,64]{1,0:T(8,128)(2,1)} %bitcast.58, bf16[4096,64]{1,0:T(8,128)(2,1)} %get-tuple-element.39.k_ref, bf16[4096,128]{1,0:T(8,128)(2,1)} %pad_maximum_fusion.v_ref, s32[8192,1]{1,0:T(8,128)} %reshape.178.qs_ref), custom_call_target="tpu_custom_call" | custom-call | tf_op jit(solution)/shard_map/pallas_call | solution.py:101
  150.1 4.5 %convolution_convert_fusion = bf16[1024,2048]{1,0:T(8,128)(2,1)} fusion(bf16[1024,256]{0,1:T(8,128)(2,1)S(1)} %bitcast.66, bf16[2048,256]{1,0:T(8,128)(2,1)} %all-gather.5.cloned.1.call-done), kind=kOutput, calls=%fused_computation.5 | convolution fusion | flops 1075838976 | bytes 5767168 | tf_op jit(solution)/shard_map/dot_general | solution.py:215
  155.1 2.0 copy.33
  157.1 27.9 %shard_map.86 = bf16[4096,64]{1,0:T(8,128)(2,1)} custom-call(s32[1]{0:T(128)} %bitcast.first_ref, s32[8]{0:T(128)} %reduce_min.8.lowest_ref, bf16[8192,64]{1,0:T(8,128)(2,1)} %bitcast.59, bf16[4096,64]{1,0:T(8,128)(2,1)} %get-tuple-element.39.k_ref, bf16[4096,128]{1,0:T(8,128)(2,1)} %pad_maximum_fusion.v_ref, s32[8192,1]{1,0:T(8,128)} %reshape.178.qs_ref), custom_call_target="tpu_custom_call" | custom-call | tf_op jit(solution)/shard_map/pallas_call | solution.py:101
  186.6 3.3 %convolution_convert_fusion.1 = bf16[1024,2048]{1,0:T(8,128)(2,1)} fusion(bf16[1024,256]{0,1:T(8,128)(2,1)S(1)} %bitcast.67, bf16[2048,256]{1,0:T(8,128)(2,1)S(1)} %copy-done.3), kind=kOutput, calls=%fused_computation.6 | convolution fusion | flops 1075838976 | bytes 5767168 | tf_op jit(solution)/shard_map/dot_general | solution.py:215
  191.1 36.7 %reduce-scatter.5.cloned.1.call-done = bf16[1024,256]{1,0:T(8,128)(2,1)} async-done(((bf16[1024,2048]{1,0:T(8,128)(2,1)}), bf16[1024,256]{1,0:T(8,128)(2,1)}) %reduce-scatter.5.cloned.1.call-update) | async-done | bytes 524304 | tf_op jit(solution)/shard_map/reduce_scatter | solution.py:219
  227.7 54.2 %reduce-scatter.3.cloned.1.call-done = bf16[1024,256]{1,0:T(8,128)(2,1)} async-done(((bf16[1024,2048]{1,0:T(8,128)(2,1)}), bf16[1024,256]{1,0:T(8,128)(2,1)}) %reduce-scatter.3.cloned.1.call-update) | async-done | bytes 524304 | tf_op jit(solution)/shard_map/reduce_scatter | solution.py:219
  282.0 2.2 pad_maximum_fusion.2
  (133 shorter events, 32.9 us)
Async XLA Ops:
  7.2 53.6 %all-gather.3.cloned.1.call-start = ((), (), s32[]{:S(2)}) async-start(), calls=%async_computation.2 | async-start | bytes 1671168 | tf_op jit(solution)/shard_map/all_gather | solution.py:141
  9.6 140.5 %all-gather.5.cloned.1.call-start = ((), (), s32[]{:S(2)}) async-start(), calls=%async_computation.3 | async-start | bytes 1114112 | tf_op jit(solution)/shard_map/all_gather | solution.py:144
  10.3 217.4 %reduce-scatter.5.cloned.1.call-start = ((), (), s32[]{:S(2)}) async-start(), calls=%async_computation.5 | async-start | bytes 4718592 | tf_op jit(solution)/shard_map/reduce_scatter | solution.py:219
  33.5 27.3 %copy-start.22 = (f32[2048]{0:T(1024)S(1)}, f32[2048]{0:T(1024)}, u32[]{:S(2)}) copy-start(f32[2048]{0:T(1024)} %param.12) | copy-start | bytes 24580
  68.7 14.9 %collective-permute-start.13 = (bf16[1,65,128]{2,0,1:T(2,128)(2,1)S(1)}, bf16[1,65,128]{2,0,1:T(2,128)(2,1)S(1)}, u32[]{:S(2)}, u32[]{:S(2)}) collective-permute-start(bf16[1,65,128]{2,0,1:T(2,128)(2,1)S(1)} %get-tuple-element.52), channel_id=1, source_target_pairs={{0,104},{8,112},{16,120},{24,0},{32,8},{40,16},{48,24},{56,32},{64... | collective-permute-start | bytes 49928 | tf_op jit(solution)/shard_map/ppermute | solution.py:24
  71.1 13.9 %collective-permute-start.10 = (bf16[1,65,128]{2,0,1:T(2,128)(2,1)S(1)}, bf16[1,65,128]{2,0,1:T(2,128)(2,1)S(1)}, u32[]{:S(2)}, u32[]{:S(2)}) collective-permute-start(bf16[1,65,128]{2,0,1:T(2,128)(2,1)S(1)} %get-tuple-element.53), channel_id=1, source_target_pairs={{0,80},{8,88},{16,96},{24,104},{32,112},{40,120},{48,0},{56,8},{64... | collective-permute-start | bytes 49928 | tf_op jit(solution)/shard_map/ppermute | solution.py:24
  71.1 14.0 %collective-permute-start.11 = (bf16[1,65,128]{2,0,1:T(2,128)(2,1)S(1)}, bf16[1,65,128]{2,0,1:T(2,128)(2,1)S(1)}, u32[]{:S(2)}, u32[]{:S(2)}) collective-permute-start(bf16[1,65,128]{2,0,1:T(2,128)(2,1)S(1)} %get-tuple-element.54), channel_id=1, source_target_pairs={{0,88},{8,96},{16,104},{24,112},{32,120},{40,0},{48,8},{56,16},{64... | collective-permute-start | bytes 49928 | tf_op jit(solution)/shard_map/ppermute | solution.py:24
  76.2 10.9 %collective-permute-start.12 = (bf16[1,65,128]{2,0,1:T(2,128)(2,1)S(1)}, bf16[1,65,128]{2,0,1:T(2,128)(2,1)S(1)}, u32[]{:S(2)}, u32[]{:S(2)}) collective-permute-start(bf16[1,65,128]{2,0,1:T(2,128)(2,1)S(1)} %get-tuple-element.55), channel_id=1, source_target_pairs={{0,96},{8,104},{16,112},{24,120},{32,0},{40,8},{48,16},{56,24},{64... | collective-permute-start | bytes 49928 | tf_op jit(solution)/shard_map/ppermute | solution.py:24
  77.4 13.6 %collective-permute-start.15 = (bf16[1,65,128]{2,0,1:T(2,128)(2,1)S(1)}, bf16[1,65,128]{2,0,1:T(2,128)(2,1)S(1)}, u32[]{:S(2)}, u32[]{:S(2)}) collective-permute-start(bf16[1,65,128]{2,0,1:T(2,128)(2,1)S(1)} %get-tuple-element.40), channel_id=1, source_target_pairs={{0,120},{8,0},{16,8},{24,16},{32,24},{40,32},{48,40},{56,48},{64,5... | collective-permute-start | bytes 49928 | tf_op jit(solution)/shard_map/ppermute | solution.py:24
  83.6 22.1 %copy-start.5 = (bf16[1,65,128]{2,0,1:T(2,128)(2,1)}, bf16[1,65,128]{2,0,1:T(2,128)(2,1)S(1)}, u32[]{:S(2)}) copy-start(bf16[1,65,128]{2,0,1:T(2,128)(2,1)S(1)} %collective-permute-done.13) | copy-start | bytes 49924
  83.6 11.8 %collective-permute-start.1 = (bf16[1,65,128]{2,0,1:T(2,128)(2,1)S(1)}, bf16[1,65,128]{2,0,1:T(2,128)(2,1)S(1)}, u32[]{:S(2)}, u32[]{:S(2)}) collective-permute-start(bf16[1,65,128]{2,0,1:T(2,128)(2,1)S(1)} %get-tuple-element.42), channel_id=1, source_target_pairs={{0,8},{8,16},{16,24},{24,32},{32,40},{40,48},{48,56},{56,64},{64,7... | collective-permute-start | bytes 49928 | tf_op jit(solution)/shard_map/ppermute | solution.py:24
  85.0 20.7 %copy-start.6 = (bf16[1,65,128]{2,0,1:T(2,128)(2,1)}, bf16[1,65,128]{2,0,1:T(2,128)(2,1)S(1)}, u32[]{:S(2)}) copy-start(bf16[1,65,128]{2,0,1:T(2,128)(2,1)S(1)} %collective-permute-done.10) | copy-start | bytes 49924
  85.0 10.7 %collective-permute-start.2 = (bf16[1,65,128]{2,0,1:T(2,128)(2,1)S(1)}, bf16[1,65,128]{2,0,1:T(2,128)(2,1)S(1)}, u32[]{:S(2)}, u32[]{:S(2)}) collective-permute-start(bf16[1,65,128]{2,0,1:T(2,128)(2,1)S(1)} %get-tuple-element.43), channel_id=1, source_target_pairs={{0,16},{8,24},{16,32},{24,40},{32,48},{40,56},{48,64},{56,72},{64,... | collective-permute-start | bytes 49928 | tf_op jit(solution)/shard_map/ppermute | solution.py:24
  85.1 12.6 %collective-permute-start.3 = (bf16[1,65,128]{2,0,1:T(2,128)(2,1)S(1)}, bf16[1,65,128]{2,0,1:T(2,128)(2,1)S(1)}, u32[]{:S(2)}, u32[]{:S(2)}) collective-permute-start(bf16[1,65,128]{2,0,1:T(2,128)(2,1)S(1)} %get-tuple-element.44), channel_id=1, source_target_pairs={{0,24},{8,32},{16,40},{24,48},{32,56},{40,64},{48,72},{56,80},{64,... | collective-permute-start | bytes 49928 | tf_op jit(solution)/shard_map/ppermute | solution.py:24
  87.1 14.1 %collective-permute-start.4 = (bf16[1,65,128]{2,0,1:T(2,128)(2,1)S(1)}, bf16[1,65,128]{2,0,1:T(2,128)(2,1)S(1)}, u32[]{:S(2)}, u32[]{:S(2)}) collective-permute-start(bf16[1,65,128]{2,0,1:T(2,128)(2,1)S(1)} %get-tuple-element.45), channel_id=1, source_target_pairs={{0,32},{8,40},{16,48},{24,56},{32,64},{40,72},{48,80},{56,88},{64,... | collective-permute-start | bytes 49928 | tf_op jit(solution)/shard_map/ppermute | solution.py:24
  91.0 10.2 %collective-permute-start.14 = (bf16[1,65,128]{2,0,1:T(2,128)(2,1)S(1)}, bf16[1,65,128]{2,0,1:T(2,128)(2,1)S(1)}, u32[]{:S(2)}, u32[]{:S(2)}) collective-permute-start(bf16[1,65,128]{2,0,1:T(2,128)(2,1)S(1)} %get-tuple-element.46), channel_id=1, source_target_pairs={{0,112},{8,120},{16,0},{24,8},{32,16},{40,24},{48,32},{56,40},{64,... | collective-permute-start | bytes 49928 | tf_op jit(solution)/shard_map/ppermute | solution.py:24
  95.4 7.4 %collective-permute-start.5 = (bf16[1,65,128]{2,0,1:T(2,128)(2,1)S(1)}, bf16[1,65,128]{2,0,1:T(2,128)(2,1)S(1)}, u32[]{:S(2)}, u32[]{:S(2)}) collective-permute-start(bf16[1,65,128]{2,0,1:T(2,128)(2,1)S(1)} %get-tuple-element.47), channel_id=1, source_target_pairs={{0,40},{8,48},{16,56},{24,64},{32,72},{40,80},{48,88},{56,96},{64,... | collective-permute-start | bytes 49928 | tf_op jit(solution)/shard_map/ppermute | solution.py:24
  95.8 21.0 %collective-permute-start = (bf16[2048,128]{1,0:T(8,128)(2,1)S(1)}, bf16[2048,128]{1,0:T(8,128)(2,1)}, u32[]{:S(2)}, u32[]{:S(2)}) collective-permute-start(bf16[2048,128]{1,0:T(8,128)(2,1)S(1)} %pad_maximum_fusion.3), channel_id=1, source_target_pairs={{0,8},{8,16},{16,24},{24,32},{32,40},{40,48},{48,56},{56,64},{64,7... | collective-permute-start | bytes 1572872 | tf_op jit(solution)/shard_map/ppermute | solution.py:19
  97.7 9.1 %collective-permute-start.6 = (bf16[1,65,128]{2,0,1:T(2,128)(2,1)S(1)}, bf16[1,65,128]{2,0,1:T(2,128)(2,1)S(1)}, u32[]{:S(2)}, u32[]{:S(2)}) collective-permute-start(bf16[1,65,128]{2,0,1:T(2,128)(2,1)S(1)} %get-tuple-element.48), channel_id=1, source_target_pairs={{0,48},{8,56},{16,64},{24,72},{32,80},{40,88},{48,96},{56,104},{64... | collective-permute-start | bytes 49928 | tf_op jit(solution)/shard_map/ppermute | solution.py:24
  101.2 5.7 %collective-permute-start.7 = (bf16[1,65,128]{2,0,1:T(2,128)(2,1)S(1)}, bf16[1,65,128]{2,0,1:T(2,128)(2,1)S(1)}, u32[]{:S(2)}, u32[]{:S(2)}) collective-permute-start(bf16[1,65,128]{2,0,1:T(2,128)(2,1)S(1)} %get-tuple-element.49), channel_id=1, source_target_pairs={{0,56},{8,64},{16,72},{24,80},{32,88},{40,96},{48,104},{56,112},{6... | collective-permute-start | bytes 49928 | tf_op jit(solution)/shard_map/ppermute | solution.py:24
  101.2 5.7 %collective-permute-start.8 = (bf16[1,65,128]{2,0,1:T(2,128)(2,1)S(1)}, bf16[1,65,128]{2,0,1:T(2,128)(2,1)S(1)}, u32[]{:S(2)}, u32[]{:S(2)}) collective-permute-start(bf16[1,65,128]{2,0,1:T(2,128)(2,1)S(1)} %get-tuple-element.50), channel_id=1, source_target_pairs={{0,64},{8,72},{16,80},{24,88},{32,96},{40,104},{48,112},{56,120},{... | collective-permute-start | bytes 49928 | tf_op jit(solution)/shard_map/ppermute | solution.py:24
  102.8 4.8 %collective-permute-start.9 = (bf16[1,65,128]{2,0,1:T(2,128)(2,1)S(1)}, bf16[1,65,128]{2,0,1:T(2,128)(2,1)S(1)}, u32[]{:S(2)}, u32[]{:S(2)}) collective-permute-start(bf16[1,65,128]{2,0,1:T(2,128)(2,1)S(1)} %get-tuple-element.51), channel_id=1, source_target_pairs={{0,72},{8,80},{16,88},{24,96},{32,104},{40,112},{48,120},{56,0},{6... | collective-permute-start | bytes 49928 | tf_op jit(solution)/shard_map/ppermute | solution.py:24
  154.7 127.3 %reduce-scatter.3.cloned.1.call-start = ((), (), s32[]{:S(2)}) async-start(), calls=%async_computation.4 | async-start | bytes 4718592 | tf_op jit(solution)/shard_map/reduce_scatter | solution.py:219
  157.1 29.5 %copy-start.3 = (bf16[2048,256]{1,0:T(8,128)(2,1)S(1)}, bf16[2048,256]{1,0:T(8,128)(2,1)}, u32[]{:S(2)}) copy-start(bf16[2048,256]{1,0:T(8,128)(2,1)} %all-gather.5.cloned.1.call-done) | copy-start | bytes 3145732
  (20 other events, 153.1 us)
Sparse Core Ops, SparseCore 0:
  11.0 49.6 all-gather.2
  63.2 44.2 all-gather.4
  154.8 72.9 reduce-scatter.4
  230.0 51.9 reduce-scatter.2
